TPU v7x, 512 devices: a whole 4x4x16 slice. The times are simulated.
512 devices in a mesh: win: 16 (over z_hi, y, core), tm: 32 (over z_lo, x).
Axes of the slice: x: 4, y: 4, z: 16 (z_hi: 2, z_lo: 8; z = z_hi * 8 + z_lo), core: 2. Of those that a mesh axis runs over, the one named last changes fastest.
Arguments:
- frame_inputs: bfloat16 [16, 4096, 2048], P('win', 'tm'), may hold values from -6 to 6
- gate_channels: bfloat16 [16, 4096, 2048], P('win', 'tm'), may hold values from -6 to 6
- state_input_weight: bfloat16 [16, 4096, 128], P('win', 'tm'), may hold values from -6 to 6
- state_output_weight: bfloat16 [16, 4096, 128], P('win', 'tm'), may hold values from -0.59765625 to 0.59765625
- head_decay_codes: int32 [2, 32], replicated, may hold values from 0 to 7
- loss_frames: int32 [16, 4096], P('win', 'tm'), may hold values 0 or 1
- gated_norm_gain: float32 [2048], replicated, may hold values from 0.1 to 1.9
- output_weight: bfloat16 [2048, 1024], P(None, 'tm'), may hold values from -0.125 to 0.125
- seam_taper_shape: int32 [16], replicated, may hold values from 0 to 3
Outputs:
- mixed: bfloat16 [16, 4096, 1024], P('win', 'tm')
All inputs are finite; a program needn't handle non-finite values. No bound on the sum of `loss_frames` on one device may be relied on, other than what follows from the above.
Results may differ from a plain program's by a relative error of at most 0.0059.
Values may be sent and summed in bfloat16 or wider, within the bound.
No kernel may reach another device: no remote copies, remote signals or barrier semaphores. Data moves between devices by JAX's collectives and lax.ppermute only.
A program may use at most 192 MiB of HBM per device.

v0:
```python
import jax
import jax.numpy as jnp
from jax import lax
from jax.sharding import PartitionSpec as P

H = 32
P_SIZE = 64
N = 128
SEAM_DEVS = 4


STATE_LOSS = 0.4
EPSILON = 1e-05


def prefix(value, axis, join, neutral, backward):
    count, mine = (lax.axis_size(axis), lax.axis_index(axis))
    pieces = jax.tree.map(lambda part: lax.all_gather(part, axis), value)
    if backward:
        pieces = jax.tree.map(lambda part: part[::-1], pieces)
        mine = count - 1 - mine
    total = jax.tree.map(
        lambda part, zero: jnp.full_like(part, 0) + jnp.asarray(zero, part.dtype), value, neutral
    )

    def lap(position, total):
        longer = join(total, jax.tree.map(lambda part: part[position], pieces))
        return jax.tree.map(lambda new, old: jnp.where(position < mine, new, old), longer, total)

    return lax.fori_loop(0, count - 1, lap, total)


def shifted(array, axis, by):
    count = lax.axis_size(axis)
    pairs = [(i, i + by) for i in range(count) if 0 <= i + by < count]
    return lax.ppermute(array, axis, pairs)


def decay_rates(head_decay_codes, window_length):
    codes_float = head_decay_codes.astype(jnp.float32)
    quick = jnp.exp2(-codes_float) / 32.0
    gentle = jnp.exp2(5.0 - codes_float) / window_length
    return jnp.where(head_decay_codes < 4, quick, gentle)


def taper_weight(taper_code, position, seam_length):
    spread = (position.astype(jnp.float32) + 0.5) / seam_length
    shapes = jnp.stack(
        [
            spread,
            spread * spread * (3.0 - 2.0 * spread),
            jnp.sin(0.5 * jnp.pi * spread) ** 2,
            spread**3 * (spread * (6.0 * spread - 15.0) + 10.0),
        ]
    )
    kind_index = jnp.arange(4).reshape((4,) + (1,) * spread.ndim)
    selected = kind_index == jnp.expand_dims(taper_code, 0)
    return jnp.sum(jnp.where(selected, shapes, 0.0), axis=0)


def link_states(earlier, later):
    return (earlier[0] * later[0], later[0][:, None, None] * earlier[1] + later[1])


def per_device(
    frame_inputs,
    gate_channels,
    state_input_weight,
    state_output_weight,
    head_decay_codes,
    loss_frames,
    gated_norm_gain,
    output_weight,
    seam_taper_shape,
):
    frames = frame_inputs[0]
    frame_count = frames.shape[0]
    chain_length = lax.axis_size("tm")
    window_length = frame_count * chain_length
    seam_length = SEAM_DEVS * frame_count
    stride_length = window_length - seam_length
    reach = chain_length - SEAM_DEVS
    group_count = H // 4
    decay_rate_pair = decay_rates(head_decay_codes, window_length)
    loss_float = loss_frames[0].astype(jnp.float32)[:, None]
    forward_log_decay = -(decay_rate_pair[0][None, :] + STATE_LOSS * loss_float)
    backward_log_decay = -(decay_rate_pair[1][None, :] + STATE_LOSS * loss_float)
    running_fwd = jnp.cumsum(forward_log_decay, axis=0)
    running_bwd = jnp.flip(jnp.cumsum(jnp.flip(backward_log_decay, 0), axis=0), 0)
    b_rows = state_input_weight[0]
    c_rows = state_output_weight[0]
    head_frames = frames.reshape(frame_count, H, P_SIZE)
    b_float = b_rows.astype(jnp.float32)[:, None, :]
    weighted_fwd = (jnp.exp(running_fwd[-1][None, :] - running_fwd)[:, :, None] * b_float).astype(
        jnp.bfloat16
    )
    weighted_bwd = (jnp.exp(running_bwd[0][None, :] - running_bwd)[:, :, None] * b_float).astype(
        jnp.bfloat16
    )
    fresh_fwd = jnp.einsum(
        "shp,shn->hpn", head_frames, weighted_fwd, preferred_element_type=jnp.float32
    )
    fresh_bwd = jnp.einsum(
        "shp,shn->hpn", head_frames, weighted_bwd, preferred_element_type=jnp.float32
    )
    identity_pair = (jnp.ones((H,), jnp.float32), jnp.zeros((H, P_SIZE, N), jnp.float32))
    _, state_fwd = prefix(
        (jnp.exp(running_fwd[-1]), fresh_fwd), "tm", link_states, identity_pair, False
    )
    _, state_bwd = prefix(
        (jnp.exp(running_bwd[0]), fresh_bwd), "tm", link_states, identity_pair, True
    )
    scores = jnp.dot(c_rows, b_rows.T, preferred_element_type=jnp.float32)
    lower_mask = jnp.arange(frame_count)[:, None] >= jnp.arange(frame_count)[None, :]

    def group_mix(group_items):
        group_fwd, group_bwd, group_frames = group_items
        exponent = jnp.where(
            lower_mask[None],
            group_fwd[:, :, None] - group_fwd[:, None, :],
            group_bwd[:, :, None] - group_bwd[:, None, :],
        )
        mixing = (scores[None] * jnp.exp(exponent)).astype(jnp.bfloat16)
        return jnp.einsum("hts,shp->thp", mixing, group_frames, preferred_element_type=jnp.float32)

    grouped_fwd = running_fwd.T.reshape(group_count, 4, frame_count)
    grouped_bwd = running_bwd.T.reshape(group_count, 4, frame_count)
    grouped_frames = head_frames.reshape(frame_count, group_count, 4, P_SIZE).transpose(1, 0, 2, 3)
    local_groups = lax.map(group_mix, (grouped_fwd, grouped_bwd, grouped_frames))
    local_part = local_groups.transpose(1, 0, 2, 3).reshape(frame_count, H, P_SIZE)
    c_float = c_rows.astype(jnp.float32)
    carried_fwd = jnp.exp(running_fwd)[:, :, None] * jnp.einsum(
        "hpn,tn->thp", state_fwd, c_float, precision=lax.Precision.HIGHEST
    )
    carried_bwd = jnp.exp(running_bwd)[:, :, None] * jnp.einsum(
        "hpn,tn->thp", state_bwd, c_float, precision=lax.Precision.HIGHEST
    )
    summed = local_part + carried_fwd + carried_bwd
    gated_rows = summed * jax.nn.silu(gate_channels[0].astype(jnp.float32)).reshape(
        frame_count, H, P_SIZE
    )
    inverse_rms = lax.rsqrt(jnp.mean(gated_rows * gated_rows, axis=-1, keepdims=True) + EPSILON)
    normed = (
        (gated_rows * inverse_rms).reshape(frame_count, H * P_SIZE) * gated_norm_gain[None, :]
    ).astype(jnp.bfloat16)
    projected_rows = jnp.dot(
        normed,
        lax.all_gather(output_weight, "tm", axis=1, tiled=True),
        preferred_element_type=jnp.float32,
    ).astype(jnp.bfloat16)
    across_previous = shifted(projected_rows, "win", 1)
    from_previous = shifted(across_previous, "tm", -reach)
    across_next = shifted(projected_rows, "win", -1)
    from_next = shifted(across_next, "tm", reach)
    window_index = lax.axis_index("win")
    window_total = lax.axis_size("win")
    position = lax.axis_index("tm") * frame_count + jnp.arange(frame_count)
    next_window = jnp.minimum(window_index + 1, window_total - 1)
    head_fade = taper_weight(seam_taper_shape[window_index], position, seam_length)[:, None]
    tail_fade = taper_weight(seam_taper_shape[next_window], position - stride_length, seam_length)[
        :, None
    ]
    own_rows = projected_rows.astype(jnp.float32)
    head_mix = head_fade * own_rows + (1.0 - head_fade) * from_previous.astype(jnp.float32)
    tail_mix = tail_fade * from_next.astype(jnp.float32) + (1.0 - tail_fade) * own_rows
    use_head = (position < seam_length) & (window_index > 0)
    use_tail = (position >= stride_length) & (window_index < window_total - 1)
    mixed = jnp.where(use_head[:, None], head_mix, jnp.where(use_tail[:, None], tail_mix, own_rows))
    return mixed.astype(jnp.bfloat16)[None]


def solution(mesh):
    in_specs = (
        P("win", "tm", None),
        P("win", "tm", None),
        P("win", "tm", None),
        P("win", "tm", None),
        P(),
        P("win", "tm"),
        P(),
        P(None, "tm"),
        P(),
    )
    out_specs = P("win", "tm", None)
    return jax.shard_map(
        per_device, mesh=mesh, in_specs=in_specs, out_specs=out_specs, check_vma=False
    )
```

profile of v0, /device:TPU:24, one launch (start us, length us, event | category | flops | bytes accessed | tf_op | source)
XLA Modules:
  0.0 1022.7 jit_solution(9995021697445433449)
XLA Ops:
  10.5 1.8 convolution_bitcast_fusion.4
  13.0 1.8 convolution_bitcast_fusion.3
  15.7 124.3 %all-gather.2 = f32[32,1,32]{2,1,0:T(1,128)S(1)} all-gather(f32[1,1,32]{2,1,0:T(1,128)S(1)} %get-tuple-element.328), channel_id=1, replica_groups=mesh['win'=16,'tm'=32] {'tm'}, dimensions={0}, use_global_device_ids=true | all-gather | bytes 4224 | tf_op jit(solution)/shard_map/all_gather | solution.py:18
  140.3 8.2 while.39
  148.5 110.8 %all-gather.3 = f32[32,1,32]{2,1,0:T(1,128)S(1)} all-gather(f32[1,1,32]{2,1,0:T(1,128)S(1)} %get-tuple-element.324), channel_id=1, replica_groups=mesh['win'=16,'tm'=32] {'tm'}, dimensions={0}, use_global_device_ids=true | all-gather | bytes 4224 | tf_op jit(solution)/shard_map/all_gather | solution.py:18
  262.5 131.9 %all-gather.10.cloned.1.call-done = f32[1024,64,128]{2,1,0:T(8,128)} async-done(((f32[32,64,128]{2,1,0:T(8,128)}), f32[1024,64,128]{2,1,0:T(8,128)}) %all-gather.10.cloned.1.call-update) | async-done | bytes 33554448 | tf_op jit(solution)/shard_map/all_gather | solution.py:18
  394.5 46.8 %while.40 = (s32[]{:T(128)}, f32[32,64,128]{2,1,0:T(8,128)S(1)}, s32[]{:T(128)}, f32[32,32]{1,0:T(8,128)S(1)}, f32[32,32,64,128]{3,2,1,0:T(8,128)}, /*index=5*/s32[]{:T(128)}, s32[]{:T(128)}) while((s32[]{:T(128)}, f32[32,64,128]{2,1,0:T(8,128)S(1)}, s32[]{:T(128)}, f32[32,32]{1,0:T(8,128)S(1)}, f32[32,32,64,128]{3,2,1,0:T(8,128)}, ...), condition=%wide.region_6.7_spmd.clone, body=%wide.region_5.6_spmd.clone.sunk | while | flops 1048580 | bytes 3146217 | solution.py:30
  396.0 1.5 fusion.53
  397.5 1.5 fusion.53
  399.0 1.5 fusion.53
  400.5 1.5 fusion.53
  402.0 1.5 fusion.53
  403.5 1.5 fusion.53
  405.0 1.5 fusion.53
  406.6 1.5 fusion.53
  408.1 1.5 fusion.53
  409.6 1.5 fusion.53
  411.1 1.5 fusion.53
  412.6 1.5 fusion.53
  414.1 1.5 fusion.53
  415.6 1.5 fusion.53
  417.1 1.5 fusion.53
  418.6 1.5 fusion.53
  420.1 1.5 fusion.53
  421.6 1.5 fusion.53
  423.1 1.5 fusion.53
  424.6 1.5 fusion.53
  426.1 1.5 fusion.53
  427.6 1.5 fusion.53
  429.2 1.5 fusion.53
  430.7 1.5 fusion.53
  432.2 1.5 fusion.53
  433.7 1.5 fusion.53
  435.2 1.5 fusion.53
  436.7 1.5 fusion.53
  438.2 1.5 fusion.53
  439.7 1.5 fusion.53
  441.2 324.4 %all-gather.12.cloned.1.call-done = f32[1024,64,128]{2,1,0:T(8,128)} async-done(((f32[32,64,128]{2,1,0:T(8,128)}), f32[1024,64,128]{2,1,0:T(8,128)}) %all-gather.12.cloned.1.call-update) | async-done | bytes 33554448 | tf_op jit(solution)/shard_map/all_gather | solution.py:18
  765.6 23.3 %rev.16 = f32[32,32,64,128]{3,2,1,0:T(8,128)} reverse(f32[32,32,64,128]{3,2,1,0:T(8,128)} %bitcast.116), dimensions={0} | reverse | bytes 67108864 | tf_op jit(solution)/shard_map/rev | solution.py:20
  788.9 1.8 fusion.17
  790.8 46.8 %while.41 = (s32[]{:T(128)}, f32[32,64,128]{2,1,0:T(8,128)S(1)}, s32[]{:T(128)}, f32[32,32]{1,0:T(8,128)S(1)}, f32[32,32,64,128]{3,2,1,0:T(8,128)}, /*index=5*/s32[]{:T(128)}, s32[]{:T(128)}) while((s32[]{:T(128)}, f32[32,64,128]{2,1,0:T(8,128)S(1)}, s32[]{:T(128)}, f32[32,32]{1,0:T(8,128)S(1)}, f32[32,32,64,128]{3,2,1,0:T(8,128)}, ...), condition=%wide.region_8.9_spmd.clone, body=%wide.region_7.8_spmd.clone.sunk | while | flops 1048580 | bytes 3146217 | solution.py:30
  790.8 1.6 fusion.54
  792.4 1.5 fusion.54
  793.9 1.5 fusion.54
  795.4 1.5 fusion.54
  796.9 1.5 fusion.54
  798.4 1.5 fusion.54
  802.9 1.5 fusion.54
  805.9 1.5 fusion.54
  809.0 1.5 fusion.54
  818.0 1.5 fusion.54
  821.0 1.5 fusion.54
  824.0 1.5 fusion.54
  833.1 1.5 fusion.54
  836.1 1.5 fusion.54
  838.9 148.5 %all-gather.8.cloned.1.call-done = bf16[2048,1024]{0,1:T(8,128)(2,1)} async-done(((bf16[2048,32]{0,1:T(8,128)(2,1)}), bf16[2048,1024]{0,1:T(8,128)(2,1)}) %all-gather.8.cloned.1.call-update) | async-done | bytes 4194320 | tf_op jit(solution)/shard_map/all_gather | solution.py:148
  987.4 3.7 convolution_convert_fusion
  991.1 1.9 collective-permute-start
  993.1 3.6 collective-permute-start.2
  996.8 2.0 collective-permute-done
  1000.1 6.1 collective-permute-done.2
  1006.2 5.1 collective-permute-start.3
  1011.3 2.3 collective-permute-done.1
  1013.7 1.5 collective-permute-done.3
  (166 shorter events, 47.7 us)
Async XLA Ops:
  6.5 133.6 %copy-start = (bf16[1,128,128]{2,1,0:T(8,128)(2,1)S(1)}, bf16[1,128,128]{2,1,0:T(8,128)(2,1)}, u32[]{:S(2)}) copy-start(bf16[1,128,128]{2,1,0:T(8,128)(2,1)} %param.18) | copy-start | bytes 98308
  6.5 133.6 %copy-start.3 = (bf16[1,128,128]{2,1,0:T(8,128)(2,1)S(1)}, bf16[1,128,128]{2,1,0:T(8,128)(2,1)}, u32[]{:S(2)}) copy-start(bf16[1,128,128]{2,1,0:T(8,128)(2,1)} %param.17) | copy-start | bytes 98308
  6.5 387.9 %all-gather.10.cloned.1.call-start = ((), (), s32[]{:S(2)}) async-start(), calls=%async_computation.1 | async-start | bytes 34603008 | tf_op jit(solution)/shard_map/all_gather | solution.py:18
  12.3 247.0 %copy-start.2 = (bf16[1,128,2048]{2,1,0:T(8,128)(2,1)S(1)}, bf16[1,128,2048]{2,1,0:T(8,128)(2,1)}, u32[]{:S(2)}) copy-start(bf16[1,128,2048]{2,1,0:T(8,128)(2,1)} %param.16) | copy-start | bytes 1572868
  12.4 248.2 %copy-start.5 = (s32[16]{0:T(128)S(1)}, s32[16]{0:T(128)}, u32[]{:S(2)}) copy-start(s32[16]{0:T(128)} %param.23) | copy-start | bytes 196
  12.4 753.2 %all-gather.12.cloned.1.call-start = ((), (), s32[]{:S(2)}) async-start(), calls=%async_computation.2 | async-start | bytes 34603008 | tf_op jit(solution)/shard_map/all_gather | solution.py:18
  14.8 972.6 %all-gather.8.cloned.1.call-start = ((), (), s32[]{:S(2)}) async-start(), calls=%async_computation | async-start | bytes 4325376 | tf_op jit(solution)/shard_map/all_gather | solution.py:148
  790.8 46.8 %copy-start.1 = (f32[1,128,2048]{1,2,0:T(8,128)S(1)}, f32[1,128,2048]{1,2,0:T(8,128)}, u32[]{:S(2)}) copy-start(f32[1,128,2048]{1,2,0:T(8,128)} %copy.55) | copy-start | bytes 3145732
  837.6 1.0 copy-start.4
  991.1 7.7 collective-permute-start
  993.1 13.1 %collective-permute-start.2 = (bf16[128,1024]{1,0:T(8,128)(2,1)S(1)}, bf16[128,1024]{1,0:T(8,128)(2,1)S(1)}, u32[]{:S(2)}, u32[]{:S(2)}) collective-permute-start(bf16[128,1024]{1,0:T(8,128)(2,1)S(1)} %convolution_convert_fusion), channel_id=1, source_target_pairs={{32,0},{64,32},{96,64},{128,96},{160,128},{192,160},{224,192},{256... | collective-permute-start | bytes 786440 | tf_op jit(solution)/shard_map/ppermute | solution.py:36
  998.8 14.9 %collective-permute-start.1 = (bf16[128,1024]{1,0:T(8,128)(2,1)S(1)}, bf16[128,1024]{1,0:T(8,128)(2,1)S(1)}, u32[]{:S(2)}, u32[]{:S(2)}) collective-permute-start(bf16[128,1024]{1,0:T(8,128)(2,1)S(1)} %collective-permute-done), channel_id=1, source_target_pairs={{28,0},{29,1},{30,2},{31,3},{60,32},{61,33},{62,34},{63,35},{92,64... | collective-permute-start | bytes 786440 | tf_op jit(solution)/shard_map/ppermute | solution.py:36
  1006.2 9.0 collective-permute-start.3
Sparse Core Ops, SparseCore 0:
  12.5 381.9 all-gather.9
  396.5 369.0 all-gather.11
  767.7 219.6 all-gather.7
where the time goes:
time: 1040 us; the launch traced here: 1020 us
  waiting for transfers between devices  617 us (59%)
  blocking collectives  235 us (23%)
  other arithmetic  97 us (9%)
  local copies, waits for them, and re-layouts  27.7 us (3%)
  matrix products  18.1 us (2%)
  between operations  13.4 us (1%)
  starting transfers between devices  12.1 us (1%)
    all_gather x2, waiting for transfers between devices, prefix(): pieces = jax.tree.map(lambda part: lax.all_gather(part, axis), value)  456 us
    all_gather x2, blocking collectives, prefix(): pieces = jax.tree.map(lambda part: lax.all_gather(part, axis), value)  235 us
    all_gather x1, waiting for transfers between devices, per_device(): lax.all_gather(output_weight, 'tm', axis=1, tiled=True)  148 us
    select_n x62, other arithmetic, lap(): jnp.where(position < mine, new, old)  91 us
    rev x2, local copies, waits for them, and re-layouts, prefix(): pieces = jax.tree.map(lambda part: part[::-1], pieces)  23.3 us
  transfers between devices with their start and end apart: 7, of which 7 were waited for; matrix products, arithmetic and copies ran while one was open for 13% of the time, Pallas kernels for 0%

commit v1 on v0

--- a/solution.py
+++ b/solution.py
@@ -1,39 +1,18 @@
 import jax
 import jax.numpy as jnp
 from jax import lax
+from jax.sharding import Mesh
 from jax.sharding import PartitionSpec as P
 
 H = 32
 P_SIZE = 64
 N = 128
 SEAM_DEVS = 4
-
+ROW = 4
+PAD_ROWS = 8
 
 STATE_LOSS = 0.4
 EPSILON = 1e-05
-
-
-def prefix(value, axis, join, neutral, backward):
-    count, mine = (lax.axis_size(axis), lax.axis_index(axis))
-    pieces = jax.tree.map(lambda part: lax.all_gather(part, axis), value)
-    if backward:
-        pieces = jax.tree.map(lambda part: part[::-1], pieces)
-        mine = count - 1 - mine
-    total = jax.tree.map(
-        lambda part, zero: jnp.full_like(part, 0) + jnp.asarray(zero, part.dtype), value, neutral
-    )
-
-    def lap(position, total):
-        longer = join(total, jax.tree.map(lambda part: part[position], pieces))
-        return jax.tree.map(lambda new, old: jnp.where(position < mine, new, old), longer, total)
-
-    return lax.fori_loop(0, count - 1, lap, total)
-
-
-def shifted(array, axis, by):
-    count = lax.axis_size(axis)
-    pairs = [(i, i + by) for i in range(count) if 0 <= i + by < count]
-    return lax.ppermute(array, axis, pairs)
 
 
 def decay_rates(head_decay_codes, window_length):
@@ -58,8 +37,65 @@
     return jnp.sum(jnp.where(selected, shapes, 0.0), axis=0)
 
 
-def link_states(earlier, later):
-    return (earlier[0] * later[0], later[0][:, None, None] * earlier[1] + later[1])
+def combine(earlier, later):
+    return (earlier[0] + later[0], jnp.exp(later[0])[..., None, None] * earlier[1] + later[1])
+
+
+def shift(value, axis, by):
+    count = lax.axis_size(axis)
+    pairs = [(i, i + by) for i in range(count) if 0 <= i + by < count]
+    return lax.ppermute(value, axis, pairs)
+
+
+def split_packed(packed):
+    return packed[..., P_SIZE, 0], packed[..., :P_SIZE, :]
+
+
+def pack(logs, states):
+    rows = jnp.broadcast_to(logs[..., None, None], logs.shape + (PAD_ROWS, N))
+    return jnp.concatenate([states, rows], axis=-2)
+
+
+def scan_states(log_fwd, log_bwd, fresh_fwd, fresh_bwd):
+    packed = pack(jnp.stack([log_fwd, log_bwd]), jnp.stack([fresh_fwd, fresh_bwd]))
+    groups = lax.axis_size("x")
+    per_group = H // groups
+    packed = packed.reshape(2, groups, per_group, P_SIZE + PAD_ROWS, N)
+    mine = lax.all_to_all(packed, "x", 1, 1, tiled=True)
+    logs, states = split_packed(mine)
+    zero_l = jnp.zeros_like(logs[:, 0])
+    zero_s = jnp.zeros_like(states[:, 0])
+    fwd_pre = []
+    acc = (zero_l[0], zero_s[0])
+    for k in range(ROW):
+        fwd_pre.append(acc)
+        acc = combine(acc, (logs[0, k], states[0, k]))
+    fwd_total = acc
+    bwd_pre = [None] * ROW
+    acc = (zero_l[1], zero_s[1])
+    for k in reversed(range(ROW)):
+        bwd_pre[k] = acc
+        acc = combine(acc, (logs[1, k], states[1, k]))
+    bwd_total = acc
+    rows = lax.axis_size("z")
+
+    def column_scan(total, step):
+        carried = shift(pack(*total), "z", step)
+        d = 1
+        while d < rows - 1:
+            got = shift(carried, "z", step * d)
+            carried = pack(*combine(split_packed(got), split_packed(carried)))
+            d *= 2
+        return split_packed(carried)
+
+    fwd_in = column_scan(fwd_total, 1)
+    bwd_in = column_scan(bwd_total, -1)
+    out_f = jnp.stack([combine(fwd_in, fwd_pre[k])[1] for k in range(ROW)])
+    out_b = jnp.stack([combine(bwd_in, bwd_pre[k])[1] for k in range(ROW)])
+    out = jnp.stack([out_f, out_b])
+    back = lax.all_to_all(out, "x", 1, 1, tiled=True)
+    back = back.reshape(2, H, P_SIZE, N)
+    return back[0], back[1]
 
 
 def per_device(
@@ -75,11 +111,11 @@
 ):
     frames = frame_inputs[0]
     frame_count = frames.shape[0]
-    chain_length = lax.axis_size("tm")
+    rows = lax.axis_size("z")
+    row_len = lax.axis_size("x")
+    chain_length = rows * row_len
     window_length = frame_count * chain_length
     seam_length = SEAM_DEVS * frame_count
-    stride_length = window_length - seam_length
-    reach = chain_length - SEAM_DEVS
     group_count = H // 4
     decay_rate_pair = decay_rates(head_decay_codes, window_length)
     loss_float = loss_frames[0].astype(jnp.float32)[:, None]
@@ -103,13 +139,7 @@
     fresh_bwd = jnp.einsum(
         "shp,shn->hpn", head_frames, weighted_bwd, preferred_element_type=jnp.float32
     )
-    identity_pair = (jnp.ones((H,), jnp.float32), jnp.zeros((H, P_SIZE, N), jnp.float32))
-    _, state_fwd = prefix(
-        (jnp.exp(running_fwd[-1]), fresh_fwd), "tm", link_states, identity_pair, False
-    )
-    _, state_bwd = prefix(
-        (jnp.exp(running_bwd[0]), fresh_bwd), "tm", link_states, identity_pair, True
-    )
+    state_fwd, state_bwd = scan_states(running_fwd[-1], running_bwd[0], fresh_fwd, fresh_bwd)
     scores = jnp.dot(c_rows, b_rows.T, preferred_element_type=jnp.float32)
     lower_mask = jnp.arange(frame_count)[:, None] >= jnp.arange(frame_count)[None, :]
 
@@ -145,43 +175,48 @@
     ).astype(jnp.bfloat16)
     projected_rows = jnp.dot(
         normed,
-        lax.all_gather(output_weight, "tm", axis=1, tiled=True),
+        lax.all_gather(output_weight, ("z", "x"), axis=1, tiled=True),
         preferred_element_type=jnp.float32,
     ).astype(jnp.bfloat16)
-    across_previous = shifted(projected_rows, "win", 1)
-    from_previous = shifted(across_previous, "tm", -reach)
-    across_next = shifted(projected_rows, "win", -1)
-    from_next = shifted(across_next, "tm", reach)
     window_index = lax.axis_index("win")
     window_total = lax.axis_size("win")
-    position = lax.axis_index("tm") * frame_count + jnp.arange(frame_count)
-    next_window = jnp.minimum(window_index + 1, window_total - 1)
-    head_fade = taper_weight(seam_taper_shape[window_index], position, seam_length)[:, None]
-    tail_fade = taper_weight(seam_taper_shape[next_window], position - stride_length, seam_length)[
-        :, None
-    ]
+    row_index = lax.axis_index("z")
+    pairs = []
+    for w in range(1, window_total):
+        pairs.append(((w - 1) * rows + rows - 1, w * rows))
+        pairs.append((w * rows, (w - 1) * rows + rows - 1))
+    partner = lax.ppermute(projected_rows, ("win", "z"), pairs)
+    seam_pos = lax.axis_index("x") * frame_count + jnp.arange(frame_count)
+    is_tail = row_index == rows - 1
+    fade_window = jnp.minimum(window_index + is_tail.astype(jnp.int32), window_total - 1)
+    fade = taper_weight(seam_taper_shape[fade_window], seam_pos, seam_length)[:, None]
     own_rows = projected_rows.astype(jnp.float32)
-    head_mix = head_fade * own_rows + (1.0 - head_fade) * from_previous.astype(jnp.float32)
-    tail_mix = tail_fade * from_next.astype(jnp.float32) + (1.0 - tail_fade) * own_rows
-    use_head = (position < seam_length) & (window_index > 0)
-    use_tail = (position >= stride_length) & (window_index < window_total - 1)
-    mixed = jnp.where(use_head[:, None], head_mix, jnp.where(use_tail[:, None], tail_mix, own_rows))
+    other_rows = partner.astype(jnp.float32)
+    head_mix = fade * own_rows + (1.0 - fade) * other_rows
+    tail_mix = fade * other_rows + (1.0 - fade) * own_rows
+    use_head = (row_index == 0) & (window_index > 0)
+    use_tail = is_tail & (window_index < window_total - 1)
+    mixed = jnp.where(use_head, head_mix, jnp.where(use_tail, tail_mix, own_rows))
     return mixed.astype(jnp.bfloat16)[None]
 
 
 def solution(mesh):
+    wins, chain = mesh.devices.shape
+    rows = chain // ROW
+    grid = Mesh(mesh.devices.reshape(wins, rows, ROW), ("win", "z", "x"))
+    blocks = ("z", "x")
     in_specs = (
-        P("win", "tm", None),
-        P("win", "tm", None),
-        P("win", "tm", None),
-        P("win", "tm", None),
+        P("win", blocks, None),
+        P("win", blocks, None),
+        P("win", blocks, None),
+        P("win", blocks, None),
         P(),
-        P("win", "tm"),
+        P("win", blocks),
         P(),
-        P(None, "tm"),
+        P(None, blocks),
         P(),
     )
-    out_specs = P("win", "tm", None)
+    out_specs = P("win", blocks, None)
     return jax.shard_map(
-        per_device, mesh=mesh, in_specs=in_specs, out_specs=out_specs, check_vma=False
-    )
+        per_device, mesh=grid, in_specs=in_specs, out_specs=out_specs, check_vma=False
+    )

time: 1040 us -> 395 us (0.38); the launches traced: 1020 us -> 394 us
  waiting for transfers between devices: 617 us -> 259 us
  blocking collectives: 235 us -> 33.2 us
  other arithmetic: 97 us -> 17.1 us
  starting transfers between devices: 12.1 us -> 41.6 us
  local copies, waits for them, and re-layouts: 27.7 us -> 13 us
    all_gather x3 -> x1, waiting for transfers between devices: 605 us -> 131 us  [per_device(): lax.all_gather(output_weight, ('z', 'x'), axis=1, tiled=True)]
    all_gather x2 -> x0, blocking collectives: 235 us -> none  [prefix(): pieces = jax.tree.map(lambda part: lax.all_gather(part, axis), value)]
    ppermute x4 -> x9, waiting for transfers between devices: 11.9 us -> 111 us  [the longest x8 98.3 us: shift(): return lax.ppermute(value, axis, pairs)]
    select_n x62 -> x0, other arithmetic: 91 us -> none  [lap(): jnp.where(position < mine, new, old)]
    all_to_all x0 -> x1, blocking collectives: none -> 33.2 us  [scan_states(): mine = lax.all_to_all(packed, 'x', 1, 1, tiled=True)]
    ppermute x4 -> x9, starting transfers between devices: 12 us -> 38 us  [the longest x8 36.1 us: shift(): return lax.ppermute(value, axis, pairs)]
    rev x2 -> x0, local copies, waits for them, and re-layouts: 23.3 us -> none  [prefix(): pieces = jax.tree.map(lambda part: part[::-1], pieces)]
    all_to_all x0 -> x1, waiting for transfers between devices: none -> 16.3 us  [scan_states(): back = lax.all_to_all(out, 'x', 1, 1, tiled=True)]
  transfers between devices with their start and end apart: 7 -> 11, of which waited for: 7 -> 11; matrix products, arithmetic and copies ran while one was open for 13% -> 7% of each run, Pallas kernels for 0% -> 0%
where the time goes in v1:
time: 395 us; the launch traced here: 394 us
  waiting for transfers between devices  259 us (66%)
  starting transfers between devices  41.6 us (11%)
  blocking collectives  33.2 us (8%)
  other arithmetic  17.1 us (4%)
  matrix products  16.3 us (4%)
  between operations  13.8 us (3%)
  local copies, waits for them, and re-layouts  13 us (3%)
    all_gather x1, waiting for transfers between devices, per_device(): lax.all_gather(output_weight, ('z', 'x'), axis=1, tiled=True)  131 us
    ppermute x8, waiting for transfers between devices, shift(): return lax.ppermute(value, axis, pairs)  98.3 us
    ppermute x8, starting transfers between devices, shift(): return lax.ppermute(value, axis, pairs)  36.1 us
    all_to_all x1, blocking collectives, scan_states(): mine = lax.all_to_all(packed, 'x', 1, 1, tiled=True)  33.2 us
    all_to_all x1, waiting for transfers between devices, scan_states(): back = lax.all_to_all(out, 'x', 1, 1, tiled=True)  16.3 us
    ppermute x1, waiting for transfers between devices, per_device(): partner = lax.ppermute(projected_rows, ('win', 'z'), pairs)  13.2 us
    dot_general x8, matrix products, group_mix(): jnp.einsum('hts,shp->thp', mixing, group_frames, preferred_element_type=j...  8.05 us
  transfers between devices with their start and end apart: 11, of which 11 were waited for; matrix products, arithmetic and copies ran while one was open for 7% of the time, Pallas kernels for 0%

profile of v1, /device:TPU:24, one launch (start us, length us, event | category | flops | bytes accessed | tf_op | source)
XLA Modules:
  0.0 393.8 jit_solution(11208446948829652580)
XLA Ops:
  6.5 0.8 compare_select_fusion
  7.3 0.7 multiply_bitcast_fusion
  8.7 0.7 fusion.53
  9.5 1.3 copy.89
  10.8 0.8 bitcast_convert_fusion
  11.6 0.6 fusion.54
  12.2 0.8 convolution_bitcast_fusion.4
  13.1 0.8 convolution_bitcast_fusion.3
  14.4 33.2 %all_to_all.10 = f32[2,4,8,72,128]{4,3,2,0,1:T(8,128)S(1)} all-to-all(f32[2,4,8,72,128]{4,3,2,0,1:T(8,128)S(1)} %copy.97), channel_id=1, replica_groups=mesh['win'=16,'z'=8,'x'=4] {'x'}, dimensions={1} | all-to-all | bytes 4718592 | tf_op jit(solution)/shard_map/all_to_all | solution.py:64
  49.0 0.8 fusion.35
  49.9 3.8 collective-permute-start
  53.7 5.0 %collective-permute-done = f32[8,72,128]{2,1,0:T(8,128)S(1)} collective-permute-done((f32[8,72,128]{2,1,0:T(8,128)S(1)}, f32[8,72,128]{2,1,0:T(8,128)S(1)}, u32[]{:S(2)}, u32[]{:S(2)}) %collective-permute-start) | collective-permute-done | bytes 294944 | tf_op jit(solution)/shard_map/ppermute | solution.py:47
  58.8 4.4 %collective-permute-start.1 = (f32[8,72,128]{2,1,0:T(8,128)S(1)}, f32[8,72,128]{2,1,0:T(8,128)S(1)}, u32[]{:S(2)}, u32[]{:S(2)}) collective-permute-start(f32[8,72,128]{2,1,0:T(8,128)S(1)} %collective-permute-done), channel_id=1, source_target_pairs={{0,4},{4,8},{8,12},{12,16},{16,20},{20,24},{24,28},{1,5},{5,9},{9,... | collective-permute-start | bytes 884744 | tf_op jit(solution)/shard_map/ppermute | solution.py:47
  63.2 4.2 %collective-permute-done.1 = f32[8,72,128]{2,1,0:T(8,128)S(1)} collective-permute-done((f32[8,72,128]{2,1,0:T(8,128)S(1)}, f32[8,72,128]{2,1,0:T(8,128)S(1)}, u32[]{:S(2)}, u32[]{:S(2)}) %collective-permute-start.1) | collective-permute-done | bytes 294944 | tf_op jit(solution)/shard_map/ppermute | solution.py:47
  67.7 5.8 %collective-permute-start.2 = (f32[8,72,128]{2,1,0:T(8,128)S(1)}, f32[8,72,128]{2,1,0:T(8,128)S(1)}, u32[]{:S(2)}, u32[]{:S(2)}) collective-permute-start(f32[8,72,128]{2,1,0:T(8,128)S(1)} %pad_maximum_fusion.3), channel_id=1, source_target_pairs={{0,8},{4,12},{8,16},{12,20},{16,24},{20,28},{1,9},{5,13},{9,17},{1... | collective-permute-start | bytes 884744 | tf_op jit(solution)/shard_map/ppermute | solution.py:47
  73.6 4.3 %collective-permute-done.2 = f32[8,72,128]{2,1,0:T(8,128)S(1)} collective-permute-done((f32[8,72,128]{2,1,0:T(8,128)S(1)}, f32[8,72,128]{2,1,0:T(8,128)S(1)}, u32[]{:S(2)}, u32[]{:S(2)}) %collective-permute-start.2) | collective-permute-done | bytes 294944 | tf_op jit(solution)/shard_map/ppermute | solution.py:47
  78.2 16.9 %collective-permute-start.3 = (f32[8,72,128]{2,1,0:T(8,128)S(1)}, f32[8,72,128]{2,1,0:T(8,128)S(1)}, u32[]{:S(2)}, u32[]{:S(2)}) collective-permute-start(f32[8,72,128]{2,1,0:T(8,128)S(1)} %pad_maximum_fusion.4), channel_id=1, source_target_pairs={{0,16},{4,20},{8,24},{12,28},{1,17},{5,21},{9,25},{13,29},{2,18},{... | collective-permute-start | bytes 884744 | tf_op jit(solution)/shard_map/ppermute | solution.py:47
  95.1 4.2 %collective-permute-done.3 = f32[8,72,128]{2,1,0:T(8,128)S(1)} collective-permute-done((f32[8,72,128]{2,1,0:T(8,128)S(1)}, f32[8,72,128]{2,1,0:T(8,128)S(1)}, u32[]{:S(2)}, u32[]{:S(2)}) %collective-permute-start.3) | collective-permute-done | bytes 294944 | tf_op jit(solution)/shard_map/ppermute | solution.py:47
  99.3 1.0 add_bitcast_fusion.5
  100.4 1.3 collective-permute-start.4
  101.7 7.3 %collective-permute-done.4 = f32[8,72,128]{2,1,0:T(8,128)S(1)} collective-permute-done((f32[8,72,128]{2,1,0:T(8,128)S(1)}, f32[8,72,128]{2,1,0:T(8,128)S(1)}, u32[]{:S(2)}, u32[]{:S(2)}) %collective-permute-start.4) | collective-permute-done | bytes 294944 | tf_op jit(solution)/shard_map/ppermute | solution.py:47
  109.0 1.3 collective-permute-start.5
  110.3 17.0 %collective-permute-done.5 = f32[8,72,128]{2,1,0:T(8,128)S(1)} collective-permute-done((f32[8,72,128]{2,1,0:T(8,128)S(1)}, f32[8,72,128]{2,1,0:T(8,128)S(1)}, u32[]{:S(2)}, u32[]{:S(2)}) %collective-permute-start.5) | collective-permute-done | bytes 294944 | tf_op jit(solution)/shard_map/ppermute | solution.py:47
  127.6 0.6 copy-done.1
  128.2 0.8 pad_maximum_fusion.6
  129.0 1.3 collective-permute-start.6
  130.3 22.7 %collective-permute-done.6 = f32[8,72,128]{2,1,0:T(8,128)} collective-permute-done((f32[8,72,128]{2,1,0:T(8,128)}, f32[8,72,128]{2,1,0:T(8,128)}, u32[]{:S(2)}, u32[]{:S(2)}) %collective-permute-start.6) | collective-permute-done | bytes 294944 | tf_op jit(solution)/shard_map/ppermute | solution.py:47
  153.0 1.4 exponential_reduce_fusion
  154.4 1.1 fusion.28
  155.6 0.8 pad_maximum_fusion.7
  156.4 1.3 collective-permute-start.7
  157.7 0.7 copy.91
  158.5 33.6 %collective-permute-done.7 = f32[8,72,128]{2,1,0:T(8,128)} collective-permute-done((f32[8,72,128]{2,1,0:T(8,128)}, f32[8,72,128]{2,1,0:T(8,128)}, u32[]{:S(2)}, u32[]{:S(2)}) %collective-permute-start.7) | collective-permute-done | bytes 294944 | tf_op jit(solution)/shard_map/ppermute | solution.py:47
  192.1 1.1 add_bitcast_fusion.2
  193.2 1.2 add_bitcast_fusion.3
  194.9 1.5 copy.105
  196.4 3.6 all-to-all-start.1
  200.0 13.6 %while.11 = (s32[]{:T(128)}, f32[8,128,4,64]{1,3,2,0:T(8,128)}, bf16[8,128,4,64]{1,3,2,0:T(8,128)(2,1)S(1)}, f32[128,128]{1,0:T(8,128)S(1)}, f32[8,4,128]{2,1,0:T(4,128)}, /*index=5*/f32[8,4,128]{2,1,0:T(4,128)S(1)}, s32[]{:T(128)}) while((s32[]{:T(128)}, f32[8,128,4,64]{1,3,2,0:T(8,128)}, bf16[8,128,4,64]{1,3,2,0:T(8,128)(2,1)S(1)}, ...), condition=%wide.region_4.5_spmd.clone, body=%wide.region_3.4_spmd.clone.sunk | while | flops 8732674 | bytes 312401 | solution.py:159
  200.1 0.7 dynamic-slice_bitcast_fusion.3
  200.8 1.0 fusion.66
  201.8 0.7 dynamic-slice_bitcast_fusion.3
  202.5 1.0 fusion.66
  203.5 0.7 dynamic-slice_bitcast_fusion.3
  204.2 1.0 fusion.66
  205.2 0.7 dynamic-slice_bitcast_fusion.3
  205.9 1.0 fusion.66
  206.9 0.7 dynamic-slice_bitcast_fusion.3
  207.6 1.0 fusion.66
  208.6 0.6 dynamic-slice_bitcast_fusion.3
  209.3 1.0 fusion.66
  210.3 0.7 dynamic-slice_bitcast_fusion.3
  211.0 1.0 fusion.66
  212.0 0.7 dynamic-slice_bitcast_fusion.3
  212.7 1.0 fusion.66
  213.7 1.3 copy.106
  215.6 0.7 iota_compare_fusion.1
  216.3 16.3 %all-to-all-done.1 = f32[2,4,8,64,128]{4,3,2,0,1:T(8,128)S(1)} async-done(((f32[2,4,8,64,128]{4,3,2,0,1:T(8,128)}), f32[2,4,8,64,128]{4,3,2,0,1:T(8,128)S(1)}, u32[]{:S(2)}, u32[]{:S(2)}) %all-to-all-start.1) | async-done | bytes 2097184 | tf_op jit(solution)/shard_map/all_to_all | solution.py:96
  232.9 1.9 fusion.15
  234.8 0.8 multiply_reduce_fusion
  236.2 130.9 %all-gather.2.cloned.1.call-done = bf16[2048,1024]{0,1:T(8,128)(2,1)} async-done(((bf16[2048,32]{0,1:T(8,128)(2,1)}), bf16[2048,1024]{0,1:T(8,128)(2,1)}) %all-gather.2.cloned.1.call-update) | async-done | bytes 4194320 | tf_op jit(solution)/shard_map/all_gather | solution.py:178
  367.1 3.7 convolution_convert_fusion
  370.8 1.9 collective-permute-start.8
  372.8 13.2 %collective-permute-done.8 = bf16[128,1024]{1,0:T(8,128)(2,1)S(1)} collective-permute-done((bf16[128,1024]{1,0:T(8,128)(2,1)S(1)}, bf16[128,1024]{1,0:T(8,128)(2,1)S(1)}, u32[]{:S(2)}, u32[]{:S(2)}) %collective-permute-start.8) | collective-permute-done | bytes 262176 | tf_op jit(solution)/shard_map/ppermute | solution.py:188
  386.0 0.9 fusion.26
  (90 shorter events, 6.2 us)
Async XLA Ops:
  6.5 151.8 %copy-start = (bf16[1,128,128]{2,1,0:T(8,128)(2,1)S(1)}, bf16[1,128,128]{2,1,0:T(8,128)(2,1)}, u32[]{:S(2)}) copy-start(bf16[1,128,128]{2,1,0:T(8,128)(2,1)} %param.14) | copy-start | bytes 98308
  6.5 360.5 %all-gather.2.cloned.1.call-start = ((), (), s32[]{:S(2)}) async-start(), calls=%async_computation.2 | async-start | bytes 4325376 | tf_op jit(solution)/shard_map/all_gather | solution.py:178
  48.4 14.8 %copy-start.11 = (f32[8]{0:T(128)}, f32[8]{0:T(128)S(1)}, u32[]{:S(2)}) copy-start(f32[8]{0:T(128)S(1)} %get-tuple-element.123) | copy-start | bytes 100
  48.4 50.9 %copy-start.12 = (f32[8]{0:T(128)}, f32[8]{0:T(128)S(1)}, u32[]{:S(2)}) copy-start(f32[8]{0:T(128)S(1)} %get-tuple-element.126) | copy-start | bytes 100
  49.0 50.3 %copy-start.10 = (f32[8]{0:T(128)}, f32[8]{0:T(128)S(1)}, u32[]{:S(2)}) copy-start(f32[8]{0:T(128)S(1)} %get-tuple-element.115) | copy-start | bytes 100
  49.9 8.9 %collective-permute-start = (f32[8,72,128]{2,1,0:T(8,128)S(1)}, f32[8,72,128]{2,1,0:T(8,128)S(1)}, u32[]{:S(2)}, u32[]{:S(2)}) collective-permute-start(f32[8,72,128]{2,1,0:T(8,128)S(1)} %pad_maximum_fusion.2), channel_id=1, source_target_pairs={{0,4},{4,8},{8,12},{12,16},{16,20},{20,24},{24,28},{1,5},{5,9},{9,... | collective-permute-start | bytes 884744 | tf_op jit(solution)/shard_map/ppermute | solution.py:47
  58.8 8.6 %collective-permute-start.1 = (f32[8,72,128]{2,1,0:T(8,128)S(1)}, f32[8,72,128]{2,1,0:T(8,128)S(1)}, u32[]{:S(2)}, u32[]{:S(2)}) collective-permute-start(f32[8,72,128]{2,1,0:T(8,128)S(1)} %collective-permute-done), channel_id=1, source_target_pairs={{0,4},{4,8},{8,12},{12,16},{16,20},{20,24},{24,28},{1,5},{5,9},{9,... | collective-permute-start | bytes 884744 | tf_op jit(solution)/shard_map/ppermute | solution.py:47
  67.7 10.1 %collective-permute-start.2 = (f32[8,72,128]{2,1,0:T(8,128)S(1)}, f32[8,72,128]{2,1,0:T(8,128)S(1)}, u32[]{:S(2)}, u32[]{:S(2)}) collective-permute-start(f32[8,72,128]{2,1,0:T(8,128)S(1)} %pad_maximum_fusion.3), channel_id=1, source_target_pairs={{0,8},{4,12},{8,16},{12,20},{16,24},{20,28},{1,9},{5,13},{9,17},{1... | collective-permute-start | bytes 884744 | tf_op jit(solution)/shard_map/ppermute | solution.py:47
  78.2 21.1 %collective-permute-start.3 = (f32[8,72,128]{2,1,0:T(8,128)S(1)}, f32[8,72,128]{2,1,0:T(8,128)S(1)}, u32[]{:S(2)}, u32[]{:S(2)}) collective-permute-start(f32[8,72,128]{2,1,0:T(8,128)S(1)} %pad_maximum_fusion.4), channel_id=1, source_target_pairs={{0,16},{4,20},{8,24},{12,28},{1,17},{5,21},{9,25},{13,29},{2,18},{... | collective-permute-start | bytes 884744 | tf_op jit(solution)/shard_map/ppermute | solution.py:47
  100.3 58.1 %copy-start.7 = (bf16[1,128,128]{2,1,0:T(8,128)(2,1)S(1)}, bf16[1,128,128]{2,1,0:T(8,128)(2,1)}, u32[]{:S(2)}) copy-start(bf16[1,128,128]{2,1,0:T(8,128)(2,1)} %param.13) | copy-start | bytes 98308
  100.4 8.6 %collective-permute-start.4 = (f32[8,72,128]{2,1,0:T(8,128)S(1)}, f32[8,72,128]{2,1,0:T(8,128)S(1)}, u32[]{:S(2)}, u32[]{:S(2)}) collective-permute-start(f32[8,72,128]{2,1,0:T(8,128)S(1)} %pad_maximum_fusion.5), channel_id=1, source_target_pairs={{4,0},{8,4},{12,8},{16,12},{20,16},{24,20},{28,24},{5,1},{9,5},{13... | collective-permute-start | bytes 884744 | tf_op jit(solution)/shard_map/ppermute | solution.py:47
  109.0 18.3 %collective-permute-start.5 = (f32[8,72,128]{2,1,0:T(8,128)S(1)}, f32[8,72,128]{2,1,0:T(8,128)S(1)}, u32[]{:S(2)}, u32[]{:S(2)}) collective-permute-start(f32[8,72,128]{2,1,0:T(8,128)S(1)} %collective-permute-done.4), channel_id=1, source_target_pairs={{4,0},{8,4},{12,8},{16,12},{20,16},{24,20},{28,24},{5,1},{9,5},{13... | collective-permute-start | bytes 884744 | tf_op jit(solution)/shard_map/ppermute | solution.py:47
  127.5 0.7 copy-start.1
  129.0 24.0 %collective-permute-start.6 = (f32[8,72,128]{2,1,0:T(8,128)}, f32[8,72,128]{2,1,0:T(8,128)}, u32[]{:S(2)}, u32[]{:S(2)}) collective-permute-start(f32[8,72,128]{2,1,0:T(8,128)} %pad_maximum_fusion.6), channel_id=1, source_target_pairs={{8,0},{12,4},{16,8},{20,12},{24,16},{28,20},{9,1},{13,5},{17,9},{2... | collective-permute-start | bytes 884744 | tf_op jit(solution)/shard_map/ppermute | solution.py:47
  156.4 35.7 %collective-permute-start.7 = (f32[8,72,128]{2,1,0:T(8,128)}, f32[8,72,128]{2,1,0:T(8,128)}, u32[]{:S(2)}, u32[]{:S(2)}) collective-permute-start(f32[8,72,128]{2,1,0:T(8,128)} %pad_maximum_fusion.7), channel_id=1, source_target_pairs={{16,0},{20,4},{24,8},{28,12},{17,1},{21,5},{25,9},{29,13},{18,2},{... | collective-permute-start | bytes 884744 | tf_op jit(solution)/shard_map/ppermute | solution.py:47
  158.4 36.0 %copy-start.2 = (f32[8,64,128]{2,1,0:T(8,128)S(1)}, f32[8,64,128]{2,1,0:T(8,128)}, u32[]{:S(2)}) copy-start(f32[8,64,128]{2,1,0:T(8,128)} %get-tuple-element.80) | copy-start | bytes 786436
  158.4 36.0 %copy-start.4 = (f32[1,8,64,128]{3,2,1,0:T(8,128)S(1)}, f32[1,8,64,128]{3,2,1,0:T(8,128)}, u32[]{:S(2)}) copy-start(f32[1,8,64,128]{3,2,1,0:T(8,128)} %get-tuple-element.79) | copy-start | bytes 786436
  196.4 36.2 %all-to-all-start.1 = ((f32[2,4,8,64,128]{4,3,2,0,1:T(8,128)}), f32[2,4,8,64,128]{4,3,2,0,1:T(8,128)S(1)}, u32[]{:S(2)}, u32[]{:S(2)}) async-start(f32[2,4,8,64,128]{4,3,2,0,1:T(8,128)} %copy.105), calls=%async_computation.1 | async-start | bytes 4194304 | tf_op jit(solution)/shard_map/all_to_all | solution.py:96
  200.0 13.7 %copy-start.6 = (f32[128,32]{1,0:T(8,128)S(1)}, f32[128,32]{1,0:T(8,128)}, u32[]{:S(2)}) copy-start(f32[128,32]{1,0:T(8,128)} %get-tuple-element.103) | copy-start | bytes 49156
  200.0 13.7 %copy-start.5 = (bf16[1,128,2048]{2,1,0:T(8,128)(2,1)S(1)}, bf16[1,128,2048]{2,1,0:T(8,128)(2,1)}, u32[]{:S(2)}) copy-start(bf16[1,128,2048]{2,1,0:T(8,128)(2,1)} %param.12) | copy-start | bytes 1572868
  200.0 15.0 %copy-start.13 = (s32[16]{0:T(128)S(1)}, s32[16]{0:T(128)}, u32[]{:S(2)}) copy-start(s32[16]{0:T(128)} %param.19) | copy-start | bytes 196
  232.9 1.9 copy-start.3
  232.9 1.9 copy-start.8
  234.8 1.0 copy-start.9
  370.8 15.2 %collective-permute-start.8 = (bf16[128,1024]{1,0:T(8,128)(2,1)S(1)}, bf16[128,1024]{1,0:T(8,128)(2,1)S(1)}, u32[]{:S(2)}, u32[]{:S(2)}) collective-permute-start(bf16[128,1024]{1,0:T(8,128)(2,1)S(1)} %convolution_convert_fusion), channel_id=1, source_target_pairs={{28,32},{32,28},{60,64},{64,60},{92,96},{96,92},{124,128},{128,124... | collective-permute-start | bytes 786440 | tf_op jit(solution)/shard_map/ppermute | solution.py:188
Sparse Core Ops, SparseCore 0:
  130.4 236.6 all-gather.1

commit v2 on v1

--- a/solution.py
+++ b/solution.py
@@ -96,6 +96,12 @@
     back = lax.all_to_all(out, "x", 1, 1, tiled=True)
     back = back.reshape(2, H, P_SIZE, N)
     return back[0], back[1]
+
+
+def gather_weight(output_weight):
+    column = lax.all_gather(output_weight, "z", axis=0)
+    row = lax.all_gather(column, "x", axis=1)
+    return row.transpose(2, 0, 1, 3).reshape(output_weight.shape[0], -1)
 
 
 def per_device(
@@ -175,7 +181,7 @@
     ).astype(jnp.bfloat16)
     projected_rows = jnp.dot(
         normed,
-        lax.all_gather(output_weight, ("z", "x"), axis=1, tiled=True),
+        gather_weight(output_weight),
         preferred_element_type=jnp.float32,
     ).astype(jnp.bfloat16)
     window_index = lax.axis_index("win")

time: 395 us -> 310 us (0.78)
  waiting for transfers between devices: 259 us -> 162 us
  local copies, waits for them, and re-layouts: 13 us -> 27.3 us
    all_gather x1 -> x2, waiting for transfers between devices: 131 us -> 44.1 us  [the longest x1 29.2 us: gather_weight(): column = lax.all_gather(output_weight, 'z', axis=0)]
    ppermute x8, waiting for transfers between devices: 98.3 us -> 77.9 us  [shift(): return lax.ppermute(value, axis, pairs)]
    all_gather x0 -> x2, local copies, waits for them, and re-layouts: none -> 10.2 us  [the longest x1 7.9 us: gather_weight(): row = lax.all_gather(column, 'x', axis=1)]
    all_to_all x1, waiting for transfers between devices: 16.3 us -> 24.7 us  [scan_states(): back = lax.all_to_all(out, 'x', 1, 1, tiled=True)]
    transpose x0 -> x1, local copies, waits for them, and re-layouts: none -> 4.59 us  [gather_weight(): return row.transpose(2, 0, 1, 3).reshape(output_weight.shape[0], -1)]
  transfers between devices with their start and end apart: 11 -> 12, of which waited for: 11 -> 12; matrix products, arithmetic and copies ran while one was open for 7% -> 10% of each run, Pallas kernels for 0% -> 0%
where the time goes in v2:
time: 310 us; the launch traced here: 309 us
  waiting for transfers between devices  162 us (52%)
  starting transfers between devices  41.8 us (13%)
  blocking collectives  33.2 us (11%)
  local copies, waits for them, and re-layouts  27.3 us (9%)
  other arithmetic  16.2 us (5%)
  matrix products  14.1 us (5%)
  between operations  13.9 us (4%)
    ppermute x8, waiting for transfers between devices, shift(): return lax.ppermute(value, axis, pairs)  77.9 us
    ppermute x8, starting transfers between devices, shift(): return lax.ppermute(value, axis, pairs)  36.1 us
    all_to_all x1, blocking collectives, scan_states(): mine = lax.all_to_all(packed, 'x', 1, 1, tiled=True)  33.2 us
    all_gather x1, waiting for transfers between devices, gather_weight(): column = lax.all_gather(output_weight, 'z', axis=0)  29.2 us
    all_to_all x1, waiting for transfers between devices, scan_states(): back = lax.all_to_all(out, 'x', 1, 1, tiled=True)  24.7 us
    ppermute x1, waiting for transfers between devices, per_device(): partner = lax.ppermute(projected_rows, ('win', 'z'), pairs)  15.5 us
    all_gather x1, waiting for transfers between devices, gather_weight(): row = lax.all_gather(column, 'x', axis=1)  14.9 us
    dot_general x8, matrix products, group_mix(): jnp.einsum('hts,shp->thp', mixing, group_frames, preferred_element_type=j...  8.07 us
  transfers between devices with their start and end apart: 12, of which 12 were waited for; matrix products, arithmetic and copies ran while one was open for 10% of the time, Pallas kernels for 0%

profile of v2, /device:TPU:24, one launch (start us, length us, event | category | flops | bytes accessed | tf_op | source)
XLA Modules:
  0.0 308.9 jit_solution(12789009684303381669)
XLA Ops:
  6.5 0.8 compare_select_fusion
  7.3 0.7 multiply_bitcast_fusion
  8.7 0.7 fusion.52
  9.5 1.3 copy.109
  10.8 0.8 bitcast_convert_fusion
  12.2 0.8 convolution_bitcast_fusion.4
  13.1 0.8 convolution_bitcast_fusion.3
  14.4 33.2 %all_to_all.10 = f32[2,4,8,72,128]{4,3,2,0,1:T(8,128)S(1)} all-to-all(f32[2,4,8,72,128]{4,3,2,0,1:T(8,128)S(1)} %copy.117), channel_id=1, replica_groups=mesh['win'=16,'z'=8,'x'=4] {'x'}, dimensions={1} | all-to-all | bytes 4718592 | tf_op jit(solution)/shard_map/all_to_all | solution.py:64
  48.9 0.8 fusion.34
  49.9 3.8 %collective-permute-start = (f32[8,72,128]{2,1,0:T(8,128)S(1)}, f32[8,72,128]{2,1,0:T(8,128)S(1)}, u32[]{:S(2)}, u32[]{:S(2)}) collective-permute-start(f32[8,72,128]{2,1,0:T(8,128)S(1)} %pad_maximum_fusion.2), channel_id=1, source_target_pairs={{0,4},{4,8},{8,12},{12,16},{16,20},{20,24},{24,28},{1,5},{5,9},{9,... | collective-permute-start | bytes 884744 | tf_op jit(solution)/shard_map/ppermute | solution.py:47
  53.7 5.0 %collective-permute-done = f32[8,72,128]{2,1,0:T(8,128)S(1)} collective-permute-done((f32[8,72,128]{2,1,0:T(8,128)S(1)}, f32[8,72,128]{2,1,0:T(8,128)S(1)}, u32[]{:S(2)}, u32[]{:S(2)}) %collective-permute-start) | collective-permute-done | bytes 294944 | tf_op jit(solution)/shard_map/ppermute | solution.py:47
  58.7 4.4 %collective-permute-start.1 = (f32[8,72,128]{2,1,0:T(8,128)S(1)}, f32[8,72,128]{2,1,0:T(8,128)S(1)}, u32[]{:S(2)}, u32[]{:S(2)}) collective-permute-start(f32[8,72,128]{2,1,0:T(8,128)S(1)} %collective-permute-done), channel_id=1, source_target_pairs={{0,4},{4,8},{8,12},{12,16},{16,20},{20,24},{24,28},{1,5},{5,9},{9,... | collective-permute-start | bytes 884744 | tf_op jit(solution)/shard_map/ppermute | solution.py:47
  63.2 4.2 %collective-permute-done.1 = f32[8,72,128]{2,1,0:T(8,128)S(1)} collective-permute-done((f32[8,72,128]{2,1,0:T(8,128)S(1)}, f32[8,72,128]{2,1,0:T(8,128)S(1)}, u32[]{:S(2)}, u32[]{:S(2)}) %collective-permute-start.1) | collective-permute-done | bytes 294944 | tf_op jit(solution)/shard_map/ppermute | solution.py:47
  67.7 5.8 %collective-permute-start.2 = (f32[8,72,128]{2,1,0:T(8,128)S(1)}, f32[8,72,128]{2,1,0:T(8,128)S(1)}, u32[]{:S(2)}, u32[]{:S(2)}) collective-permute-start(f32[8,72,128]{2,1,0:T(8,128)S(1)} %pad_maximum_fusion.3), channel_id=1, source_target_pairs={{0,8},{4,12},{8,16},{12,20},{16,24},{20,28},{1,9},{5,13},{9,17},{1... | collective-permute-start | bytes 884744 | tf_op jit(solution)/shard_map/ppermute | solution.py:47
  73.6 4.3 %collective-permute-done.2 = f32[8,72,128]{2,1,0:T(8,128)S(1)} collective-permute-done((f32[8,72,128]{2,1,0:T(8,128)S(1)}, f32[8,72,128]{2,1,0:T(8,128)S(1)}, u32[]{:S(2)}, u32[]{:S(2)}) %collective-permute-start.2) | collective-permute-done | bytes 294944 | tf_op jit(solution)/shard_map/ppermute | solution.py:47
  78.2 16.9 %collective-permute-start.3 = (f32[8,72,128]{2,1,0:T(8,128)S(1)}, f32[8,72,128]{2,1,0:T(8,128)S(1)}, u32[]{:S(2)}, u32[]{:S(2)}) collective-permute-start(f32[8,72,128]{2,1,0:T(8,128)S(1)} %pad_maximum_fusion.4), channel_id=1, source_target_pairs={{0,16},{4,20},{8,24},{12,28},{1,17},{5,21},{9,25},{13,29},{2,18},{... | collective-permute-start | bytes 884744 | tf_op jit(solution)/shard_map/ppermute | solution.py:47
  95.0 4.2 %collective-permute-done.3 = f32[8,72,128]{2,1,0:T(8,128)S(1)} collective-permute-done((f32[8,72,128]{2,1,0:T(8,128)S(1)}, f32[8,72,128]{2,1,0:T(8,128)S(1)}, u32[]{:S(2)}, u32[]{:S(2)}) %collective-permute-start.3) | collective-permute-done | bytes 294944 | tf_op jit(solution)/shard_map/ppermute | solution.py:47
  99.3 1.0 add_bitcast_fusion.5
  100.3 1.3 collective-permute-start.4
  101.6 7.4 %collective-permute-done.4 = f32[8,72,128]{2,1,0:T(8,128)} collective-permute-done((f32[8,72,128]{2,1,0:T(8,128)S(1)}, f32[8,72,128]{2,1,0:T(8,128)}, u32[]{:S(2)}, u32[]{:S(2)}) %collective-permute-start.4) | collective-permute-done | bytes 294944 | tf_op jit(solution)/shard_map/ppermute | solution.py:47
  109.0 1.3 collective-permute-start.5
  110.4 17.2 %collective-permute-done.5 = f32[8,72,128]{2,1,0:T(8,128)} collective-permute-done((f32[8,72,128]{2,1,0:T(8,128)}, f32[8,72,128]{2,1,0:T(8,128)}, u32[]{:S(2)}, u32[]{:S(2)}) %collective-permute-start.5) | collective-permute-done | bytes 294944 | tf_op jit(solution)/shard_map/ppermute | solution.py:47
  127.6 0.9 fusion.49
  128.5 1.1 slice_add_fusion
  129.8 1.3 collective-permute-start.6
  131.1 29.2 %collective-permute-done.6 = f32[8,72,128]{2,1,0:T(8,128)S(1)} collective-permute-done((f32[8,72,128]{2,1,0:T(8,128)S(1)}, f32[8,72,128]{2,1,0:T(8,128)S(1)}, u32[]{:S(2)}, u32[]{:S(2)}) %collective-permute-start.6) | collective-permute-done | bytes 294944 | tf_op jit(solution)/shard_map/ppermute | solution.py:47
  160.2 0.7 exponential_reduce_fusion
  161.1 0.8 pad_maximum_fusion.7
  161.8 1.3 collective-permute-start.7
  163.1 0.7 copy.111
  164.0 29.2 %all-gather.5.cloned.1.call-done = bf16[16384,32]{0,1:T(8,128)(2,1)} async-done(((bf16[2048,32]{0,1:T(8,128)(2,1)}), bf16[16384,32]{0,1:T(8,128)(2,1)}) %all-gather.5.cloned.1.call-update) | async-done | bytes 1048592 | tf_op jit(solution)/shard_map/all_gather | solution.py:102
  193.1 2.3 copy.137
  195.5 6.4 %collective-permute-done.7 = f32[8,72,128]{2,1,0:T(8,128)} collective-permute-done((f32[8,72,128]{2,1,0:T(8,128)}, f32[8,72,128]{2,1,0:T(8,128)}, u32[]{:S(2)}, u32[]{:S(2)}) %collective-permute-start.7) | collective-permute-done | bytes 294944 | tf_op jit(solution)/shard_map/ppermute | solution.py:47
  201.9 1.1 add_bitcast_fusion.2
  203.1 1.2 add_bitcast_fusion.3
  204.8 1.5 copy.125
  206.3 3.8 %all-to-all-start.1 = ((f32[2,4,8,64,128]{4,3,2,0,1:T(8,128)}), f32[2,4,8,64,128]{4,3,2,0,1:T(8,128)S(1)}, u32[]{:S(2)}, u32[]{:S(2)}) async-start(f32[2,4,8,64,128]{4,3,2,0,1:T(8,128)} %copy.125), calls=%async_computation.1 | async-start | bytes 4194304 | tf_op jit(solution)/shard_map/all_to_all | solution.py:96
  210.1 13.6 %while.11 = (s32[]{:T(128)}, f32[8,128,4,64]{1,3,2,0:T(8,128)}, bf16[8,128,4,64]{1,3,2,0:T(8,128)(2,1)S(1)}, f32[128,128]{1,0:T(8,128)S(1)}, f32[8,4,128]{2,1,0:T(4,128)}, /*index=5*/f32[8,4,128]{2,1,0:T(4,128)S(1)}, s32[]{:T(128)}) while((s32[]{:T(128)}, f32[8,128,4,64]{1,3,2,0:T(8,128)}, bf16[8,128,4,64]{1,3,2,0:T(8,128)(2,1)S(1)}, ...), condition=%wide.region_4.5_spmd.clone, body=%wide.region_3.4_spmd.clone.sunk | while | flops 8732674 | bytes 312401 | solution.py:165
  210.1 0.7 dynamic-slice_bitcast_fusion.3
  210.9 1.0 fusion.65
  211.9 0.7 dynamic-slice_bitcast_fusion.3
  212.6 1.0 fusion.65
  213.6 0.7 dynamic-slice_bitcast_fusion.3
  214.3 1.0 fusion.65
  215.3 0.7 dynamic-slice_bitcast_fusion.3
  216.0 1.0 fusion.65
  217.6 1.0 fusion.65
  218.7 0.7 dynamic-slice_bitcast_fusion.3
  219.3 1.0 fusion.65
  221.0 1.0 fusion.65
  222.0 0.7 dynamic-slice_bitcast_fusion.3
  222.7 1.0 fusion.65
  223.8 1.3 copy.126
  225.8 0.6 iota_compare_fusion.1
  226.5 24.7 %all-to-all-done.1 = f32[2,4,8,64,128]{4,3,2,0,1:T(8,128)S(1)} async-done(((f32[2,4,8,64,128]{4,3,2,0,1:T(8,128)}), f32[2,4,8,64,128]{4,3,2,0,1:T(8,128)S(1)}, u32[]{:S(2)}, u32[]{:S(2)}) %all-to-all-start.1) | async-done | bytes 2097184 | tf_op jit(solution)/shard_map/all_to_all | solution.py:96
  251.5 1.9 fusion.15
  253.4 0.8 multiply_reduce_fusion
  254.6 14.9 %all-gather.7.cloned.1.call-done = bf16[8,8192,32]{1,2,0:T(8,128)(2,1)} async-done(((bf16[8,2048,32]{1,2,0:T(8,128)(2,1)}), bf16[8,8192,32]{1,2,0:T(8,128)(2,1)}) %all-gather.7.cloned.1.call-update) | async-done | bytes 4194320 | tf_op jit(solution)/shard_map/all_gather | solution.py:103
  269.5 7.9 %reshape.307 = bf16[8,4,2048,32]{2,1,3,0:T(4,128)(2,1)} reshape(bf16[8,8192,32]{1,2,0:T(8,128)(2,1)} %all-gather.7.cloned.1.call-done) | data formatting | bytes 8388608 | tf_op jit(solution)/shard_map/all_gather | solution.py:103
  277.4 4.6 %copy.128 = bf16[2048,8,4,32]{0,3,2,1:T(8,128)(2,1)S(1)} copy(bf16[2048,8,4,32]{0,2,3,1:T(4,128)(2,1)} %bitcast.215) | data formatting | bytes 8388608 | tf_op jit(solution)/shard_map/transpose | solution.py:104
  282.0 1.5 convolution_convert_fusion
  283.6 1.9 collective-permute-start.8
  285.6 15.5 %collective-permute-done.8 = bf16[128,1024]{1,0:T(8,128)(2,1)S(1)} collective-permute-done((bf16[128,1024]{1,0:T(8,128)(2,1)S(1)}, bf16[128,1024]{1,0:T(8,128)(2,1)S(1)}, u32[]{:S(2)}, u32[]{:S(2)}) %collective-permute-start.8) | collective-permute-done | bytes 262176 | tf_op jit(solution)/shard_map/ppermute | solution.py:194
  301.1 0.9 fusion.25
  (110 shorter events, 8.0 us)
Async XLA Ops:
  6.5 157.3 %copy-start = (bf16[1,128,128]{2,1,0:T(8,128)(2,1)S(1)}, bf16[1,128,128]{2,1,0:T(8,128)(2,1)}, u32[]{:S(2)}) copy-start(bf16[1,128,128]{2,1,0:T(8,128)(2,1)} %param.14) | copy-start | bytes 98308
  6.5 186.6 %all-gather.5.cloned.1.call-start = ((), (), s32[]{:S(2)}) async-start(), calls=%async_computation.2 | async-start | bytes 1179648 | tf_op jit(solution)/shard_map/all_gather | solution.py:102
  48.3 14.8 %copy-start.11 = (f32[8]{0:T(128)}, f32[8]{0:T(128)S(1)}, u32[]{:S(2)}) copy-start(f32[8]{0:T(128)S(1)} %get-tuple-element.123) | copy-start | bytes 100
  48.4 50.9 %copy-start.13 = (f32[8]{0:T(128)}, f32[8]{0:T(128)S(1)}, u32[]{:S(2)}) copy-start(f32[8]{0:T(128)S(1)} %get-tuple-element.126) | copy-start | bytes 100
  48.9 50.3 %copy-start.9 = (f32[8]{0:T(128)}, f32[8]{0:T(128)S(1)}, u32[]{:S(2)}) copy-start(f32[8]{0:T(128)S(1)} %get-tuple-element.115) | copy-start | bytes 100
  49.9 8.9 %collective-permute-start = (f32[8,72,128]{2,1,0:T(8,128)S(1)}, f32[8,72,128]{2,1,0:T(8,128)S(1)}, u32[]{:S(2)}, u32[]{:S(2)}) collective-permute-start(f32[8,72,128]{2,1,0:T(8,128)S(1)} %pad_maximum_fusion.2), channel_id=1, source_target_pairs={{0,4},{4,8},{8,12},{12,16},{16,20},{20,24},{24,28},{1,5},{5,9},{9,... | collective-permute-start | bytes 884744 | tf_op jit(solution)/shard_map/ppermute | solution.py:47
  58.7 8.6 %collective-permute-start.1 = (f32[8,72,128]{2,1,0:T(8,128)S(1)}, f32[8,72,128]{2,1,0:T(8,128)S(1)}, u32[]{:S(2)}, u32[]{:S(2)}) collective-permute-start(f32[8,72,128]{2,1,0:T(8,128)S(1)} %collective-permute-done), channel_id=1, source_target_pairs={{0,4},{4,8},{8,12},{12,16},{16,20},{20,24},{24,28},{1,5},{5,9},{9,... | collective-permute-start | bytes 884744 | tf_op jit(solution)/shard_map/ppermute | solution.py:47
  67.7 10.1 %collective-permute-start.2 = (f32[8,72,128]{2,1,0:T(8,128)S(1)}, f32[8,72,128]{2,1,0:T(8,128)S(1)}, u32[]{:S(2)}, u32[]{:S(2)}) collective-permute-start(f32[8,72,128]{2,1,0:T(8,128)S(1)} %pad_maximum_fusion.3), channel_id=1, source_target_pairs={{0,8},{4,12},{8,16},{12,20},{16,24},{20,28},{1,9},{5,13},{9,17},{1... | collective-permute-start | bytes 884744 | tf_op jit(solution)/shard_map/ppermute | solution.py:47
  78.2 21.1 %collective-permute-start.3 = (f32[8,72,128]{2,1,0:T(8,128)S(1)}, f32[8,72,128]{2,1,0:T(8,128)S(1)}, u32[]{:S(2)}, u32[]{:S(2)}) collective-permute-start(f32[8,72,128]{2,1,0:T(8,128)S(1)} %pad_maximum_fusion.4), channel_id=1, source_target_pairs={{0,16},{4,20},{8,24},{12,28},{1,17},{5,21},{9,25},{13,29},{2,18},{... | collective-permute-start | bytes 884744 | tf_op jit(solution)/shard_map/ppermute | solution.py:47
  100.2 63.6 %copy-start.6 = (bf16[1,128,128]{2,1,0:T(8,128)(2,1)S(1)}, bf16[1,128,128]{2,1,0:T(8,128)(2,1)}, u32[]{:S(2)}) copy-start(bf16[1,128,128]{2,1,0:T(8,128)(2,1)} %param.13) | copy-start | bytes 98308
  100.3 8.7 %collective-permute-start.4 = (f32[8,72,128]{2,1,0:T(8,128)S(1)}, f32[8,72,128]{2,1,0:T(8,128)}, u32[]{:S(2)}, u32[]{:S(2)}) collective-permute-start(f32[8,72,128]{2,1,0:T(8,128)S(1)} %pad_maximum_fusion.5), channel_id=1, source_target_pairs={{4,0},{8,4},{12,8},{16,12},{20,16},{24,20},{28,24},{5,1},{9,5},{13... | collective-permute-start | bytes 884744 | tf_op jit(solution)/shard_map/ppermute | solution.py:47
  109.0 18.6 %collective-permute-start.5 = (f32[8,72,128]{2,1,0:T(8,128)}, f32[8,72,128]{2,1,0:T(8,128)}, u32[]{:S(2)}, u32[]{:S(2)}) collective-permute-start(f32[8,72,128]{2,1,0:T(8,128)} %collective-permute-done.4), channel_id=1, source_target_pairs={{4,0},{8,4},{12,8},{16,12},{20,16},{24,20},{28,24},{5,1},{9,5},{13... | collective-permute-start | bytes 884744 | tf_op jit(solution)/shard_map/ppermute | solution.py:47
  110.4 159.2 %all-gather.7.cloned.1.call-start = ((), (), s32[]{:S(2)}) async-start(), calls=%async_computation.3 | async-start | bytes 5242880 | tf_op jit(solution)/shard_map/all_gather | solution.py:103
  129.8 30.5 %collective-permute-start.6 = (f32[8,72,128]{2,1,0:T(8,128)S(1)}, f32[8,72,128]{2,1,0:T(8,128)S(1)}, u32[]{:S(2)}, u32[]{:S(2)}) collective-permute-start(f32[8,72,128]{2,1,0:T(8,128)S(1)} %pad_maximum_fusion.6), channel_id=1, source_target_pairs={{8,0},{12,4},{16,8},{20,12},{24,16},{28,20},{9,1},{13,5},{17,9},{2... | collective-permute-start | bytes 884744 | tf_op jit(solution)/shard_map/ppermute | solution.py:47
  161.8 40.1 %collective-permute-start.7 = (f32[8,72,128]{2,1,0:T(8,128)}, f32[8,72,128]{2,1,0:T(8,128)}, u32[]{:S(2)}, u32[]{:S(2)}) collective-permute-start(f32[8,72,128]{2,1,0:T(8,128)} %pad_maximum_fusion.7), channel_id=1, source_target_pairs={{16,0},{20,4},{24,8},{28,12},{17,1},{21,5},{25,9},{29,13},{18,2},{... | collective-permute-start | bytes 884744 | tf_op jit(solution)/shard_map/ppermute | solution.py:47
  163.9 38.0 %copy-start.10 = (f32[8]{0:T(128)S(1)}, f32[8]{0:T(128)}, u32[]{:S(2)}) copy-start(f32[8]{0:T(128)} %copy-done.9) | copy-start | bytes 100
  163.9 38.0 %copy-start.15 = (f32[8]{0:T(128)S(1)}, f32[8]{0:T(128)}, u32[]{:S(2)}) copy-start(f32[8]{0:T(128)} %get-tuple-element.118) | copy-start | bytes 100
  164.0 38.0 %copy-start.16 = (f32[8]{0:T(128)S(1)}, f32[8]{0:T(128)}, u32[]{:S(2)}) copy-start(f32[8]{0:T(128)} %get-tuple-element.65) | copy-start | bytes 100
  193.1 9.9 %copy-start.12 = (f32[8]{0:T(128)S(1)}, f32[8]{0:T(128)}, u32[]{:S(2)}) copy-start(f32[8]{0:T(128)} %copy-done.11) | copy-start | bytes 100
  193.1 9.9 %copy-start.14 = (f32[8]{0:T(128)S(1)}, f32[8]{0:T(128)}, u32[]{:S(2)}) copy-start(f32[8]{0:T(128)} %copy-done.13) | copy-start | bytes 100
  193.1 9.9 %copy-start.17 = (f32[8]{0:T(128)S(1)}, f32[8]{0:T(128)}, u32[]{:S(2)}) copy-start(f32[8]{0:T(128)} %get-tuple-element.120) | copy-start | bytes 100
  193.1 9.9 %copy-start.18 = (f32[8]{0:T(128)S(1)}, f32[8]{0:T(128)}, u32[]{:S(2)}) copy-start(f32[8]{0:T(128)} %get-tuple-element.121) | copy-start | bytes 100
  193.1 9.9 %copy-start.19 = (f32[8]{0:T(128)S(1)}, f32[8]{0:T(128)}, u32[]{:S(2)}) copy-start(f32[8]{0:T(128)} %get-tuple-element.111) | copy-start | bytes 100
  195.5 8.8 %copy-start.1 = (f32[8,64,128]{2,1,0:T(8,128)S(1)}, f32[8,64,128]{2,1,0:T(8,128)}, u32[]{:S(2)}) copy-start(f32[8,64,128]{2,1,0:T(8,128)} %get-tuple-element.80) | copy-start | bytes 786436
  195.5 8.8 %copy-start.3 = (f32[1,8,64,128]{3,2,1,0:T(8,128)S(1)}, f32[1,8,64,128]{3,2,1,0:T(8,128)}, u32[]{:S(2)}) copy-start(f32[1,8,64,128]{3,2,1,0:T(8,128)} %get-tuple-element.79) | copy-start | bytes 786436
  206.3 44.9 %all-to-all-start.1 = ((f32[2,4,8,64,128]{4,3,2,0,1:T(8,128)}), f32[2,4,8,64,128]{4,3,2,0,1:T(8,128)S(1)}, u32[]{:S(2)}, u32[]{:S(2)}) async-start(f32[2,4,8,64,128]{4,3,2,0,1:T(8,128)} %copy.125), calls=%async_computation.1 | async-start | bytes 4194304 | tf_op jit(solution)/shard_map/all_to_all | solution.py:96
  210.1 13.7 %copy-start.5 = (f32[128,32]{1,0:T(8,128)S(1)}, f32[128,32]{1,0:T(8,128)}, u32[]{:S(2)}) copy-start(f32[128,32]{1,0:T(8,128)} %get-tuple-element.103) | copy-start | bytes 49156
  210.1 13.7 %copy-start.4 = (bf16[1,128,2048]{2,1,0:T(8,128)(2,1)S(1)}, bf16[1,128,2048]{2,1,0:T(8,128)(2,1)}, u32[]{:S(2)}) copy-start(bf16[1,128,2048]{2,1,0:T(8,128)(2,1)} %param.12) | copy-start | bytes 1572868
  210.1 15.0 %copy-start.8 = (f32[2048]{0:T(1024)S(1)}, f32[2048]{0:T(1024)}, u32[]{:S(2)}) copy-start(f32[2048]{0:T(1024)} %param.17) | copy-start | bytes 24580
  210.1 15.1 %copy-start.20 = (s32[16]{0:T(128)S(1)}, s32[16]{0:T(128)}, u32[]{:S(2)}) copy-start(s32[16]{0:T(128)} %param.19) | copy-start | bytes 196
  251.4 1.9 copy-start.2
  251.5 1.9 copy-start.7
  283.6 17.5 %collective-permute-start.8 = (bf16[128,1024]{1,0:T(8,128)(2,1)S(1)}, bf16[128,1024]{1,0:T(8,128)(2,1)S(1)}, u32[]{:S(2)}, u32[]{:S(2)}) collective-permute-start(bf16[128,1024]{1,0:T(8,128)(2,1)S(1)} %convolution_convert_fusion), channel_id=1, source_target_pairs={{28,32},{32,28},{60,64},{64,60},{92,96},{96,92},{124,128},{128,124... | collective-permute-start | bytes 786440 | tf_op jit(solution)/shard_map/ppermute | solution.py:194
Sparse Core Ops, SparseCore 0:
  110.5 82.6 all-gather.4
  195.6 73.9 all-gather.6

commit v3 on v2

--- a/solution.py
+++ b/solution.py
@@ -58,42 +58,37 @@
 
 def scan_states(log_fwd, log_bwd, fresh_fwd, fresh_bwd):
     packed = pack(jnp.stack([log_fwd, log_bwd]), jnp.stack([fresh_fwd, fresh_bwd]))
-    groups = lax.axis_size("x")
-    per_group = H // groups
-    packed = packed.reshape(2, groups, per_group, P_SIZE + PAD_ROWS, N)
-    mine = lax.all_to_all(packed, "x", 1, 1, tiled=True)
-    logs, states = split_packed(mine)
-    zero_l = jnp.zeros_like(logs[:, 0])
-    zero_s = jnp.zeros_like(states[:, 0])
-    fwd_pre = []
-    acc = (zero_l[0], zero_s[0])
+    parts = lax.axis_size("x")
+    per_part = 2 * H // parts
+    packed = packed.reshape(parts, per_part, P_SIZE + PAD_ROWS, N)
+    mine = lax.all_to_all(packed, "x", 0, 0, tiled=True)
+    is_bwd = lax.axis_index("x") >= parts // 2
+    ordered = jnp.where(is_bwd, mine[::-1], mine)
+    logs, states = split_packed(ordered)
+    acc = (jnp.zeros_like(logs[0]), jnp.zeros_like(states[0]))
+    pre = []
     for k in range(ROW):
-        fwd_pre.append(acc)
-        acc = combine(acc, (logs[0, k], states[0, k]))
-    fwd_total = acc
-    bwd_pre = [None] * ROW
-    acc = (zero_l[1], zero_s[1])
-    for k in reversed(range(ROW)):
-        bwd_pre[k] = acc
-        acc = combine(acc, (logs[1, k], states[1, k]))
-    bwd_total = acc
+        pre.append(acc)
+        acc = combine(acc, (logs[k], states[k]))
     rows = lax.axis_size("z")
-
-    def column_scan(total, step):
-        carried = shift(pack(*total), "z", step)
-        d = 1
-        while d < rows - 1:
-            got = shift(carried, "z", step * d)
-            carried = pack(*combine(split_packed(got), split_packed(carried)))
-            d *= 2
-        return split_packed(carried)
-
-    fwd_in = column_scan(fwd_total, 1)
-    bwd_in = column_scan(bwd_total, -1)
-    out_f = jnp.stack([combine(fwd_in, fwd_pre[k])[1] for k in range(ROW)])
-    out_b = jnp.stack([combine(bwd_in, bwd_pre[k])[1] for k in range(ROW)])
-    out = jnp.stack([out_f, out_b])
-    back = lax.all_to_all(out, "x", 1, 1, tiled=True)
+    total = acc
+    entering = (jnp.zeros_like(acc[0]), jnp.zeros_like(acc[1]))
+    d = 1
+    while d < rows:
+        pairs = []
+        for z in range(rows):
+            for x in range(parts):
+                to = z + d if x < parts // 2 else z - d
+                if 0 <= to < rows:
+                    pairs.append((z * parts + x, to * parts + x))
+        got = split_packed(lax.ppermute(pack(*total), ("z", "x"), pairs))
+        entering = combine(got, entering)
+        if d * 2 < rows:
+            total = combine(got, total)
+        d *= 2
+    out = jnp.stack([combine(entering, pre[k])[1] for k in range(ROW)])
+    out = jnp.where(is_bwd, out[::-1], out)
+    back = lax.all_to_all(out, "x", 0, 0, tiled=True)
     back = back.reshape(2, H, P_SIZE, N)
     return back[0], back[1]
 

time: 310 us -> 275 us (0.89)
  waiting for transfers between devices: 162 us -> 99.1 us
  starting transfers between devices: 41.8 us -> 94.8 us
  blocking collectives: 33.2 us -> 0 us
  other arithmetic: 16.2 us -> 21.4 us
    all_to_all x1 -> x2, starting transfers between devices: 3.79 us -> 57 us  [the longest x1 52.5 us: scan_states(): back = lax.all_to_all(out, 'x', 0, 0, tiled=True)]
    ppermute x8 -> x3, waiting for transfers between devices: 77.9 us -> 30.4 us  [scan_states(): got = split_packed(lax.ppermute(pack(*total), ('z', 'x'), pairs))]
    all_to_all x1 -> x0, blocking collectives: 33.2 us -> none  [scan_states(): mine = lax.all_to_all(packed, 'x', 1, 1, tiled=True)]
    all_to_all x1 -> x2, waiting for transfers between devices: 24.7 us -> 56.2 us  [the longest x1 29.4 us: scan_states(): mine = lax.all_to_all(packed, 'x', 0, 0, tiled=True)]
    all_gather x1, waiting for transfers between devices: 29.2 us -> 4.79 us  [gather_weight(): column = lax.all_gather(output_weight, 'z', axis=0)]
    all_gather x1, waiting for transfers between devices: 14.9 us -> 0.02 us  [gather_weight(): row = lax.all_gather(column, 'x', axis=1)]
    ppermute x8 -> x3, starting transfers between devices: 36.1 us -> 27.5 us  [scan_states(): got = split_packed(lax.ppermute(pack(*total), ('z', 'x'), pairs))]
    ppermute x1, starting transfers between devices: 1.92 us -> 10.2 us  [per_device(): partner = lax.ppermute(projected_rows, ('win', 'z'), pairs)]
  transfers between devices with their start and end apart: 12 -> 8, of which waited for: 12 -> 6; matrix products, arithmetic and copies ran while one was open for 10% -> 12% of each run, Pallas kernels for 0% -> 0%
where the time goes in v3:
time: 275 us; the launch traced here: 274 us
  waiting for transfers between devices  99.1 us (36%)
  starting transfers between devices  94.8 us (34%)
  local copies, waits for them, and re-layouts  30.3 us (11%)
  other arithmetic  21.4 us (8%)
  matrix products  14.1 us (5%)
  between operations  13.8 us (5%)
    all_to_all x1, starting transfers between devices, scan_states(): back = lax.all_to_all(out, 'x', 0, 0, tiled=True)  52.5 us
    ppermute x3, waiting for transfers between devices, scan_states(): got = split_packed(lax.ppermute(pack(*total), ('z', 'x'), pairs))  30.4 us
    all_to_all x1, waiting for transfers between devices, scan_states(): mine = lax.all_to_all(packed, 'x', 0, 0, tiled=True)  29.4 us
    ppermute x3, starting transfers between devices, scan_states(): got = split_packed(lax.ppermute(pack(*total), ('z', 'x'), pairs))  27.5 us
    all_to_all x1, waiting for transfers between devices, scan_states(): back = lax.all_to_all(out, 'x', 0, 0, tiled=True)  26.8 us
    ppermute x1, starting transfers between devices, per_device(): partner = lax.ppermute(projected_rows, ('win', 'z'), pairs)  10.2 us
    dot_general x8, matrix products, group_mix(): jnp.einsum('hts,shp->thp', mixing, group_frames, preferred_element_type=j...  8.03 us
    all_gather x1, local copies, waits for them, and re-layouts, gather_weight(): row = lax.all_gather(column, 'x', axis=1)  7.87 us
  transfers between devices with their start and end apart: 8, of which 6 were waited for; matrix products, arithmetic and copies ran while one was open for 12% of the time, Pallas kernels for 0%

profile of v3, /device:TPU:24, one launch (start us, length us, event | category | flops | bytes accessed | tf_op | source)
XLA Modules:
  0.0 273.6 jit_solution(10819471263926440155)
XLA Ops:
  6.5 0.8 compare_select_fusion
  7.3 0.7 multiply_bitcast_fusion
  8.7 0.7 fusion.42
  9.5 1.3 copy.88
  10.8 0.8 bitcast_convert_fusion
  11.6 0.6 fusion.43
  12.2 0.8 convolution_bitcast_fusion.4
  13.1 0.8 convolution_bitcast_fusion.3
  14.0 1.6 pad_maximum_fusion
  15.7 4.5 %all-to-all-start = ((f32[4,16,72,128]{3,2,1,0:T(8,128)}), f32[4,16,72,128]{3,2,1,0:T(8,128)}, u32[]{:S(2)}, u32[]{:S(2)}) async-start(f32[4,16,72,128]{3,2,1,0:T(8,128)} %bitcast.21), calls=%async_computation | async-start | bytes 4718592 | tf_op jit(solution)/shard_map/all_to_all | solution.py:64
  20.2 29.4 %all-to-all-done = f32[4,16,72,128]{3,2,1,0:T(8,128)} async-done(((f32[4,16,72,128]{3,2,1,0:T(8,128)}), f32[4,16,72,128]{3,2,1,0:T(8,128)}, u32[]{:S(2)}, u32[]{:S(2)}) %all-to-all-start) | async-done | bytes 2359328 | tf_op jit(solution)/shard_map/all_to_all | solution.py:64
  49.6 2.6 reverse_select_fusion
  52.3 0.9 exponential_reduce_fusion
  53.1 1.0 fusion.26
  54.3 0.7 copy-done.1
  55.0 0.9 pad_maximum_fusion.2
  55.8 3.8 %collective-permute-start = (f32[16,72,128]{2,1,0:T(8,128)}, f32[16,72,128]{2,1,0:T(8,128)S(1)}, u32[]{:S(2)}, u32[]{:S(2)}) collective-permute-start(f32[16,72,128]{2,1,0:T(8,128)} %pad_maximum_fusion.2), channel_id=1, source_target_pairs={{0,4},{1,5},{4,8},{5,9},{6,2},{7,3},{8,12},{9,13},{10,6},{11,7},{1... | collective-permute-start | bytes 1769480 | tf_op jit(solution)/shard_map/ppermute | solution.py:84
  59.8 11.9 %collective-permute-done = f32[16,72,128]{2,1,0:T(8,128)S(1)} collective-permute-done((f32[16,72,128]{2,1,0:T(8,128)}, f32[16,72,128]{2,1,0:T(8,128)S(1)}, u32[]{:S(2)}, u32[]{:S(2)}) %collective-permute-start) | collective-permute-done | bytes 589856 | tf_op jit(solution)/shard_map/ppermute | solution.py:84
  71.8 0.7 copy-done.3
  73.1 1.3 multiply_add_fusion.1
  74.5 5.7 %collective-permute-start.1 = (f32[16,72,128]{2,1,0:T(8,128)S(1)}, f32[16,72,128]{2,1,0:T(8,128)S(1)}, u32[]{:S(2)}, u32[]{:S(2)}) collective-permute-start(f32[16,72,128]{2,1,0:T(8,128)S(1)} %pad_maximum_fusion.3), channel_id=1, source_target_pairs={{0,8},{1,9},{4,12},{5,13},{8,16},{9,17},{10,2},{11,3},{12,20},{13,... | collective-permute-start | bytes 1769480 | tf_op jit(solution)/shard_map/ppermute | solution.py:84
  80.2 18.5 %collective-permute-done.1 = f32[16,72,128]{2,1,0:T(8,128)S(1)} collective-permute-done((f32[16,72,128]{2,1,0:T(8,128)S(1)}, f32[16,72,128]{2,1,0:T(8,128)S(1)}, u32[]{:S(2)}, u32[]{:S(2)}) %collective-permute-start.1) | collective-permute-done | bytes 589856 | tf_op jit(solution)/shard_map/ppermute | solution.py:84
  98.8 0.9 copy-done.4
  99.6 0.6 slice.107
  100.2 1.3 copy.102
  101.5 1.3 exponential_bitcast_fusion.2
  102.8 1.2 multiply_add_fusion
  104.0 0.9 pad_maximum_fusion.4
  104.9 18.0 %collective-permute-start.2 = (f32[16,72,128]{2,1,0:T(8,128)}, f32[16,72,128]{2,1,0:T(8,128)}, u32[]{:S(2)}, u32[]{:S(2)}) collective-permute-start(f32[16,72,128]{2,1,0:T(8,128)} %pad_maximum_fusion.4), channel_id=1, source_target_pairs={{0,16},{1,17},{4,20},{5,21},{8,24},{9,25},{12,28},{13,29},{18,2},{... | collective-permute-start | bytes 1769480 | tf_op jit(solution)/shard_map/ppermute | solution.py:84
  122.9 0.7 copy.90
  123.7 4.8 %all-gather.5.cloned.1.call-done = bf16[16384,32]{0,1:T(8,128)(2,1)} async-done(((bf16[2048,32]{0,1:T(8,128)(2,1)}), bf16[16384,32]{0,1:T(8,128)(2,1)}) %all-gather.5.cloned.1.call-update) | async-done | bytes 1048592 | tf_op jit(solution)/shard_map/all_gather | solution.py:97
  128.5 2.3 copy.105
  130.9 1.6 add_bitcast_fusion.2
  133.0 1.6 reverse_select_fusion.1
  134.6 52.5 %all-to-all-start.1 = ((f32[4,16,64,128]{3,2,1,0:T(8,128)}), f32[4,16,64,128]{3,2,1,0:T(8,128)S(1)}, u32[]{:S(2)}, u32[]{:S(2)}) async-start(f32[4,16,64,128]{3,2,1,0:T(8,128)} %reverse_select_fusion.1), calls=%async_computation.1 | async-start | bytes 4194304 | tf_op jit(solution)/shard_map/all_to_all | solution.py:91
  187.1 13.7 %while.11 = (s32[]{:T(128)}, f32[8,128,4,64]{1,3,2,0:T(8,128)}, bf16[8,128,4,64]{1,3,2,0:T(8,128)(2,1)S(1)}, f32[128,128]{1,0:T(8,128)S(1)}, f32[8,4,128]{2,1,0:T(4,128)}, /*index=5*/f32[8,4,128]{2,1,0:T(4,128)S(1)}, s32[]{:T(128)}) while((s32[]{:T(128)}, f32[8,128,4,64]{1,3,2,0:T(8,128)}, bf16[8,128,4,64]{1,3,2,0:T(8,128)(2,1)S(1)}, ...), condition=%wide.region_4.5_spmd.clone, body=%wide.region_3.4_spmd.clone.sunk | while | flops 8732674 | bytes 312401 | solution.py:160
  187.1 0.7 dynamic-slice_bitcast_fusion.3
  187.9 1.0 fusion.53
  188.9 0.7 dynamic-slice_bitcast_fusion.3
  189.6 1.0 fusion.53
  190.6 0.7 dynamic-slice_bitcast_fusion.3
  191.3 1.0 fusion.53
  192.3 0.7 dynamic-slice_bitcast_fusion.3
  193.0 1.0 fusion.53
  194.0 0.7 dynamic-slice_bitcast_fusion.3
  194.7 1.0 fusion.53
  195.7 0.7 dynamic-slice_bitcast_fusion.3
  196.4 1.0 fusion.53
  197.4 0.7 dynamic-slice_bitcast_fusion.3
  198.1 1.0 fusion.53
  199.1 0.7 dynamic-slice_bitcast_fusion.3
  199.8 1.0 fusion.53
  200.9 1.3 copy.98
  202.3 0.6 dynamic_slice.14
  202.8 0.7 iota_compare_fusion.1
  203.6 26.8 %all-to-all-done.1 = f32[4,16,64,128]{3,2,1,0:T(8,128)S(1)} async-done(((f32[4,16,64,128]{3,2,1,0:T(8,128)}), f32[4,16,64,128]{3,2,1,0:T(8,128)S(1)}, u32[]{:S(2)}, u32[]{:S(2)}) %all-to-all-start.1) | async-done | bytes 2097184 | tf_op jit(solution)/shard_map/all_to_all | solution.py:91
  230.6 1.9 fusion.15
  232.6 0.8 multiply_reduce_fusion
  233.8 7.9 %reshape.290 = bf16[8,4,2048,32]{2,1,3,0:T(4,128)(2,1)} reshape(bf16[8,8192,32]{1,2,0:T(8,128)(2,1)} %all-gather.7.cloned.1.call-done) | data formatting | bytes 8388608 | tf_op jit(solution)/shard_map/all_gather | solution.py:98
  241.7 4.6 %copy.100 = bf16[2048,8,4,32]{0,3,2,1:T(8,128)(2,1)S(1)} copy(bf16[2048,8,4,32]{0,2,3,1:T(4,128)(2,1)} %bitcast.151) | data formatting | bytes 8388608 | tf_op jit(solution)/shard_map/transpose | solution.py:99
  246.3 1.5 convolution_convert_fusion
  247.8 10.2 %collective-permute-start.3 = (bf16[128,1024]{1,0:T(8,128)(2,1)S(1)}, bf16[128,1024]{1,0:T(8,128)(2,1)S(1)}, u32[]{:S(2)}, u32[]{:S(2)}) collective-permute-start(bf16[128,1024]{1,0:T(8,128)(2,1)S(1)} %convolution_convert_fusion), channel_id=1, source_target_pairs={{28,32},{32,28},{60,64},{64,60},{92,96},{96,92},{124,128},{128,124... | collective-permute-start | bytes 786440 | tf_op jit(solution)/shard_map/ppermute | solution.py:189
  258.1 7.6 %collective-permute-done.3 = bf16[128,1024]{1,0:T(8,128)(2,1)S(1)} collective-permute-done((bf16[128,1024]{1,0:T(8,128)(2,1)S(1)}, bf16[128,1024]{1,0:T(8,128)(2,1)S(1)}, u32[]{:S(2)}, u32[]{:S(2)}) %collective-permute-start.3) | collective-permute-done | bytes 262176 | tf_op jit(solution)/shard_map/ppermute | solution.py:189
  265.8 0.9 fusion.30
  (90 shorter events, 3.7 us)
Async XLA Ops:
  6.5 117.0 %copy-start = (bf16[1,128,128]{2,1,0:T(8,128)(2,1)S(1)}, bf16[1,128,128]{2,1,0:T(8,128)(2,1)}, u32[]{:S(2)}) copy-start(bf16[1,128,128]{2,1,0:T(8,128)(2,1)} %param.14) | copy-start | bytes 98308
  8.5 0.9 copy-start.6
  15.7 34.0 %all-to-all-start = ((f32[4,16,72,128]{3,2,1,0:T(8,128)}), f32[4,16,72,128]{3,2,1,0:T(8,128)}, u32[]{:S(2)}, u32[]{:S(2)}) async-start(f32[4,16,72,128]{3,2,1,0:T(8,128)} %bitcast.21), calls=%async_computation | async-start | bytes 4718592 | tf_op jit(solution)/shard_map/all_to_all | solution.py:64
  20.2 108.3 %all-gather.5.cloned.1.call-start = ((), (), s32[]{:S(2)}) async-start(), calls=%async_computation.2 | async-start | bytes 1179648 | tf_op jit(solution)/shard_map/all_gather | solution.py:97
  53.1 18.6 %copy-start.19 = (f32[16]{0:T(128)}, f32[16]{0:T(128)S(1)}, u32[]{:S(2)}) copy-start(f32[16]{0:T(128)S(1)} %get-tuple-element.68) | copy-start | bytes 196
  53.1 19.4 %copy-start.13 = (f32[16]{0:T(128)}, f32[16]{0:T(128)S(1)}, u32[]{:S(2)}) copy-start(f32[16]{0:T(128)S(1)} %get-tuple-element.64) | copy-start | bytes 196
  53.1 19.4 %copy-start.14 = (f32[16]{0:T(128)}, f32[16]{0:T(128)S(1)}, u32[]{:S(2)}) copy-start(f32[16]{0:T(128)S(1)} %get-tuple-element.66) | copy-start | bytes 196
  53.1 19.4 %copy-start.20 = (f32[16]{0:T(128)}, f32[16]{0:T(128)S(1)}, u32[]{:S(2)}) copy-start(f32[16]{0:T(128)S(1)} %broadcast_multiply_fusion) | copy-start | bytes 196
  54.2 0.8 copy-start.1
  55.8 15.8 %collective-permute-start = (f32[16,72,128]{2,1,0:T(8,128)}, f32[16,72,128]{2,1,0:T(8,128)S(1)}, u32[]{:S(2)}, u32[]{:S(2)}) collective-permute-start(f32[16,72,128]{2,1,0:T(8,128)} %pad_maximum_fusion.2), channel_id=1, source_target_pairs={{0,4},{1,5},{4,8},{5,9},{6,2},{7,3},{8,12},{9,13},{10,6},{11,7},{1... | collective-permute-start | bytes 1769480 | tf_op jit(solution)/shard_map/ppermute | solution.py:84
  59.7 174.1 %all-gather.7.cloned.1.call-start = ((), (), s32[]{:S(2)}) async-start(), calls=%async_computation.3 | async-start | bytes 5242880 | tf_op jit(solution)/shard_map/all_gather | solution.py:98
  71.7 0.8 copy-start.3
  72.5 0.6 copy-start.16
  74.4 48.5 %copy-start.7 = (f32[128,32]{1,0:T(8,128)S(1)}, f32[128,32]{1,0:T(8,128)}, u32[]{:S(2)}) copy-start(f32[128,32]{1,0:T(8,128)} %copy-done.6) | copy-start | bytes 49156
  74.4 49.2 %copy-start.10 = (bf16[1,128,128]{2,1,0:T(8,128)(2,1)S(1)}, bf16[1,128,128]{2,1,0:T(8,128)(2,1)}, u32[]{:S(2)}) copy-start(bf16[1,128,128]{2,1,0:T(8,128)(2,1)} %param.13) | copy-start | bytes 98308
  74.5 24.2 %collective-permute-start.1 = (f32[16,72,128]{2,1,0:T(8,128)S(1)}, f32[16,72,128]{2,1,0:T(8,128)S(1)}, u32[]{:S(2)}, u32[]{:S(2)}) collective-permute-start(f32[16,72,128]{2,1,0:T(8,128)S(1)} %pad_maximum_fusion.3), channel_id=1, source_target_pairs={{0,8},{1,9},{4,12},{5,13},{8,16},{9,17},{10,2},{11,3},{12,20},{13,... | collective-permute-start | bytes 1769480 | tf_op jit(solution)/shard_map/ppermute | solution.py:84
  98.8 0.9 copy-start.4
  104.9 26.0 %collective-permute-start.2 = (f32[16,72,128]{2,1,0:T(8,128)}, f32[16,72,128]{2,1,0:T(8,128)}, u32[]{:S(2)}, u32[]{:S(2)}) collective-permute-start(f32[16,72,128]{2,1,0:T(8,128)} %pad_maximum_fusion.4), channel_id=1, source_target_pairs={{0,16},{1,17},{4,20},{5,21},{8,24},{9,25},{12,28},{13,29},{18,2},{... | collective-permute-start | bytes 1769480 | tf_op jit(solution)/shard_map/ppermute | solution.py:84
  130.9 1.7 copy-start.2
  130.9 1.7 copy-start.15
  130.9 1.7 copy-start.17
  130.9 1.7 copy-start.18
  134.6 95.8 %all-to-all-start.1 = ((f32[4,16,64,128]{3,2,1,0:T(8,128)}), f32[4,16,64,128]{3,2,1,0:T(8,128)S(1)}, u32[]{:S(2)}, u32[]{:S(2)}) async-start(f32[4,16,64,128]{3,2,1,0:T(8,128)} %reverse_select_fusion.1), calls=%async_computation.1 | async-start | bytes 4194304 | tf_op jit(solution)/shard_map/all_to_all | solution.py:91
  187.1 13.8 %copy-start.9 = (f32[128,32]{1,0:T(8,128)S(1)}, f32[128,32]{1,0:T(8,128)}, u32[]{:S(2)}) copy-start(f32[128,32]{1,0:T(8,128)} %get-tuple-element.92) | copy-start | bytes 49156
  187.1 13.8 %copy-start.8 = (bf16[1,128,2048]{2,1,0:T(8,128)(2,1)S(1)}, bf16[1,128,2048]{2,1,0:T(8,128)(2,1)}, u32[]{:S(2)}) copy-start(bf16[1,128,2048]{2,1,0:T(8,128)(2,1)} %param.12) | copy-start | bytes 1572868
  187.1 15.1 %copy-start.12 = (f32[2048]{0:T(1024)S(1)}, f32[2048]{0:T(1024)}, u32[]{:S(2)}) copy-start(f32[2048]{0:T(1024)} %param.17) | copy-start | bytes 24580
  187.1 15.2 %copy-start.21 = (s32[16]{0:T(128)S(1)}, s32[16]{0:T(128)}, u32[]{:S(2)}) copy-start(s32[16]{0:T(128)} %param.19) | copy-start | bytes 196
  230.6 1.9 copy-start.5
  230.6 1.9 copy-start.11
  247.8 18.0 %collective-permute-start.3 = (bf16[128,1024]{1,0:T(8,128)(2,1)S(1)}, bf16[128,1024]{1,0:T(8,128)(2,1)S(1)}, u32[]{:S(2)}, u32[]{:S(2)}) collective-permute-start(bf16[128,1024]{1,0:T(8,128)(2,1)S(1)} %convolution_convert_fusion), channel_id=1, source_target_pairs={{28,32},{32,28},{60,64},{64,60},{92,96},{96,92},{124,128},{128,124... | collective-permute-start | bytes 786440 | tf_op jit(solution)/shard_map/ppermute | solution.py:189
Sparse Core Ops, SparseCore 0:
  59.8 68.6 all-gather.4
  131.0 93.5 all-gather.6

commit v4 on v3

--- a/solution.py
+++ b/solution.py
@@ -56,12 +56,19 @@
     return jnp.concatenate([states, rows], axis=-2)
 
 
-def scan_states(log_fwd, log_bwd, fresh_fwd, fresh_bwd):
+def scan_states(log_fwd, log_bwd, fresh_fwd, fresh_bwd, output_weight):
     packed = pack(jnp.stack([log_fwd, log_bwd]), jnp.stack([fresh_fwd, fresh_bwd]))
     parts = lax.axis_size("x")
     per_part = 2 * H // parts
-    packed = packed.reshape(parts, per_part, P_SIZE + PAD_ROWS, N)
-    mine = lax.all_to_all(packed, "x", 0, 0, tiled=True)
+    state_len = per_part * (P_SIZE + PAD_ROWS) * N
+    weight_flat = output_weight.astype(jnp.float32).reshape(1, -1)
+    send = jnp.concatenate(
+        [packed.reshape(parts, state_len), jnp.broadcast_to(weight_flat, (parts, weight_flat.shape[1]))],
+        axis=1,
+    )
+    got = lax.all_to_all(send, "x", 0, 0, tiled=True)
+    mine = got[:, :state_len].reshape(parts, per_part, P_SIZE + PAD_ROWS, N)
+    weight_row = got[:, state_len:].reshape((parts,) + output_weight.shape).astype(jnp.bfloat16)
     is_bwd = lax.axis_index("x") >= parts // 2
     ordered = jnp.where(is_bwd, mine[::-1], mine)
     logs, states = split_packed(ordered)
@@ -87,16 +94,15 @@
             total = combine(got, total)
         d *= 2
     out = jnp.stack([combine(entering, pre[k])[1] for k in range(ROW)])
-    out = jnp.where(is_bwd, out[::-1], out)
+    out = jnp.where(is_bwd, out[::-1], out).astype(jnp.bfloat16)
     back = lax.all_to_all(out, "x", 0, 0, tiled=True)
     back = back.reshape(2, H, P_SIZE, N)
-    return back[0], back[1]
-
-
-def gather_weight(output_weight):
-    column = lax.all_gather(output_weight, "z", axis=0)
-    row = lax.all_gather(column, "x", axis=1)
-    return row.transpose(2, 0, 1, 3).reshape(output_weight.shape[0], -1)
+    return back[0], back[1], weight_row
+
+
+def gather_weight(weight_row):
+    whole = lax.all_gather(weight_row, "z", axis=0)
+    return whole.transpose(2, 0, 1, 3).reshape(weight_row.shape[1], -1)
 
 
 def per_device(
@@ -140,7 +146,9 @@
     fresh_bwd = jnp.einsum(
         "shp,shn->hpn", head_frames, weighted_bwd, preferred_element_type=jnp.float32
     )
-    state_fwd, state_bwd = scan_states(running_fwd[-1], running_bwd[0], fresh_fwd, fresh_bwd)
+    state_fwd, state_bwd, weight_row = scan_states(
+        running_fwd[-1], running_bwd[0], fresh_fwd, fresh_bwd, output_weight
+    )
     scores = jnp.dot(c_rows, b_rows.T, preferred_element_type=jnp.float32)
     lower_mask = jnp.arange(frame_count)[:, None] >= jnp.arange(frame_count)[None, :]
 
@@ -159,12 +167,11 @@
     grouped_frames = head_frames.reshape(frame_count, group_count, 4, P_SIZE).transpose(1, 0, 2, 3)
     local_groups = lax.map(group_mix, (grouped_fwd, grouped_bwd, grouped_frames))
     local_part = local_groups.transpose(1, 0, 2, 3).reshape(frame_count, H, P_SIZE)
-    c_float = c_rows.astype(jnp.float32)
     carried_fwd = jnp.exp(running_fwd)[:, :, None] * jnp.einsum(
-        "hpn,tn->thp", state_fwd, c_float, precision=lax.Precision.HIGHEST
+        "hpn,tn->thp", state_fwd, c_rows, preferred_element_type=jnp.float32
     )
     carried_bwd = jnp.exp(running_bwd)[:, :, None] * jnp.einsum(
-        "hpn,tn->thp", state_bwd, c_float, precision=lax.Precision.HIGHEST
+        "hpn,tn->thp", state_bwd, c_rows, preferred_element_type=jnp.float32
     )
     summed = local_part + carried_fwd + carried_bwd
     gated_rows = summed * jax.nn.silu(gate_channels[0].astype(jnp.float32)).reshape(
@@ -176,7 +183,7 @@
     ).astype(jnp.bfloat16)
     projected_rows = jnp.dot(
         normed,
-        gather_weight(output_weight),
+        gather_weight(weight_row),
         preferred_element_type=jnp.float32,
     ).astype(jnp.bfloat16)
     window_index = lax.axis_index("win")

time: 275 us -> 290 us (1.055)
  starting transfers between devices: 94.8 us -> 129 us
  waiting for transfers between devices: 99.1 us -> 71.4 us
  matrix products: 14.1 us -> 21.8 us
    ppermute x3, starting transfers between devices: 27.5 us -> 80.9 us  [scan_states(): got = split_packed(lax.ppermute(pack(*total), ('z', 'x'), pairs))]
    all_to_all x1, waiting for transfers between devices: 26.8 us -> 0.01 us  [scan_states(): back = lax.all_to_all(out, 'x', 0, 0, tiled=True)]
    all_to_all x1, starting transfers between devices: 52.5 us -> 32.1 us  [scan_states(): back = lax.all_to_all(out, 'x', 0, 0, tiled=True)]
    all_to_all x1, waiting for transfers between devices: 29.4 us -> 40.4 us  [scan_states(): got = lax.all_to_all(send, 'x', 0, 0, tiled=True)]
    all_gather x2 -> x0, local copies, waits for them, and re-layouts: 10.2 us -> none  [the longest x1 7.87 us: gather_weight(): row = lax.all_gather(column, 'x', axis=1)]
    dot_general x8, matrix products: 8.03 us -> 14.8 us  [group_mix(): jnp.einsum('hts,shp->thp', mixing, group_frames, preferred_element_type=j...]
    ppermute x3, waiting for transfers between devices: 30.4 us -> 24.8 us  [scan_states(): got = split_packed(lax.ppermute(pack(*total), ('z', 'x'), pairs))]
    convert_element_type x0 -> x2, local copies, waits for them, and re-layouts: none -> 5.23 us  [scan_states(): got[:, state_len:].reshape((parts,) + output_weight.shape)]
  transfers between devices with their start and end apart: 8 -> 7, of which waited for: 6 -> 5; matrix products, arithmetic and copies ran while one was open for 12% -> 13% of each run, Pallas kernels for 0% -> 0%
where the time goes in v4:
time: 290 us; the launch traced here: 287 us
  starting transfers between devices  129 us (44%)
  waiting for transfers between devices  71.4 us (25%)
  local copies, waits for them, and re-layouts  30.8 us (11%)
  matrix products  21.8 us (8%)
  other arithmetic  20.6 us (7%)
  between operations  13.8 us (5%)
    ppermute x3, starting transfers between devices, scan_states(): got = split_packed(lax.ppermute(pack(*total), ('z', 'x'), pairs))  80.9 us
    all_to_all x1, waiting for transfers between devices, scan_states(): got = lax.all_to_all(send, 'x', 0, 0, tiled=True)  40.4 us
    all_to_all x1, starting transfers between devices, scan_states(): back = lax.all_to_all(out, 'x', 0, 0, tiled=True)  32.1 us
    ppermute x3, waiting for transfers between devices, scan_states(): got = split_packed(lax.ppermute(pack(*total), ('z', 'x'), pairs))  24.8 us
    dot_general x8, matrix products, group_mix(): jnp.einsum('hts,shp->thp', mixing, group_frames, preferred_element_type=j...  14.8 us
    ppermute x1, starting transfers between devices, per_device(): partner = lax.ppermute(projected_rows, ('win', 'z'), pairs)  11.6 us
    ppermute x1, waiting for transfers between devices, per_device(): partner = lax.ppermute(projected_rows, ('win', 'z'), pairs)  6.26 us
    unnamed x44, local copies, waits for them, and re-layouts  6.12 us
  transfers between devices with their start and end apart: 7, of which 5 were waited for; matrix products, arithmetic and copies ran while one was open for 13% of the time, Pallas kernels for 0%

profile of v4, /device:TPU:24, one launch (start us, length us, event | category | flops | bytes accessed | tf_op | source)
XLA Modules:
  0.0 287.4 jit_solution(12791049014200509700)
XLA Ops:
  6.5 0.7 multiply_bitcast_fusion
  7.2 0.8 compare_select_fusion
  8.8 0.8 bitcast_convert_fusion
  9.6 0.6 fusion.44
  10.3 1.3 copy.70
  11.7 0.7 fusion.45
  12.3 0.8 convolution_bitcast_fusion.4
  13.1 0.8 convolution_bitcast_fusion.3
  14.1 1.6 pad_maximum_fusion.1
  15.7 2.8 reshape.305
  18.5 1.1 copy.78
  19.6 1.0 reshape.323
  20.6 1.0 pad.11.clone
  21.6 2.1 pad_maximum_fusion
  23.8 4.7 %all_to_all.11 = f32[4,1,212992]{2,1,0:T(1,128)} reshape(f32[4,212992]{1,0:T(4,128)S(1)} %pad_maximum_fusion) | data formatting | bytes 6815744 | tf_op jit(solution)/shard_map/all_to_all | solution.py:69
  28.4 4.3 %all-to-all-start = ((f32[4,1,212992]{2,1,0:T(1,128)}), f32[4,1,212992]{2,1,0:T(1,128)S(1)}, u32[]{:S(2)}, u32[]{:S(2)}) async-start(f32[4,1,212992]{2,1,0:T(1,128)} %all_to_all.11), calls=%async_computation | async-start | bytes 6815744 | tf_op jit(solution)/shard_map/all_to_all | solution.py:69
  32.7 40.4 %all-to-all-done = f32[4,1,212992]{2,1,0:T(1,128)S(1)} async-done(((f32[4,1,212992]{2,1,0:T(1,128)}), f32[4,1,212992]{2,1,0:T(1,128)S(1)}, u32[]{:S(2)}, u32[]{:S(2)}) %all-to-all-start) | async-done | bytes 3407904 | tf_op jit(solution)/shard_map/all_to_all | solution.py:69
  73.1 3.5 %copy.85 = f32[4,1,212992]{2,0,1:T(4,128)S(1)} copy(f32[4,1,212992]{2,1,0:T(1,128)S(1)} %all-to-all-done) | data formatting | bytes 6815744
  77.2 0.8 exponential_reduce_fusion
  78.2 1.0 fusion.27
  79.3 3.9 %collective-permute-start = (f32[16,72,128]{2,1,0:T(8,128)S(1)}, f32[16,72,128]{2,1,0:T(8,128)S(1)}, u32[]{:S(2)}, u32[]{:S(2)}) collective-permute-start(f32[16,72,128]{2,1,0:T(8,128)S(1)} %pad_maximum_fusion.3), channel_id=1, source_target_pairs={{0,4},{1,5},{4,8},{5,9},{6,2},{7,3},{8,12},{9,13},{10,6},{11,7},{1... | collective-permute-start | bytes 1769480 | tf_op jit(solution)/shard_map/ppermute | solution.py:91
  83.2 11.3 %collective-permute-done = f32[16,72,128]{2,1,0:T(8,128)S(1)} collective-permute-done((f32[16,72,128]{2,1,0:T(8,128)S(1)}, f32[16,72,128]{2,1,0:T(8,128)S(1)}, u32[]{:S(2)}, u32[]{:S(2)}) %collective-permute-start) | collective-permute-done | bytes 589856 | tf_op jit(solution)/shard_map/ppermute | solution.py:91
  94.6 0.7 fusion.40
  95.4 0.9 pad_maximum_fusion.4
  96.3 6.6 %collective-permute-start.1 = (f32[16,72,128]{2,1,0:T(8,128)}, f32[16,72,128]{2,1,0:T(8,128)}, u32[]{:S(2)}, u32[]{:S(2)}) collective-permute-start(f32[16,72,128]{2,1,0:T(8,128)} %pad_maximum_fusion.4), channel_id=1, source_target_pairs={{0,8},{1,9},{4,12},{5,13},{8,16},{9,17},{10,2},{11,3},{12,20},{13,... | collective-permute-start | bytes 1769480 | tf_op jit(solution)/shard_map/ppermute | solution.py:91
  103.0 2.6 convert_element_type.104
  105.6 2.6 copy.81
  108.3 4.5 %collective-permute-done.1 = f32[16,72,128]{2,1,0:T(8,128)} collective-permute-done((f32[16,72,128]{2,1,0:T(8,128)}, f32[16,72,128]{2,1,0:T(8,128)}, u32[]{:S(2)}, u32[]{:S(2)}) %collective-permute-start.1) | collective-permute-done | bytes 589856 | tf_op jit(solution)/shard_map/ppermute | solution.py:91
  112.8 1.6 exponential_reduce_fusion.4
  114.5 1.2 multiply_add_fusion
  115.7 0.9 pad_maximum_fusion.5
  116.6 70.4 %collective-permute-start.2 = (f32[16,72,128]{2,1,0:T(8,128)}, f32[16,72,128]{2,1,0:T(8,128)}, u32[]{:S(2)}, u32[]{:S(2)}) collective-permute-start(f32[16,72,128]{2,1,0:T(8,128)} %pad_maximum_fusion.5), channel_id=1, source_target_pairs={{0,16},{1,17},{4,20},{5,21},{8,24},{9,25},{12,28},{13,29},{18,2},{... | collective-permute-start | bytes 1769480 | tf_op jit(solution)/shard_map/ppermute | solution.py:91
  187.1 1.5 copy.72
  188.6 0.8 fusion.34
  189.4 8.9 %collective-permute-done.2 = f32[16,72,128]{2,1,0:T(8,128)} collective-permute-done((f32[16,72,128]{2,1,0:T(8,128)}, f32[16,72,128]{2,1,0:T(8,128)}, u32[]{:S(2)}, u32[]{:S(2)}) %collective-permute-start.2) | collective-permute-done | bytes 589856 | tf_op jit(solution)/shard_map/ppermute | solution.py:91
  198.3 1.5 add_bitcast_fusion.2
  200.2 1.3 fusion.12
  201.5 32.1 %all-to-all-start.1 = ((bf16[4,16,64,128]{3,2,1,0:T(8,128)(2,1)}), bf16[4,16,64,128]{3,2,1,0:T(8,128)(2,1)S(1)}, u32[]{:S(2)}, u32[]{:S(2)}) async-start(bf16[4,16,64,128]{3,2,1,0:T(8,128)(2,1)} %fusion.12), calls=%async_computation.1 | async-start | bytes 2097152 | tf_op jit(solution)/shard_map/all_to_all | solution.py:98
  233.6 20.4 %while.11 = (s32[]{:T(128)}, f32[8,128,4,64]{1,3,2,0:T(8,128)}, bf16[8,128,4,64]{1,3,2,0:T(8,128)(2,1)}, f32[128,128]{1,0:T(8,128)S(1)}, f32[8,4,128]{2,1,0:T(4,128)}, /*index=5*/f32[8,4,128]{2,1,0:T(4,128)S(1)}, s32[]{:T(128)}) while((s32[]{:T(128)}, f32[8,128,4,64]{1,3,2,0:T(8,128)}, bf16[8,128,4,64]{1,3,2,0:T(8,128)(2,1)}, ...), condition=%wide.region_4.5_spmd.clone, body=%wide.region_3.4_spmd.clone.sunk | while | flops 8732674 | bytes 312409 | solution.py:168
  233.6 0.7 dynamic-slice_bitcast_fusion.3
  234.3 1.8 fusion.55
  236.2 0.7 dynamic-slice_bitcast_fusion.3
  236.9 1.9 fusion.55
  238.7 0.7 dynamic-slice_bitcast_fusion.3
  239.4 1.9 fusion.55
  241.3 0.7 dynamic-slice_bitcast_fusion.3
  242.0 1.9 fusion.55
  243.9 0.7 dynamic-slice_bitcast_fusion.3
  244.6 1.9 fusion.55
  246.4 0.7 dynamic-slice_bitcast_fusion.3
  247.1 1.8 fusion.55
  249.0 0.7 dynamic-slice_bitcast_fusion.3
  249.7 1.8 fusion.55
  251.5 0.7 dynamic-slice_bitcast_fusion.3
  252.2 1.8 fusion.55
  254.4 0.6 dynamic_slice.14
  255.0 0.6 iota_compare_fusion.1
  256.1 0.8 copy-done.19
  257.0 0.5 multiply_reduce_fusion
  257.5 0.3 multiply_convert_fusion.6
  257.9 3.7 %convolution_convert_fusion = bf16[128,1024]{1,0:T(8,128)(2,1)S(1)} fusion(bf16[128,2048]{0,1:T(8,128)(2,1)S(1)} %bitcast.146, bf16[2048,1024]{0,1:T(8,128)(2,1)} %bitcast.145), kind=kOutput, calls=%fused_computation.35 | convolution fusion | flops 537001984 | bytes 4980736 | tf_op jit(solution)/shard_map/dot_general | solution.py:184
  261.6 11.6 %collective-permute-start.3 = (bf16[128,1024]{1,0:T(8,128)(2,1)S(1)}, bf16[128,1024]{1,0:T(8,128)(2,1)S(1)}, u32[]{:S(2)}, u32[]{:S(2)}) collective-permute-start(bf16[128,1024]{1,0:T(8,128)(2,1)S(1)} %convolution_convert_fusion), channel_id=1, source_target_pairs={{28,32},{32,28},{60,64},{64,60},{92,96},{96,92},{124,128},{128,124... | collective-permute-start | bytes 786440 | tf_op jit(solution)/shard_map/ppermute | solution.py:196
  273.3 6.3 %collective-permute-done.3 = bf16[128,1024]{1,0:T(8,128)(2,1)S(1)} collective-permute-done((bf16[128,1024]{1,0:T(8,128)(2,1)S(1)}, bf16[128,1024]{1,0:T(8,128)(2,1)S(1)}, u32[]{:S(2)}, u32[]{:S(2)}) %collective-permute-start.3) | collective-permute-done | bytes 262176 | tf_op jit(solution)/shard_map/ppermute | solution.py:196
  279.6 0.9 fusion.31
  (89 shorter events, 3.8 us)
Async XLA Ops:
  6.5 182.0 %copy-start = (bf16[1,128,128]{2,1,0:T(8,128)(2,1)S(1)}, bf16[1,128,128]{2,1,0:T(8,128)(2,1)}, u32[]{:S(2)}) copy-start(bf16[1,128,128]{2,1,0:T(8,128)(2,1)} %param.14) | copy-start | bytes 98308
  8.8 1.4 copy-start.5
  11.7 2.4 copy-start.1
  28.4 44.7 %all-to-all-start = ((f32[4,1,212992]{2,1,0:T(1,128)}), f32[4,1,212992]{2,1,0:T(1,128)S(1)}, u32[]{:S(2)}, u32[]{:S(2)}) async-start(f32[4,1,212992]{2,1,0:T(1,128)} %all_to_all.11), calls=%async_computation | async-start | bytes 6815744 | tf_op jit(solution)/shard_map/all_to_all | solution.py:69
  32.7 225.2 %all-gather.2.cloned.1.call-start = ((), (), s32[]{:S(2)}) async-start(), calls=%async_computation.2 | async-start | bytes 4718592 | tf_op jit(solution)/shard_map/all_gather | solution.py:104
  78.0 5.2 %copy-start.12 = (f32[16]{0:T(128)}, f32[16]{0:T(128)S(1)}, u32[]{:S(2)}) copy-start(f32[16]{0:T(128)S(1)} %get-tuple-element.65) | copy-start | bytes 196
  78.0 5.3 %copy-start.16 = (f32[16]{0:T(128)}, f32[16]{0:T(128)S(1)}, u32[]{:S(2)}) copy-start(f32[16]{0:T(128)S(1)} %get-tuple-element.67) | copy-start | bytes 196
  78.0 5.3 %copy-start.17 = (f32[16]{0:T(128)}, f32[16]{0:T(128)S(1)}, u32[]{:S(2)}) copy-start(f32[16]{0:T(128)S(1)} %broadcast_multiply_fusion) | copy-start | bytes 196
  79.3 15.2 %collective-permute-start = (f32[16,72,128]{2,1,0:T(8,128)S(1)}, f32[16,72,128]{2,1,0:T(8,128)S(1)}, u32[]{:S(2)}, u32[]{:S(2)}) collective-permute-start(f32[16,72,128]{2,1,0:T(8,128)S(1)} %pad_maximum_fusion.3), channel_id=1, source_target_pairs={{0,4},{1,5},{4,8},{5,9},{6,2},{7,3},{8,12},{9,13},{10,6},{11,7},{1... | collective-permute-start | bytes 1769480 | tf_op jit(solution)/shard_map/ppermute | solution.py:91
  94.5 1.7 copy-start.3
  96.3 16.6 %collective-permute-start.1 = (f32[16,72,128]{2,1,0:T(8,128)}, f32[16,72,128]{2,1,0:T(8,128)}, u32[]{:S(2)}, u32[]{:S(2)}) collective-permute-start(f32[16,72,128]{2,1,0:T(8,128)} %pad_maximum_fusion.4), channel_id=1, source_target_pairs={{0,8},{1,9},{4,12},{5,13},{8,16},{9,17},{10,2},{11,3},{12,20},{13,... | collective-permute-start | bytes 1769480 | tf_op jit(solution)/shard_map/ppermute | solution.py:91
  105.6 7.2 %copy-start.4 = (f32[16,72,128]{2,1,0:T(8,128)S(1)}, f32[16,72,128]{2,1,0:T(8,128)}, u32[]{:S(2)}) copy-start(f32[16,72,128]{2,1,0:T(8,128)} %copy-done.3) | copy-start | bytes 1769476
  108.2 80.3 %copy-start.8 = (bf16[1,128,128]{2,1,0:T(8,128)(2,1)S(1)}, bf16[1,128,128]{2,1,0:T(8,128)(2,1)}, u32[]{:S(2)}) copy-start(bf16[1,128,128]{2,1,0:T(8,128)(2,1)} %param.13) | copy-start | bytes 98308
  115.6 84.1 %copy-start.2 = (f32[16,64,128]{2,1,0:T(8,128)S(1)}, f32[16,64,128]{2,1,0:T(8,128)}, u32[]{:S(2)}) copy-start(f32[16,64,128]{2,1,0:T(8,128)} %get-tuple-element.90) | copy-start | bytes 1572868
  116.6 81.7 %collective-permute-start.2 = (f32[16,72,128]{2,1,0:T(8,128)}, f32[16,72,128]{2,1,0:T(8,128)}, u32[]{:S(2)}, u32[]{:S(2)}) collective-permute-start(f32[16,72,128]{2,1,0:T(8,128)} %pad_maximum_fusion.5), channel_id=1, source_target_pairs={{0,16},{1,17},{4,20},{5,21},{8,24},{9,25},{12,28},{13,29},{18,2},{... | collective-permute-start | bytes 1769480 | tf_op jit(solution)/shard_map/ppermute | solution.py:91
  188.6 11.2 %copy-start.13 = (f32[16]{0:T(128)S(1)}, f32[16]{0:T(128)}, u32[]{:S(2)}) copy-start(f32[16]{0:T(128)} %copy-done.12) | copy-start | bytes 196
  188.6 11.2 %copy-start.14 = (f32[16]{0:T(128)S(1)}, f32[16]{0:T(128)}, u32[]{:S(2)}) copy-start(f32[16]{0:T(128)} %get-tuple-element.63) | copy-start | bytes 196
  188.6 11.2 %copy-start.15 = (f32[16]{0:T(128)S(1)}, f32[16]{0:T(128)}, u32[]{:S(2)}) copy-start(f32[16]{0:T(128)} %get-tuple-element.72) | copy-start | bytes 196
  200.2 33.4 %copy-start.10 = (f32[128,128]{1,0:T(8,128)S(1)}, f32[128,128]{1,0:T(8,128)}, u32[]{:S(2)}) copy-start(f32[128,128]{1,0:T(8,128)} %fusion.34) | copy-start | bytes 196612
  201.5 52.5 %copy-start.11 = (f32[2048]{0:T(1024)S(1)}, f32[2048]{0:T(1024)}, u32[]{:S(2)}) copy-start(f32[2048]{0:T(1024)} %param.17) | copy-start | bytes 24580
  201.5 52.6 %copy-start.7 = (f32[128,32]{1,0:T(8,128)S(1)}, f32[128,32]{1,0:T(8,128)}, u32[]{:S(2)}) copy-start(f32[128,32]{1,0:T(8,128)} %get-tuple-element.100) | copy-start | bytes 49156
  201.5 52.6 %copy-start.6 = (bf16[1,128,2048]{2,1,0:T(8,128)(2,1)S(1)}, bf16[1,128,2048]{2,1,0:T(8,128)(2,1)}, u32[]{:S(2)}) copy-start(bf16[1,128,2048]{2,1,0:T(8,128)(2,1)} %param.12) | copy-start | bytes 1572868
  201.5 54.2 %all-to-all-start.1 = ((bf16[4,16,64,128]{3,2,1,0:T(8,128)(2,1)}), bf16[4,16,64,128]{3,2,1,0:T(8,128)(2,1)S(1)}, u32[]{:S(2)}, u32[]{:S(2)}) async-start(bf16[4,16,64,128]{3,2,1,0:T(8,128)(2,1)} %fusion.12), calls=%async_computation.1 | async-start | bytes 2097152 | tf_op jit(solution)/shard_map/all_to_all | solution.py:98
  233.6 20.8 %copy-start.18 = (s32[16]{0:T(128)S(1)}, s32[16]{0:T(128)}, u32[]{:S(2)}) copy-start(s32[16]{0:T(128)} %param.19) | copy-start | bytes 196
  254.0 1.8 copy-start.9
  255.7 1.2 copy-start.19
  261.6 18.0 %collective-permute-start.3 = (bf16[128,1024]{1,0:T(8,128)(2,1)S(1)}, bf16[128,1024]{1,0:T(8,128)(2,1)S(1)}, u32[]{:S(2)}, u32[]{:S(2)}) collective-permute-start(bf16[128,1024]{1,0:T(8,128)(2,1)S(1)} %convolution_convert_fusion), channel_id=1, source_target_pairs={{28,32},{32,28},{60,64},{64,60},{92,96},{96,92},{124,128},{128,124... | collective-permute-start | bytes 786440 | tf_op jit(solution)/shard_map/ppermute | solution.py:196
Sparse Core Ops, SparseCore 0:
  108.4 147.8 all-gather.1

commit v5 on v3

--- a/solution.py
+++ b/solution.py
@@ -94,9 +94,20 @@
 
 
 def gather_weight(output_weight):
-    column = lax.all_gather(output_weight, "z", axis=0)
+    half = lax.axis_index("win") % 2
+    half_rows = output_weight.shape[0] // 2
+    mine = lax.dynamic_slice_in_dim(output_weight, half * half_rows, half_rows, axis=0)
+    column = lax.all_gather(mine, "z", axis=0)
     row = lax.all_gather(column, "x", axis=1)
-    return row.transpose(2, 0, 1, 3).reshape(output_weight.shape[0], -1)
+    gathered = row.transpose(2, 0, 1, 3).reshape(half_rows, -1)
+    wins = lax.axis_size("win")
+    pairs = [(w, w ^ 1) for w in range(wins)]
+    other = lax.ppermute(gathered, "win", pairs)
+    return jnp.where(
+        half == 0,
+        jnp.concatenate([gathered, other], axis=0),
+        jnp.concatenate([other, gathered], axis=0),
+    )
 
 
 def per_device(

time: 275 us -> 296 us (1.076); the launches traced: 274 us -> 290 us
  blocking collectives: 0 us -> 79.1 us
  starting transfers between devices: 94.8 us -> 53.2 us
  waiting for transfers between devices: 99.1 us -> 78.2 us
  matrix products: 14.1 us -> 18.9 us
  local copies, waits for them, and re-layouts: 30.3 us -> 26.2 us
    all_gather x0 -> x1, blocking collectives: none -> 79.1 us  [gather_weight(): column = lax.all_gather(mine, 'z', axis=0)]
    all_to_all x1, starting transfers between devices: 52.5 us -> 3.74 us  [scan_states(): back = lax.all_to_all(out, 'x', 0, 0, tiled=True)]
    all_to_all x1, waiting for transfers between devices: 26.8 us -> 0.01 us  [scan_states(): back = lax.all_to_all(out, 'x', 0, 0, tiled=True)]
    all_gather x1, waiting for transfers between devices: 0.02 us -> 17.4 us  [gather_weight(): row = lax.all_gather(column, 'x', axis=1)]
    ppermute x3, waiting for transfers between devices: 30.4 us -> 21.9 us  [scan_states(): got = split_packed(lax.ppermute(pack(*total), ('z', 'x'), pairs))]
    ppermute x3, starting transfers between devices: 27.5 us -> 34.6 us  [scan_states(): got = split_packed(lax.ppermute(pack(*total), ('z', 'x'), pairs))]
    all_gather x1 -> x0, waiting for transfers between devices: 4.79 us -> none  [gather_weight(): column = lax.all_gather(output_weight, 'z', axis=0)]
    dot_general x1, matrix products: 1.53 us -> 5.04 us  [per_device(): jnp.dot(normed, gather_weight(output_weight), preferred_element_type=jnp....]
  transfers between devices with their start and end apart: 8 -> 8, of which waited for: 6 -> 5; matrix products, arithmetic and copies ran while one was open for 12% -> 12% of each run, Pallas kernels for 0% -> 0%
where the time goes in v5:
time: 296 us; the launch traced here: 290 us
  blocking collectives  79.1 us (27%)
  waiting for transfers between devices  78.2 us (26%)
  starting transfers between devices  53.2 us (18%)
  local copies, waits for them, and re-layouts  26.2 us (9%)
  other arithmetic  20.6 us (7%)
  matrix products  18.9 us (6%)
  between operations  13.8 us (5%)
    all_gather x1, blocking collectives, gather_weight(): column = lax.all_gather(mine, 'z', axis=0)  79.1 us
    ppermute x3, starting transfers between devices, scan_states(): got = split_packed(lax.ppermute(pack(*total), ('z', 'x'), pairs))  34.6 us
    all_to_all x1, waiting for transfers between devices, scan_states(): mine = lax.all_to_all(packed, 'x', 0, 0, tiled=True)  29.4 us
    ppermute x3, waiting for transfers between devices, scan_states(): got = split_packed(lax.ppermute(pack(*total), ('z', 'x'), pairs))  21.9 us
    all_gather x1, waiting for transfers between devices, gather_weight(): row = lax.all_gather(column, 'x', axis=1)  17.4 us
    ppermute x1, waiting for transfers between devices, per_device(): partner = lax.ppermute(projected_rows, ('win', 'z'), pairs)  9.49 us
    ppermute x1, starting transfers between devices, per_device(): partner = lax.ppermute(projected_rows, ('win', 'z'), pairs)  8.33 us
    dot_general x8, matrix products, group_mix(): jnp.einsum('hts,shp->thp', mixing, group_frames, preferred_element_type=j...  8 us
  transfers between devices with their start and end apart: 8, of which 5 were waited for; matrix products, arithmetic and copies ran while one was open for 12% of the time, Pallas kernels for 0%

profile of v5, /device:TPU:24, one launch (start us, length us, event | category | flops | bytes accessed | tf_op | source)
XLA Modules:
  0.0 289.9 jit_solution(1249156855436761947)
XLA Ops:
  6.5 0.8 compare_select_fusion
  7.3 0.7 multiply_bitcast_fusion
  8.7 0.7 fusion.52
  9.5 1.3 copy.88
  10.8 0.8 bitcast_convert_fusion
  11.6 0.6 fusion.53
  12.3 0.8 convolution_bitcast_fusion.4
  13.1 0.8 convolution_bitcast_fusion.3
  14.0 1.6 pad_maximum_fusion
  15.6 4.5 %all-to-all-start = ((f32[4,16,72,128]{3,2,1,0:T(8,128)}), f32[4,16,72,128]{3,2,1,0:T(8,128)}, u32[]{:S(2)}, u32[]{:S(2)}) async-start(f32[4,16,72,128]{3,2,1,0:T(8,128)} %bitcast.21), calls=%async_computation | async-start | bytes 4718592 | tf_op jit(solution)/shard_map/all_to_all | solution.py:64
  20.2 29.4 %all-to-all-done = f32[4,16,72,128]{3,2,1,0:T(8,128)} async-done(((f32[4,16,72,128]{3,2,1,0:T(8,128)}), f32[4,16,72,128]{3,2,1,0:T(8,128)}, u32[]{:S(2)}, u32[]{:S(2)}) %all-to-all-start) | async-done | bytes 2359328 | tf_op jit(solution)/shard_map/all_to_all | solution.py:64
  49.6 2.6 reverse_select_fusion
  52.2 0.9 exponential_reduce_fusion
  53.1 1.0 fusion.35
  54.2 0.7 copy-done.1
  55.0 3.9 %collective-permute-start = (f32[16,72,128]{2,1,0:T(8,128)S(1)}, f32[16,72,128]{2,1,0:T(8,128)S(1)}, u32[]{:S(2)}, u32[]{:S(2)}) collective-permute-start(f32[16,72,128]{2,1,0:T(8,128)S(1)} %pad_maximum_fusion.2), channel_id=1, source_target_pairs={{0,4},{1,5},{4,8},{5,9},{6,2},{7,3},{8,12},{9,13},{10,6},{11,7},{1... | collective-permute-start | bytes 1769480 | tf_op jit(solution)/shard_map/ppermute | solution.py:84
  59.4 11.1 %collective-permute-done = f32[16,72,128]{2,1,0:T(8,128)S(1)} collective-permute-done((f32[16,72,128]{2,1,0:T(8,128)S(1)}, f32[16,72,128]{2,1,0:T(8,128)S(1)}, u32[]{:S(2)}, u32[]{:S(2)}) %collective-permute-start) | collective-permute-done | bytes 589856 | tf_op jit(solution)/shard_map/ppermute | solution.py:84
  70.5 0.8 copy-done.3
  72.0 1.3 multiply_add_fusion.1
  73.5 5.8 %collective-permute-start.1 = (f32[16,72,128]{2,1,0:T(8,128)S(1)}, f32[16,72,128]{2,1,0:T(8,128)S(1)}, u32[]{:S(2)}, u32[]{:S(2)}) collective-permute-start(f32[16,72,128]{2,1,0:T(8,128)S(1)} %pad_maximum_fusion.3), channel_id=1, source_target_pairs={{0,8},{1,9},{4,12},{5,13},{8,16},{9,17},{10,2},{11,3},{12,20},{13,... | collective-permute-start | bytes 1769480 | tf_op jit(solution)/shard_map/ppermute | solution.py:84
  79.3 10.8 %collective-permute-done.1 = f32[16,72,128]{2,1,0:T(8,128)S(1)} collective-permute-done((f32[16,72,128]{2,1,0:T(8,128)S(1)}, f32[16,72,128]{2,1,0:T(8,128)S(1)}, u32[]{:S(2)}, u32[]{:S(2)}) %collective-permute-start.1) | collective-permute-done | bytes 589856 | tf_op jit(solution)/shard_map/ppermute | solution.py:84
  90.1 0.8 copy-done.4
  90.9 0.6 slice.107
  91.5 1.3 copy.102
  92.8 1.2 exponential_bitcast_fusion.2
  94.0 1.2 multiply_add_fusion
  95.3 0.9 pad_maximum_fusion.4
  96.2 25.0 %collective-permute-start.2 = (f32[16,72,128]{2,1,0:T(8,128)}, f32[16,72,128]{2,1,0:T(8,128)}, u32[]{:S(2)}, u32[]{:S(2)}) collective-permute-start(f32[16,72,128]{2,1,0:T(8,128)} %pad_maximum_fusion.4), channel_id=1, source_target_pairs={{0,16},{1,17},{4,20},{5,21},{8,24},{9,25},{12,28},{13,29},{18,2},{... | collective-permute-start | bytes 1769480 | tf_op jit(solution)/shard_map/ppermute | solution.py:84
  121.1 79.1 %all-gather = bf16[8192,32]{0,1:T(8,128)(2,1)S(1)} all-gather(bf16[1024,32]{0,1:T(8,128)(2,1)S(1)} %constant_dynamic-slice_fusion), channel_id=2, replica_groups=mesh['win'=16,'z'=8,'x'=4] {'z'}, dimensions={0}, use_global_device_ids=true | all-gather | bytes 589824 | tf_op jit(solution)/shard_map/all_gather | solution.py:100
  200.2 0.8 copy.105
  201.1 1.5 copy.90
  202.6 1.6 fusion.42
  204.2 1.6 add_bitcast_fusion.2
  206.3 1.5 reverse_select_fusion.1
  207.8 3.7 %all-to-all-start.1 = ((f32[4,16,64,128]{3,2,1,0:T(8,128)}), f32[4,16,64,128]{3,2,1,0:T(8,128)S(1)}, u32[]{:S(2)}, u32[]{:S(2)}) async-start(f32[4,16,64,128]{3,2,1,0:T(8,128)} %reverse_select_fusion.1), calls=%async_computation.1 | async-start | bytes 4194304 | tf_op jit(solution)/shard_map/all_to_all | solution.py:91
  211.6 13.5 %while.11 = (s32[]{:T(128)}, f32[8,128,4,64]{1,3,2,0:T(8,128)}, bf16[8,128,4,64]{1,3,2,0:T(8,128)(2,1)S(1)}, f32[128,128]{1,0:T(8,128)S(1)}, f32[8,4,128]{2,1,0:T(4,128)}, /*index=5*/f32[8,4,128]{2,1,0:T(4,128)S(1)}, s32[]{:T(128)}) while((s32[]{:T(128)}, f32[8,128,4,64]{1,3,2,0:T(8,128)}, bf16[8,128,4,64]{1,3,2,0:T(8,128)(2,1)S(1)}, ...), condition=%wide.region_4.5_spmd.clone, body=%wide.region_3.4_spmd.clone.sunk | while | flops 8732674 | bytes 312401 | solution.py:171
  211.6 0.7 dynamic-slice_bitcast_fusion.3
  212.3 1.0 fusion.62
  213.3 0.7 dynamic-slice_bitcast_fusion.3
  214.0 1.0 fusion.62
  215.0 0.7 dynamic-slice_bitcast_fusion.3
  215.7 1.0 fusion.62
  216.7 0.7 dynamic-slice_bitcast_fusion.3
  217.3 1.0 fusion.62
  218.3 0.7 dynamic-slice_bitcast_fusion.3
  219.0 1.0 fusion.62
  220.0 0.7 dynamic-slice_bitcast_fusion.3
  220.7 1.0 fusion.62
  221.7 0.7 dynamic-slice_bitcast_fusion.3
  222.4 1.0 fusion.62
  223.4 0.7 dynamic-slice_bitcast_fusion.3
  224.1 1.0 fusion.62
  225.7 17.4 %all-gather.4.cloned.1.call-done = bf16[8,4096,32]{1,2,0:T(8,128)(2,1)} async-done(((bf16[8,1024,32]{1,2,0:T(8,128)(2,1)}), bf16[8,4096,32]{1,2,0:T(8,128)(2,1)}) %all-gather.4.cloned.1.call-update) | async-done | bytes 2097168 | tf_op jit(solution)/shard_map/all_gather | solution.py:101
  243.1 4.5 %reshape.287 = bf16[8,4,1024,32]{2,1,3,0:T(4,128)(2,1)} reshape(bf16[8,4096,32]{1,2,0:T(8,128)(2,1)} %all-gather.4.cloned.1.call-done) | data formatting | bytes 4194304 | tf_op jit(solution)/shard_map/all_gather | solution.py:101
  247.6 3.7 %copy.100 = bf16[1024,8,4,32]{0,3,2,1:T(8,128)(2,1)} copy(bf16[1024,8,4,32]{0,2,3,1:T(4,128)(2,1)} %bitcast.152) | data formatting | bytes 4194304 | tf_op jit(solution)/shard_map/transpose | solution.py:102
  251.3 1.9 collective-permute-start.3
  253.2 0.7 iota_compare_fusion.1
  253.9 1.3 copy.98
  256.0 1.8 fusion.22
  257.8 0.8 multiply_reduce_fusion
  259.2 5.0 %fusion.24 = bf16[128,1024]{1,0:T(8,128)(2,1)S(1)} fusion(bf16[128,2048]{0,1:T(8,128)(2,1)S(1)} %fusion.25, bf16[1024,1024]{0,1:T(8,128)(2,1)} %collective-permute-done.3, bf16[1024,1024]{0,1:T(8,128)(2,1)} %bitcast.43, pred[]{:T(512)S(6)} %eq.31), kind=kOutput, calls=%fused_computation.39 | convolution fusion | flops 555876352 | bytes 4980737 | tf_op jit(solution)/shard_map/dot_general | solution.py:188
  264.2 8.3 %collective-permute-start.4 = (bf16[128,1024]{1,0:T(8,128)(2,1)S(1)}, bf16[128,1024]{1,0:T(8,128)(2,1)S(1)}, u32[]{:S(2)}, u32[]{:S(2)}) collective-permute-start(bf16[128,1024]{1,0:T(8,128)(2,1)S(1)} %fusion.24), channel_id=1, source_target_pairs={{28,32},{32,28},{60,64},{64,60},{92,96},{96,92},{124,128},{128,124... | collective-permute-start | bytes 786440 | tf_op jit(solution)/shard_map/ppermute | solution.py:200
  272.7 9.5 %collective-permute-done.4 = bf16[128,1024]{1,0:T(8,128)(2,1)S(1)} collective-permute-done((bf16[128,1024]{1,0:T(8,128)(2,1)S(1)}, bf16[128,1024]{1,0:T(8,128)(2,1)S(1)}, u32[]{:S(2)}, u32[]{:S(2)}) %collective-permute-start.4) | collective-permute-done | bytes 262176 | tf_op jit(solution)/shard_map/ppermute | solution.py:200
  282.2 0.9 fusion.39
  (91 shorter events, 5.2 us)
Async XLA Ops:
  6.5 114.6 %copy-start = (bf16[2048,32]{0,1:T(8,128)(2,1)S(1)}, bf16[2048,32]{0,1:T(8,128)(2,1)}, u32[]{:S(2)}) copy-start(bf16[2048,32]{0,1:T(8,128)(2,1)} %param.18) | copy-start | bytes 393220
  8.5 0.9 copy-start.6
  15.6 34.0 %all-to-all-start = ((f32[4,16,72,128]{3,2,1,0:T(8,128)}), f32[4,16,72,128]{3,2,1,0:T(8,128)}, u32[]{:S(2)}, u32[]{:S(2)}) async-start(f32[4,16,72,128]{3,2,1,0:T(8,128)} %bitcast.21), calls=%async_computation | async-start | bytes 4718592 | tf_op jit(solution)/shard_map/all_to_all | solution.py:64
  20.2 222.9 %all-gather.4.cloned.1.call-start = ((), (), s32[]{:S(2)}) async-start(), calls=%async_computation.2 | async-start | bytes 2621440 | tf_op jit(solution)/shard_map/all_gather | solution.py:101
  53.1 6.3 %copy-start.14 = (f32[16]{0:T(128)}, f32[16]{0:T(128)S(1)}, u32[]{:S(2)}) copy-start(f32[16]{0:T(128)S(1)} %get-tuple-element.66) | copy-start | bytes 196
  53.1 6.3 %copy-start.19 = (f32[16]{0:T(128)}, f32[16]{0:T(128)S(1)}, u32[]{:S(2)}) copy-start(f32[16]{0:T(128)S(1)} %get-tuple-element.68) | copy-start | bytes 196
  53.1 18.3 %copy-start.13 = (f32[16]{0:T(128)}, f32[16]{0:T(128)S(1)}, u32[]{:S(2)}) copy-start(f32[16]{0:T(128)S(1)} %get-tuple-element.64) | copy-start | bytes 196
  53.1 18.3 %copy-start.20 = (f32[16]{0:T(128)}, f32[16]{0:T(128)S(1)}, u32[]{:S(2)}) copy-start(f32[16]{0:T(128)S(1)} %broadcast_multiply_fusion.1) | copy-start | bytes 196
  54.2 0.8 copy-start.1
  55.0 15.5 %collective-permute-start = (f32[16,72,128]{2,1,0:T(8,128)S(1)}, f32[16,72,128]{2,1,0:T(8,128)S(1)}, u32[]{:S(2)}, u32[]{:S(2)}) collective-permute-start(f32[16,72,128]{2,1,0:T(8,128)S(1)} %pad_maximum_fusion.2), channel_id=1, source_target_pairs={{0,4},{1,5},{4,8},{5,9},{6,2},{7,3},{8,12},{9,13},{10,6},{11,7},{1... | collective-permute-start | bytes 1769480 | tf_op jit(solution)/shard_map/ppermute | solution.py:84
  70.5 0.8 copy-start.3
  71.4 0.6 copy-start.16
  73.5 16.6 %collective-permute-start.1 = (f32[16,72,128]{2,1,0:T(8,128)S(1)}, f32[16,72,128]{2,1,0:T(8,128)S(1)}, u32[]{:S(2)}, u32[]{:S(2)}) collective-permute-start(f32[16,72,128]{2,1,0:T(8,128)S(1)} %pad_maximum_fusion.3), channel_id=1, source_target_pairs={{0,8},{1,9},{4,12},{5,13},{8,16},{9,17},{10,2},{11,3},{12,20},{13,... | collective-permute-start | bytes 1769480 | tf_op jit(solution)/shard_map/ppermute | solution.py:84
  90.1 0.8 copy-start.4
  96.2 108.0 %collective-permute-start.2 = (f32[16,72,128]{2,1,0:T(8,128)}, f32[16,72,128]{2,1,0:T(8,128)}, u32[]{:S(2)}, u32[]{:S(2)}) collective-permute-start(f32[16,72,128]{2,1,0:T(8,128)} %pad_maximum_fusion.4), channel_id=1, source_target_pairs={{0,16},{1,17},{4,20},{5,21},{8,24},{9,25},{12,28},{13,29},{18,2},{... | collective-permute-start | bytes 1769480 | tf_op jit(solution)/shard_map/ppermute | solution.py:84
  200.2 5.6 %copy-start.2 = (f32[16,64,128]{2,1,0:T(8,128)S(1)}, f32[16,64,128]{2,1,0:T(8,128)}, u32[]{:S(2)}) copy-start(f32[16,64,128]{2,1,0:T(8,128)} %get-tuple-element.85) | copy-start | bytes 1572868
  202.6 3.2 %copy-start.15 = (f32[16]{0:T(128)S(1)}, f32[16]{0:T(128)}, u32[]{:S(2)}) copy-start(f32[16]{0:T(128)} %copy-done.14) | copy-start | bytes 196
  202.6 3.2 %copy-start.17 = (f32[16]{0:T(128)S(1)}, f32[16]{0:T(128)}, u32[]{:S(2)}) copy-start(f32[16]{0:T(128)} %get-tuple-element.63) | copy-start | bytes 196
  202.6 3.2 %copy-start.18 = (f32[16]{0:T(128)S(1)}, f32[16]{0:T(128)}, u32[]{:S(2)}) copy-start(f32[16]{0:T(128)} %get-tuple-element.69) | copy-start | bytes 196
  207.8 3.8 %copy-start.10 = (f32[128,128]{1,0:T(8,128)S(1)}, f32[128,128]{1,0:T(8,128)}, u32[]{:S(2)}) copy-start(f32[128,128]{1,0:T(8,128)} %fusion.42) | copy-start | bytes 196612
  207.8 47.5 %all-to-all-start.1 = ((f32[4,16,64,128]{3,2,1,0:T(8,128)}), f32[4,16,64,128]{3,2,1,0:T(8,128)S(1)}, u32[]{:S(2)}, u32[]{:S(2)}) async-start(f32[4,16,64,128]{3,2,1,0:T(8,128)} %reverse_select_fusion.1), calls=%async_computation.1 | async-start | bytes 4194304 | tf_op jit(solution)/shard_map/all_to_all | solution.py:91
  211.5 13.6 %copy-start.21 = (s32[16]{0:T(128)S(1)}, s32[16]{0:T(128)}, u32[]{:S(2)}) copy-start(s32[16]{0:T(128)} %param.19) | copy-start | bytes 196
  247.6 6.3 %copy-start.8 = (f32[128,32]{1,0:T(8,128)S(1)}, f32[128,32]{1,0:T(8,128)}, u32[]{:S(2)}) copy-start(f32[128,32]{1,0:T(8,128)} %get-tuple-element.92) | copy-start | bytes 49156
  247.6 6.4 %copy-start.7 = (bf16[1,128,2048]{2,1,0:T(8,128)(2,1)S(1)}, bf16[1,128,2048]{2,1,0:T(8,128)(2,1)}, u32[]{:S(2)}) copy-start(bf16[1,128,2048]{2,1,0:T(8,128)(2,1)} %param.12) | copy-start | bytes 1572868
  251.3 7.9 %collective-permute-start.3 = (bf16[1024,1024]{0,1:T(8,128)(2,1)}, bf16[1024,1024]{0,1:T(8,128)(2,1)}, u32[]{:S(2)}, u32[]{:S(2)}) collective-permute-start(bf16[1024,1024]{0,1:T(8,128)(2,1)} %bitcast.43), channel_id=1, source_target_pairs={{0,32},{32,0},{64,96},{96,64},{128,160},{160,128},{192,224},{224,1... | collective-permute-start | bytes 6291464 | tf_op jit(solution)/shard_map/ppermute | solution.py:105
  255.2 0.8 copy-start.9
  255.5 2.3 copy-start.5
  255.5 2.3 copy-start.11
  257.8 1.0 copy-start.12
  264.2 17.9 %collective-permute-start.4 = (bf16[128,1024]{1,0:T(8,128)(2,1)S(1)}, bf16[128,1024]{1,0:T(8,128)(2,1)S(1)}, u32[]{:S(2)}, u32[]{:S(2)}) collective-permute-start(bf16[128,1024]{1,0:T(8,128)(2,1)S(1)} %fusion.24), channel_id=1, source_target_pairs={{28,32},{32,28},{60,64},{64,60},{92,96},{96,92},{124,128},{128,124... | collective-permute-start | bytes 786440 | tf_op jit(solution)/shard_map/ppermute | solution.py:200
Sparse Core Ops, SparseCore 0:
  201.2 41.7 all-gather.3

commit v6 on v5

--- a/solution.py
+++ b/solution.py
@@ -96,9 +96,9 @@
 def gather_weight(output_weight):
     half = lax.axis_index("win") % 2
     half_rows = output_weight.shape[0] // 2
-    mine = lax.dynamic_slice_in_dim(output_weight, half * half_rows, half_rows, axis=0)
-    column = lax.all_gather(mine, "z", axis=0)
-    row = lax.all_gather(column, "x", axis=1)
+    column = lax.all_gather(output_weight, "z", axis=0)
+    mine = lax.dynamic_slice_in_dim(column, half * half_rows, half_rows, axis=1)
+    row = lax.all_gather(mine, "x", axis=1)
     gathered = row.transpose(2, 0, 1, 3).reshape(half_rows, -1)
     wins = lax.axis_size("win")
     pairs = [(w, w ^ 1) for w in range(wins)]

time: 296 us -> 252 us (0.85); the launches traced: 290 us -> 250 us
  blocking collectives: 79.1 us -> 0 us
  starting transfers between devices: 53.2 us -> 98.7 us
  waiting for transfers between devices: 78.2 us -> 71.2 us
    all_gather x1 -> x0, blocking collectives: 79.1 us -> none  [gather_weight(): column = lax.all_gather(mine, 'z', axis=0)]
    all_to_all x1, starting transfers between devices: 3.74 us -> 47.8 us  [scan_states(): back = lax.all_to_all(out, 'x', 0, 0, tiled=True)]
    all_gather x1 -> x2, waiting for transfers between devices: 17.4 us -> 0.01 us  [the longest x1 0.01 us: gather_weight(): row = lax.all_gather(mine, 'x', axis=1)]
    ppermute x3, waiting for transfers between devices: 21.9 us -> 32.7 us  [scan_states(): got = split_packed(lax.ppermute(pack(*total), ('z', 'x'), pairs))]
    unnamed x47 -> x55, local copies, waits for them, and re-layouts: 6.2 us -> 8.51 us
  transfers between devices with their start and end apart: 8 -> 9, of which waited for: 5 -> 6; matrix products, arithmetic and copies ran while one was open for 12% -> 17% of each run, Pallas kernels for 0% -> 0%
where the time goes in v6:
time: 252 us; the launch traced here: 250 us
  starting transfers between devices  98.7 us (39%)
  waiting for transfers between devices  71.2 us (28%)
  local copies, waits for them, and re-layouts  26.5 us (11%)
  other arithmetic  22.1 us (9%)
  matrix products  17.5 us (7%)
  between operations  13.9 us (6%)
    all_to_all x1, starting transfers between devices, scan_states(): back = lax.all_to_all(out, 'x', 0, 0, tiled=True)  47.8 us
    ppermute x3, starting transfers between devices, scan_states(): got = split_packed(lax.ppermute(pack(*total), ('z', 'x'), pairs))  34.1 us
    ppermute x3, waiting for transfers between devices, scan_states(): got = split_packed(lax.ppermute(pack(*total), ('z', 'x'), pairs))  32.7 us
    all_to_all x1, waiting for transfers between devices, scan_states(): mine = lax.all_to_all(packed, 'x', 0, 0, tiled=True)  29.4 us
    ppermute x1, starting transfers between devices, per_device(): partner = lax.ppermute(projected_rows, ('win', 'z'), pairs)  10.3 us
    unnamed x55, local copies, waits for them, and re-layouts  8.51 us
    dot_general x8, matrix products, group_mix(): jnp.einsum('hts,shp->thp', mixing, group_frames, preferred_element_type=j...  7.98 us
    ppermute x1, waiting for transfers between devices, per_device(): partner = lax.ppermute(projected_rows, ('win', 'z'), pairs)  7.59 us
  transfers between devices with their start and end apart: 9, of which 6 were waited for; matrix products, arithmetic and copies ran while one was open for 17% of the time, Pallas kernels for 0%

profile of v6, /device:TPU:24, one launch (start us, length us, event | category | flops | bytes accessed | tf_op | source)
XLA Modules:
  0.0 249.8 jit_solution(7624003176556669129)
XLA Ops:
  6.5 0.8 compare_select_fusion
  7.3 0.7 multiply_bitcast_fusion
  8.7 0.7 fusion.52
  9.5 1.3 copy.88
  10.8 0.8 bitcast_convert_fusion
  12.3 0.8 convolution_bitcast_fusion.4
  13.1 0.8 convolution_bitcast_fusion.3
  14.0 1.6 pad_maximum_fusion
  15.7 4.5 %all-to-all-start = ((f32[4,16,72,128]{3,2,1,0:T(8,128)}), f32[4,16,72,128]{3,2,1,0:T(8,128)}, u32[]{:S(2)}, u32[]{:S(2)}) async-start(f32[4,16,72,128]{3,2,1,0:T(8,128)} %bitcast.21), calls=%async_computation | async-start | bytes 4718592 | tf_op jit(solution)/shard_map/all_to_all | solution.py:64
  20.2 29.4 %all-to-all-done = f32[4,16,72,128]{3,2,1,0:T(8,128)} async-done(((f32[4,16,72,128]{3,2,1,0:T(8,128)}), f32[4,16,72,128]{3,2,1,0:T(8,128)}, u32[]{:S(2)}, u32[]{:S(2)}) %all-to-all-start) | async-done | bytes 2359328 | tf_op jit(solution)/shard_map/all_to_all | solution.py:64
  49.7 2.6 %reverse_select_fusion = f32[4,16,72,128]{3,2,1,0:T(8,128)S(1)} fusion(f32[4,16,72,128]{3,2,1,0:T(8,128)} %all-to-all-done, pred[]{:T(512)S(6)} %ge.19), kind=kLoop, calls=%fused_computation.24 | loop fusion | flops 589824 | bytes 4718593 | tf_op jit(solution)/shard_map/jit(_where)/select_n | solution.py:66
  52.3 0.9 exponential_reduce_fusion
  53.2 1.0 fusion.35
  54.3 0.7 copy-done.1
  55.0 0.9 pad_maximum_fusion.2
  55.9 3.8 %collective-permute-start = (f32[16,72,128]{2,1,0:T(8,128)}, f32[16,72,128]{2,1,0:T(8,128)S(1)}, u32[]{:S(2)}, u32[]{:S(2)}) collective-permute-start(f32[16,72,128]{2,1,0:T(8,128)} %pad_maximum_fusion.2), channel_id=1, source_target_pairs={{0,4},{1,5},{4,8},{5,9},{6,2},{7,3},{8,12},{9,13},{10,6},{11,7},{1... | collective-permute-start | bytes 1769480 | tf_op jit(solution)/shard_map/ppermute | solution.py:84
  59.8 11.9 %collective-permute-done = f32[16,72,128]{2,1,0:T(8,128)S(1)} collective-permute-done((f32[16,72,128]{2,1,0:T(8,128)}, f32[16,72,128]{2,1,0:T(8,128)S(1)}, u32[]{:S(2)}, u32[]{:S(2)}) %collective-permute-start) | collective-permute-done | bytes 589856 | tf_op jit(solution)/shard_map/ppermute | solution.py:84
  71.7 0.8 copy-done.3
  73.1 1.3 multiply_add_fusion.1
  74.5 0.7 fusion.48
  75.3 5.7 %collective-permute-start.1 = (f32[16,72,128]{2,1,0:T(8,128)S(1)}, f32[16,72,128]{2,1,0:T(8,128)S(1)}, u32[]{:S(2)}, u32[]{:S(2)}) collective-permute-start(f32[16,72,128]{2,1,0:T(8,128)S(1)} %pad_maximum_fusion.3), channel_id=1, source_target_pairs={{0,8},{1,9},{4,12},{5,13},{8,16},{9,17},{10,2},{11,3},{12,20},{13,... | collective-permute-start | bytes 1769480 | tf_op jit(solution)/shard_map/ppermute | solution.py:84
  81.0 17.9 %collective-permute-done.1 = f32[16,72,128]{2,1,0:T(8,128)S(1)} collective-permute-done((f32[16,72,128]{2,1,0:T(8,128)S(1)}, f32[16,72,128]{2,1,0:T(8,128)S(1)}, u32[]{:S(2)}, u32[]{:S(2)}) %collective-permute-start.1) | collective-permute-done | bytes 589856 | tf_op jit(solution)/shard_map/ppermute | solution.py:84
  98.8 0.8 copy-done.4
  100.3 1.2 copy.102
  101.5 1.2 exponential_bitcast_fusion.2
  102.7 1.2 multiply_add_fusion
  104.0 0.9 pad_maximum_fusion.4
  104.8 24.6 %collective-permute-start.2 = (f32[16,72,128]{2,1,0:T(8,128)}, f32[16,72,128]{2,1,0:T(8,128)}, u32[]{:S(2)}, u32[]{:S(2)}) collective-permute-start(f32[16,72,128]{2,1,0:T(8,128)} %pad_maximum_fusion.4), channel_id=1, source_target_pairs={{0,16},{1,17},{4,20},{5,21},{8,24},{9,25},{12,28},{13,29},{18,2},{... | collective-permute-start | bytes 1769480 | tf_op jit(solution)/shard_map/ppermute | solution.py:84
  129.4 0.7 copy.90
  130.3 1.8 copy.104
  132.2 1.1 copy.103
  133.3 3.0 %collective-permute-done.2 = f32[16,72,128]{2,1,0:T(8,128)} collective-permute-done((f32[16,72,128]{2,1,0:T(8,128)}, f32[16,72,128]{2,1,0:T(8,128)}, u32[]{:S(2)}, u32[]{:S(2)}) %collective-permute-start.2) | collective-permute-done | bytes 589856 | tf_op jit(solution)/shard_map/ppermute | solution.py:84
  136.3 1.6 add_bitcast_fusion.2
  138.4 1.5 reverse_select_fusion.1
  139.9 47.8 %all-to-all-start.1 = ((f32[4,16,64,128]{3,2,1,0:T(8,128)}), f32[4,16,64,128]{3,2,1,0:T(8,128)S(1)}, u32[]{:S(2)}, u32[]{:S(2)}) async-start(f32[4,16,64,128]{3,2,1,0:T(8,128)} %reverse_select_fusion.1), calls=%async_computation.1 | async-start | bytes 4194304 | tf_op jit(solution)/shard_map/all_to_all | solution.py:91
  187.7 13.6 %while.11 = (s32[]{:T(128)}, f32[8,128,4,64]{1,3,2,0:T(8,128)}, bf16[8,128,4,64]{1,3,2,0:T(8,128)(2,1)S(1)}, f32[128,128]{1,0:T(8,128)S(1)}, f32[8,4,128]{2,1,0:T(4,128)}, /*index=5*/f32[8,4,128]{2,1,0:T(4,128)S(1)}, s32[]{:T(128)}) while((s32[]{:T(128)}, f32[8,128,4,64]{1,3,2,0:T(8,128)}, bf16[8,128,4,64]{1,3,2,0:T(8,128)(2,1)S(1)}, ...), condition=%wide.region_4.5_spmd.clone, body=%wide.region_3.4_spmd.clone.sunk | while | flops 8732674 | bytes 312401 | solution.py:171
  187.7 0.7 dynamic-slice_bitcast_fusion.3
  188.4 1.0 fusion.62
  189.4 0.7 dynamic-slice_bitcast_fusion.3
  190.1 1.0 fusion.62
  191.1 0.7 dynamic-slice_bitcast_fusion.3
  191.8 1.0 fusion.62
  192.8 0.7 dynamic-slice_bitcast_fusion.3
  193.5 1.0 fusion.62
  194.5 0.7 dynamic-slice_bitcast_fusion.3
  195.2 1.0 fusion.62
  196.2 0.7 dynamic-slice_bitcast_fusion.3
  196.9 1.0 fusion.62
  197.9 0.7 dynamic-slice_bitcast_fusion.3
  198.6 1.0 fusion.62
  199.6 0.7 dynamic-slice_bitcast_fusion.3
  200.3 1.0 fusion.62
  201.9 4.5 %reshape.287 = bf16[8,4,1024,32]{2,1,3,0:T(4,128)(2,1)} reshape(bf16[8,4096,32]{1,2,0:T(8,128)(2,1)} %all-gather.7.cloned.1.call-done) | data formatting | bytes 4194304 | tf_op jit(solution)/shard_map/all_gather | solution.py:101
  206.4 3.7 %copy.100 = bf16[1024,8,4,32]{0,3,2,1:T(8,128)(2,1)} copy(bf16[1024,8,4,32]{0,2,3,1:T(4,128)(2,1)} %bitcast.152) | data formatting | bytes 4194304 | tf_op jit(solution)/shard_map/transpose | solution.py:102
  210.1 1.9 collective-permute-start.3
  212.0 0.7 iota_compare_fusion.1
  212.8 1.3 copy.98
  214.1 1.4 all-to-all-done.1
  215.7 1.9 fusion.22
  217.7 0.8 multiply_reduce_fusion
  219.0 5.0 %fusion.24 = bf16[128,1024]{1,0:T(8,128)(2,1)S(1)} fusion(bf16[128,2048]{0,1:T(8,128)(2,1)S(1)} %fusion.25, bf16[1024,1024]{0,1:T(8,128)(2,1)} %collective-permute-done.3, bf16[1024,1024]{0,1:T(8,128)(2,1)} %bitcast.43, pred[]{:T(512)S(6)} %eq.31), kind=kOutput, calls=%fused_computation.39 | convolution fusion | flops 555876352 | bytes 4980737 | tf_op jit(solution)/shard_map/dot_general | solution.py:188
  224.0 10.3 %collective-permute-start.4 = (bf16[128,1024]{1,0:T(8,128)(2,1)S(1)}, bf16[128,1024]{1,0:T(8,128)(2,1)S(1)}, u32[]{:S(2)}, u32[]{:S(2)}) collective-permute-start(bf16[128,1024]{1,0:T(8,128)(2,1)S(1)} %fusion.24), channel_id=1, source_target_pairs={{28,32},{32,28},{60,64},{64,60},{92,96},{96,92},{124,128},{128,124... | collective-permute-start | bytes 786440 | tf_op jit(solution)/shard_map/ppermute | solution.py:200
  234.4 7.6 %collective-permute-done.4 = bf16[128,1024]{1,0:T(8,128)(2,1)S(1)} collective-permute-done((bf16[128,1024]{1,0:T(8,128)(2,1)S(1)}, bf16[128,1024]{1,0:T(8,128)(2,1)S(1)}, u32[]{:S(2)}, u32[]{:S(2)}) %collective-permute-start.4) | collective-permute-done | bytes 262176 | tf_op jit(solution)/shard_map/ppermute | solution.py:200
  242.0 0.9 fusion.39
  (100 shorter events, 5.6 us)
Async XLA Ops:
  6.5 123.6 %copy-start = (bf16[1,128,128]{2,1,0:T(8,128)(2,1)S(1)}, bf16[1,128,128]{2,1,0:T(8,128)(2,1)}, u32[]{:S(2)}) copy-start(bf16[1,128,128]{2,1,0:T(8,128)(2,1)} %param.14) | copy-start | bytes 98308
  8.5 0.9 copy-start.6
  15.7 34.0 %all-to-all-start = ((f32[4,16,72,128]{3,2,1,0:T(8,128)}), f32[4,16,72,128]{3,2,1,0:T(8,128)}, u32[]{:S(2)}, u32[]{:S(2)}) async-start(f32[4,16,72,128]{3,2,1,0:T(8,128)} %bitcast.21), calls=%async_computation | async-start | bytes 4718592 | tf_op jit(solution)/shard_map/all_to_all | solution.py:64
  20.2 110.1 %all-gather.5.cloned.1.call-start = ((), (), s32[]{:S(2)}) async-start(), calls=%async_computation.2 | async-start | bytes 1179648 | tf_op jit(solution)/shard_map/all_gather | solution.py:99
  53.2 6.7 %copy-start.13 = (f32[16]{0:T(128)}, f32[16]{0:T(128)S(1)}, u32[]{:S(2)}) copy-start(f32[16]{0:T(128)S(1)} %get-tuple-element.64) | copy-start | bytes 196
  53.2 6.7 %copy-start.14 = (f32[16]{0:T(128)}, f32[16]{0:T(128)S(1)}, u32[]{:S(2)}) copy-start(f32[16]{0:T(128)S(1)} %get-tuple-element.66) | copy-start | bytes 196
  53.2 20.0 %copy-start.18 = (f32[16]{0:T(128)}, f32[16]{0:T(128)S(1)}, u32[]{:S(2)}) copy-start(f32[16]{0:T(128)S(1)} %get-tuple-element.68) | copy-start | bytes 196
  53.2 20.0 %copy-start.22 = (f32[16]{0:T(128)}, f32[16]{0:T(128)S(1)}, u32[]{:S(2)}) copy-start(f32[16]{0:T(128)S(1)} %broadcast_multiply_fusion.1) | copy-start | bytes 196
  54.2 0.8 copy-start.1
  55.9 15.8 %collective-permute-start = (f32[16,72,128]{2,1,0:T(8,128)}, f32[16,72,128]{2,1,0:T(8,128)S(1)}, u32[]{:S(2)}, u32[]{:S(2)}) collective-permute-start(f32[16,72,128]{2,1,0:T(8,128)} %pad_maximum_fusion.2), channel_id=1, source_target_pairs={{0,4},{1,5},{4,8},{5,9},{6,2},{7,3},{8,12},{9,13},{10,6},{11,7},{1... | collective-permute-start | bytes 1769480 | tf_op jit(solution)/shard_map/ppermute | solution.py:84
  59.8 142.1 %all-gather.7.cloned.1.call-start = ((), (), s32[]{:S(2)}) async-start(), calls=%async_computation.3 | async-start | bytes 2621440 | tf_op jit(solution)/shard_map/all_gather | solution.py:101
  71.7 0.8 copy-start.3
  74.5 55.0 %copy-start.7 = (f32[128,32]{1,0:T(8,128)S(1)}, f32[128,32]{1,0:T(8,128)}, u32[]{:S(2)}) copy-start(f32[128,32]{1,0:T(8,128)} %copy-done.6) | copy-start | bytes 49156
  74.5 55.7 %copy-start.10 = (bf16[1,128,128]{2,1,0:T(8,128)(2,1)S(1)}, bf16[1,128,128]{2,1,0:T(8,128)(2,1)}, u32[]{:S(2)}) copy-start(bf16[1,128,128]{2,1,0:T(8,128)(2,1)} %param.13) | copy-start | bytes 98308
  75.3 23.5 %collective-permute-start.1 = (f32[16,72,128]{2,1,0:T(8,128)S(1)}, f32[16,72,128]{2,1,0:T(8,128)S(1)}, u32[]{:S(2)}, u32[]{:S(2)}) collective-permute-start(f32[16,72,128]{2,1,0:T(8,128)S(1)} %pad_maximum_fusion.3), channel_id=1, source_target_pairs={{0,8},{1,9},{4,12},{5,13},{8,16},{9,17},{10,2},{11,3},{12,20},{13,... | collective-permute-start | bytes 1769480 | tf_op jit(solution)/shard_map/ppermute | solution.py:84
  98.8 0.8 copy-start.4
  104.8 31.5 %collective-permute-start.2 = (f32[16,72,128]{2,1,0:T(8,128)}, f32[16,72,128]{2,1,0:T(8,128)}, u32[]{:S(2)}, u32[]{:S(2)}) collective-permute-start(f32[16,72,128]{2,1,0:T(8,128)} %pad_maximum_fusion.4), channel_id=1, source_target_pairs={{0,16},{1,17},{4,20},{5,21},{8,24},{9,25},{12,28},{13,29},{18,2},{... | collective-permute-start | bytes 1769480 | tf_op jit(solution)/shard_map/ppermute | solution.py:84
  130.3 6.1 %copy-start.19 = (f32[16]{0:T(128)S(1)}, f32[16]{0:T(128)}, u32[]{:S(2)}) copy-start(f32[16]{0:T(128)} %copy-done.18) | copy-start | bytes 196
  130.3 6.0 %copy-start.20 = (f32[16]{0:T(128)S(1)}, f32[16]{0:T(128)}, u32[]{:S(2)}) copy-start(f32[16]{0:T(128)} %get-tuple-element.100) | copy-start | bytes 196
  130.3 6.0 %copy-start.21 = (f32[16]{0:T(128)S(1)}, f32[16]{0:T(128)}, u32[]{:S(2)}) copy-start(f32[16]{0:T(128)} %get-tuple-element.105) | copy-start | bytes 196
  130.3 6.0 %copy-start.23 = (f32[16]{0:T(128)S(1)}, f32[16]{0:T(128)}, u32[]{:S(2)}) copy-start(f32[16]{0:T(128)} %copy-done.22) | copy-start | bytes 196
  132.2 5.7 %copy-start.2 = (f32[16,64,128]{2,1,0:T(8,128)S(1)}, f32[16,64,128]{2,1,0:T(8,128)}, u32[]{:S(2)}) copy-start(f32[16,64,128]{2,1,0:T(8,128)} %get-tuple-element.85) | copy-start | bytes 1572868
  132.2 5.7 %copy-start.15 = (f32[16]{0:T(128)S(1)}, f32[16]{0:T(128)}, u32[]{:S(2)}) copy-start(f32[16]{0:T(128)} %copy-done.14) | copy-start | bytes 196
  132.2 5.7 %copy-start.16 = (f32[16]{0:T(128)S(1)}, f32[16]{0:T(128)}, u32[]{:S(2)}) copy-start(f32[16]{0:T(128)} %get-tuple-element.63) | copy-start | bytes 196
  132.2 5.7 %copy-start.17 = (f32[16]{0:T(128)S(1)}, f32[16]{0:T(128)}, u32[]{:S(2)}) copy-start(f32[16]{0:T(128)} %get-tuple-element.69) | copy-start | bytes 196
  139.9 75.6 %all-to-all-start.1 = ((f32[4,16,64,128]{3,2,1,0:T(8,128)}), f32[4,16,64,128]{3,2,1,0:T(8,128)S(1)}, u32[]{:S(2)}, u32[]{:S(2)}) async-start(f32[4,16,64,128]{3,2,1,0:T(8,128)} %reverse_select_fusion.1), calls=%async_computation.1 | async-start | bytes 4194304 | tf_op jit(solution)/shard_map/all_to_all | solution.py:91
  187.7 13.6 %copy-start.24 = (s32[16]{0:T(128)S(1)}, s32[16]{0:T(128)}, u32[]{:S(2)}) copy-start(s32[16]{0:T(128)} %param.19) | copy-start | bytes 196
  206.4 6.3 %copy-start.9 = (f32[128,32]{1,0:T(8,128)S(1)}, f32[128,32]{1,0:T(8,128)}, u32[]{:S(2)}) copy-start(f32[128,32]{1,0:T(8,128)} %get-tuple-element.92) | copy-start | bytes 49156
  206.4 6.3 %copy-start.8 = (bf16[1,128,2048]{2,1,0:T(8,128)(2,1)S(1)}, bf16[1,128,2048]{2,1,0:T(8,128)(2,1)}, u32[]{:S(2)}) copy-start(bf16[1,128,2048]{2,1,0:T(8,128)(2,1)} %param.12) | copy-start | bytes 1572868
  210.1 8.9 %collective-permute-start.3 = (bf16[1024,1024]{0,1:T(8,128)(2,1)}, bf16[1024,1024]{0,1:T(8,128)(2,1)}, u32[]{:S(2)}, u32[]{:S(2)}) collective-permute-start(bf16[1024,1024]{0,1:T(8,128)(2,1)} %bitcast.43), channel_id=1, source_target_pairs={{0,32},{32,0},{64,96},{96,64},{128,160},{160,128},{192,224},{224,1... | collective-permute-start | bytes 6291464 | tf_op jit(solution)/shard_map/ppermute | solution.py:105
  215.7 1.9 copy-start.5
  215.7 1.9 copy-start.11
  217.7 1.0 copy-start.12
  224.0 18.0 %collective-permute-start.4 = (bf16[128,1024]{1,0:T(8,128)(2,1)S(1)}, bf16[128,1024]{1,0:T(8,128)(2,1)S(1)}, u32[]{:S(2)}, u32[]{:S(2)}) collective-permute-start(bf16[128,1024]{1,0:T(8,128)(2,1)S(1)} %fusion.24), channel_id=1, source_target_pairs={{28,32},{32,28},{60,64},{64,60},{92,96},{96,92},{124,128},{128,124... | collective-permute-start | bytes 786440 | tf_op jit(solution)/shard_map/ppermute | solution.py:200
Sparse Core Ops, SparseCore 0:
  59.9 68.2 all-gather.4
  133.5 60.7 all-gather.6

commit v7 on v6

--- a/solution.py
+++ b/solution.py
@@ -56,12 +56,13 @@
     return jnp.concatenate([states, rows], axis=-2)
 
 
-def scan_states(log_fwd, log_bwd, fresh_fwd, fresh_bwd):
+def scan_states(log_fwd, log_bwd, fresh_fwd, fresh_bwd, hold):
     packed = pack(jnp.stack([log_fwd, log_bwd]), jnp.stack([fresh_fwd, fresh_bwd]))
     parts = lax.axis_size("x")
     per_part = 2 * H // parts
     packed = packed.reshape(parts, per_part, P_SIZE + PAD_ROWS, N)
     mine = lax.all_to_all(packed, "x", 0, 0, tiled=True)
+    mine, hold = lax.optimization_barrier((mine, hold))
     is_bwd = lax.axis_index("x") >= parts // 2
     ordered = jnp.where(is_bwd, mine[::-1], mine)
     logs, states = split_packed(ordered)
@@ -90,7 +91,7 @@
     out = jnp.where(is_bwd, out[::-1], out)
     back = lax.all_to_all(out, "x", 0, 0, tiled=True)
     back = back.reshape(2, H, P_SIZE, N)
-    return back[0], back[1]
+    return back[0], back[1], hold
 
 
 def gather_weight(output_weight):
@@ -151,7 +152,6 @@
     fresh_bwd = jnp.einsum(
         "shp,shn->hpn", head_frames, weighted_bwd, preferred_element_type=jnp.float32
     )
-    state_fwd, state_bwd = scan_states(running_fwd[-1], running_bwd[0], fresh_fwd, fresh_bwd)
     scores = jnp.dot(c_rows, b_rows.T, preferred_element_type=jnp.float32)
     lower_mask = jnp.arange(frame_count)[:, None] >= jnp.arange(frame_count)[None, :]
 
@@ -170,6 +170,9 @@
     grouped_frames = head_frames.reshape(frame_count, group_count, 4, P_SIZE).transpose(1, 0, 2, 3)
     local_groups = lax.map(group_mix, (grouped_fwd, grouped_bwd, grouped_frames))
     local_part = local_groups.transpose(1, 0, 2, 3).reshape(frame_count, H, P_SIZE)
+    state_fwd, state_bwd, local_part = scan_states(
+        running_fwd[-1], running_bwd[0], fresh_fwd, fresh_bwd, local_part
+    )
     c_float = c_rows.astype(jnp.float32)
     carried_fwd = jnp.exp(running_fwd)[:, :, None] * jnp.einsum(
         "hpn,tn->thp", state_fwd, c_float, precision=lax.Precision.HIGHEST

time: 252 us -> 239 us (0.948); the launches traced: 250 us -> 234 us
  starting transfers between devices: 98.7 us -> 76.9 us
  waiting for transfers between devices: 71.2 us -> 89.9 us
  local copies, waits for them, and re-layouts: 26.5 us -> 19.4 us
  other arithmetic: 22.1 us -> 17.9 us
    all_to_all x1, waiting for transfers between devices: 1.38 us -> 13.7 us  [scan_states(): back = lax.all_to_all(out, 'x', 0, 0, tiled=True)]
    all_to_all x1, starting transfers between devices: 47.8 us -> 37.3 us  [scan_states(): back = lax.all_to_all(out, 'x', 0, 0, tiled=True)]
    all_to_all x1, waiting for transfers between devices: 29.4 us -> 19.9 us  [scan_states(): mine = lax.all_to_all(packed, 'x', 0, 0, tiled=True)]
    ppermute x1, starting transfers between devices: 10.3 us -> 1.92 us  [per_device(): partner = lax.ppermute(projected_rows, ('win', 'z'), pairs)]
    ppermute x1, waiting for transfers between devices: 7.59 us -> 14.2 us  [per_device(): partner = lax.ppermute(projected_rows, ('win', 'z'), pairs)]
    sub x8, local copies, waits for them, and re-layouts: 5.48 us -> 0.02 us  [group_mix(): group_bwd[:, :, None] - group_bwd[:, None, :]]
    all_gather x1, waiting for transfers between devices: 0.01 us -> 5.19 us  [gather_weight(): column = lax.all_gather(output_weight, 'z', axis=0)]
    ppermute x3, waiting for transfers between devices: 32.7 us -> 36.1 us  [scan_states(): got = split_packed(lax.ppermute(pack(*total), ('z', 'x'), pairs))]
  transfers between devices with their start and end apart: 9 -> 9, of which waited for: 6 -> 7; matrix products, arithmetic and copies ran while one was open for 17% -> 15% of each run, Pallas kernels for 0% -> 0%
where the time goes in v7:
time: 239 us; the launch traced here: 234 us
  waiting for transfers between devices  89.9 us (38%)
  starting transfers between devices  76.9 us (32%)
  local copies, waits for them, and re-layouts  19.4 us (8%)
  other arithmetic  17.9 us (7%)
  matrix products  16.3 us (7%)
  between operations  13.8 us (6%)
    all_to_all x1, starting transfers between devices, scan_states(): back = lax.all_to_all(out, 'x', 0, 0, tiled=True)  37.3 us
    ppermute x3, waiting for transfers between devices, scan_states(): got = split_packed(lax.ppermute(pack(*total), ('z', 'x'), pairs))  36.1 us
    ppermute x3, starting transfers between devices, scan_states(): got = split_packed(lax.ppermute(pack(*total), ('z', 'x'), pairs))  31.3 us
    all_to_all x1, waiting for transfers between devices, scan_states(): mine = lax.all_to_all(packed, 'x', 0, 0, tiled=True)  19.9 us
    ppermute x1, waiting for transfers between devices, per_device(): partner = lax.ppermute(projected_rows, ('win', 'z'), pairs)  14.2 us
    all_to_all x1, waiting for transfers between devices, scan_states(): back = lax.all_to_all(out, 'x', 0, 0, tiled=True)  13.7 us
    dot_general x8, matrix products, group_mix(): jnp.einsum('hts,shp->thp', mixing, group_frames, preferred_element_type=j...  8.02 us
    unnamed x33, local copies, waits for them, and re-layouts  7.28 us
  transfers between devices with their start and end apart: 9, of which 7 were waited for; matrix products, arithmetic and copies ran while one was open for 15% of the time, Pallas kernels for 0%

profile of v7, /device:TPU:24, one launch (start us, length us, event | category | flops | bytes accessed | tf_op | source)
XLA Modules:
  0.0 234.2 jit_solution(1750789310867851117)
XLA Ops:
  6.5 0.8 compare_select_fusion
  7.3 0.7 multiply_bitcast_fusion
  8.3 0.2 reduce_window_sum.17
  8.5 0.2 reduce_window_sum.18
  8.7 0.7 fusion.52
  9.5 1.3 copy.90
  10.8 0.8 bitcast_convert_fusion
  11.7 0.8 convolution_bitcast_fusion.4
  12.5 0.8 convolution_bitcast_fusion.3
  13.4 0.1 broadcast_in_dim.46
  13.5 1.6 pad_maximum_fusion
  15.1 4.4 %all-to-all-start = ((f32[4,16,72,128]{3,2,1,0:T(8,128)}), f32[4,16,72,128]{3,2,1,0:T(8,128)S(1)}, u32[]{:S(2)}, u32[]{:S(2)}) async-start(f32[4,16,72,128]{3,2,1,0:T(8,128)} %bitcast.152), calls=%async_computation | async-start | bytes 4718592 | tf_op jit(solution)/shard_map/all_to_all | solution.py:64
  19.6 0.7 all-gather.5.cloned.1.call-update
  20.4 0.1 fusion.42
  20.5 8.2 %while.11 = (s32[]{:T(128)}, f32[8,128,4,64]{1,3,2,0:T(8,128)}, bf16[8,128,4,64]{1,3,2,0:T(8,128)(2,1)S(1)}, f32[128,128]{1,0:T(8,128)S(1)}, f32[8,4,128]{2,1,0:...) while((s32[]{:T(128)}, f32[8,128,4,64]{1,3,2,0:T(8,128)}, ...), condition=%wide.region_4.5_spmd.clone, body=%wide.region_3.4_spmd.clone.sunk | while | flops 8732674 | bytes 312401 | solution.py:171
  20.6 1.0 fusion.62
  21.6 1.0 fusion.62
  22.6 1.0 fusion.62
  23.7 1.0 fusion.62
  24.7 1.0 fusion.62
  25.7 1.0 fusion.62
  26.7 1.0 fusion.62
  27.8 1.0 fusion.62
  28.8 19.9 %all-to-all-done = f32[4,16,72,128]{3,2,1,0:T(8,128)S(1)} async-done(((f32[4,16,72,128]{3,2,1,0:T(8,128)}), f32[4,16,72,128]{3,2,1,0:T(8,128)S(1)}, u32[]{:S(2)}, u32[]{:S(2)}) %all-to-all-start) | async-done | bytes 2359328 | tf_op jit(solution)/shard_map/all_to_all | solution.py:64
  48.7 1.4 copy-done.1
  50.1 2.6 %reverse_select_fusion = f32[4,16,72,128]{3,2,1,0:T(8,128)S(1)} fusion(f32[4,16,72,128]{3,2,1,0:T(8,128)} %copy-done.1, pred[]{:T(512)S(6)} %ge.19), kind=kLoop, calls=%fused_computation.24 | loop fusion | flops 589824 | bytes 4718593 | tf_op jit(solution)/shard_map/jit(_where)/select_n | solution.py:67
  52.7 0.3 exponential_reduce_fusion
  53.1 1.0 fusion.35
  54.2 3.9 %collective-permute-start = (f32[16,72,128]{2,1,0:T(8,128)S(1)}, f32[16,72,128]{2,1,0:T(8,128)S(1)}, u32[]{:S(2)}, u32[]{:S(2)}) collective-permute-start(f32[16,72,128]{2,1,0:T(8,128)S(1)} %pad_maximum_fusion.2), channel_id=1, source_target_pairs={{0,4},{1,5},{4,8},{5,9},{6,2},{7,3},{8,12},{9,13},{10,6},{11,7},{1... | collective-permute-start | bytes 1769480 | tf_op jit(solution)/shard_map/ppermute | solution.py:85
  58.1 22.1 %collective-permute-done = f32[16,72,128]{2,1,0:T(8,128)S(1)} collective-permute-done((f32[16,72,128]{2,1,0:T(8,128)S(1)}, f32[16,72,128]{2,1,0:T(8,128)S(1)}, u32[]{:S(2)}, u32[]{:S(2)}) %collective-permute-start) | collective-permute-done | bytes 589856 | tf_op jit(solution)/shard_map/ppermute | solution.py:85
  80.2 0.8 copy-done.3
  81.1 1.2 multiply_add_fusion.1
  82.4 0.9 pad_maximum_fusion.3
  83.2 6.8 %collective-permute-start.1 = (f32[16,72,128]{2,1,0:T(8,128)}, f32[16,72,128]{2,1,0:T(8,128)}, u32[]{:S(2)}, u32[]{:S(2)}) collective-permute-start(f32[16,72,128]{2,1,0:T(8,128)} %pad_maximum_fusion.3), channel_id=1, source_target_pairs={{0,8},{1,9},{4,12},{5,13},{8,16},{9,17},{10,2},{11,3},{12,20},{13,... | collective-permute-start | bytes 1769480 | tf_op jit(solution)/shard_map/ppermute | solution.py:85
  90.1 5.2 %all-gather.5.cloned.1.call-done = bf16[16384,32]{0,1:T(8,128)(2,1)} async-done(((bf16[2048,32]{0,1:T(8,128)(2,1)}), bf16[16384,32]{0,1:T(8,128)(2,1)}) %all-gather.5.cloned.1.call-update) | async-done | bytes 1048592 | tf_op jit(solution)/shard_map/all_gather | solution.py:100
  95.3 1.8 copy.104
  97.1 1.1 copy.103
  98.2 3.4 %collective-permute-done.1 = f32[16,72,128]{2,1,0:T(8,128)} collective-permute-done((f32[16,72,128]{2,1,0:T(8,128)}, f32[16,72,128]{2,1,0:T(8,128)}, u32[]{:S(2)}, u32[]{:S(2)}) %collective-permute-start.1) | collective-permute-done | bytes 589856 | tf_op jit(solution)/shard_map/ppermute | solution.py:85
  101.6 0.8 slice.107
  102.6 1.2 multiply_add_fusion
  103.9 20.6 %collective-permute-start.2 = (f32[16,72,128]{2,1,0:T(8,128)S(1)}, f32[16,72,128]{2,1,0:T(8,128)S(1)}, u32[]{:S(2)}, u32[]{:S(2)}) collective-permute-start(f32[16,72,128]{2,1,0:T(8,128)S(1)} %pad_maximum_fusion.4), channel_id=1, source_target_pairs={{0,16},{1,17},{4,20},{5,21},{8,24},{9,25},{12,28},{13,29},{18,2},{... | collective-permute-start | bytes 1769480 | tf_op jit(solution)/shard_map/ppermute | solution.py:85
  124.5 10.7 %collective-permute-done.2 = f32[16,72,128]{2,1,0:T(8,128)S(1)} collective-permute-done((f32[16,72,128]{2,1,0:T(8,128)S(1)}, f32[16,72,128]{2,1,0:T(8,128)S(1)}, u32[]{:S(2)}, u32[]{:S(2)}) %collective-permute-start.2) | collective-permute-done | bytes 589856 | tf_op jit(solution)/shard_map/ppermute | solution.py:85
  135.1 1.3 add_bitcast_fusion.2
  136.4 0.2 add_bitcast_fusion.1
  136.6 0.2 pad_maximum_fusion.1
  136.9 1.5 reverse_select_fusion.1
  138.4 37.3 %all-to-all-start.1 = ((f32[4,16,64,128]{3,2,1,0:T(8,128)}), f32[4,16,64,128]{3,2,1,0:T(8,128)S(1)}, u32[]{:S(2)}, u32[]{:S(2)}) async-start(f32[4,16,64,128]{3,2,1,0:T(8,128)} %reverse_select_fusion.1), calls=%async_computation.1 | async-start | bytes 4194304 | tf_op jit(solution)/shard_map/all_to_all | solution.py:92
  175.7 0.6 dynamic_slice.17
  176.4 4.5 %reshape.287 = bf16[8,4,1024,32]{2,1,3,0:T(4,128)(2,1)} reshape(bf16[8,4096,32]{1,2,0:T(8,128)(2,1)} %all-gather.7.cloned.1.call-done) | data formatting | bytes 4194304 | tf_op jit(solution)/shard_map/all_gather | solution.py:102
  180.9 3.7 %copy.100 = bf16[1024,8,4,32]{0,3,2,1:T(8,128)(2,1)} copy(bf16[1024,8,4,32]{0,2,3,1:T(4,128)(2,1)} %bitcast.153) | data formatting | bytes 4194304 | tf_op jit(solution)/shard_map/transpose | solution.py:103
  184.6 1.9 collective-permute-start.3
  186.5 0.7 iota_compare_fusion.1
  187.2 1.2 copy.98
  188.5 13.7 %all-to-all-done.1 = f32[4,16,64,128]{3,2,1,0:T(8,128)S(1)} async-done(((f32[4,16,64,128]{3,2,1,0:T(8,128)}), f32[4,16,64,128]{3,2,1,0:T(8,128)S(1)}, u32[]{:S(2)}, u32[]{:S(2)}) %all-to-all-start.1) | async-done | bytes 2097184 | tf_op jit(solution)/shard_map/all_to_all | solution.py:92
  202.2 0.2 fusion.51
  202.5 0.6 fusion.22
  203.1 0.6 copy-done.6
  203.7 0.8 multiply_reduce_fusion
  204.6 0.1 broadcast_multiply_fusion
  204.7 0.3 fusion.25
  205.1 5.0 %fusion.24 = bf16[128,1024]{1,0:T(8,128)(2,1)S(1)} fusion(bf16[128,2048]{0,1:T(8,128)(2,1)S(1)} %fusion.25, bf16[1024,1024]{0,1:T(8,128)(2,1)} %collective-permute-done.3, bf16[1024,1024]{0,1:T(8,128)(2,1)} %bitcast.43, pred[]{:T(512)S(6)} %eq.31), kind=kOutput, calls=%fused_computation.39 | convolution fusion | flops 555876352 | bytes 4980737 | tf_op jit(solution)/shard_map/dot_general | solution.py:191
  210.1 1.9 collective-permute-start.4
  212.1 14.2 %collective-permute-done.4 = bf16[128,1024]{1,0:T(8,128)(2,1)S(1)} collective-permute-done((bf16[128,1024]{1,0:T(8,128)(2,1)S(1)}, bf16[128,1024]{1,0:T(8,128)(2,1)S(1)}, u32[]{:S(2)}, u32[]{:S(2)}) %collective-permute-start.4) | collective-permute-done | bytes 262176 | tf_op jit(solution)/shard_map/ppermute | solution.py:203
  226.4 0.9 fusion.39
  (78 shorter events, 1.7 us)
Async XLA Ops:
  6.5 13.9 %copy-start = (bf16[1,128,128]{2,1,0:T(8,128)(2,1)S(1)}, bf16[1,128,128]{2,1,0:T(8,128)(2,1)}, u32[]{:S(2)}) copy-start(bf16[1,128,128]{2,1,0:T(8,128)(2,1)} %param.14) | copy-start | bytes 98308
  15.1 5.3 %copy-start.9 = (bf16[1,128,128]{2,1,0:T(8,128)(2,1)S(1)}, bf16[1,128,128]{2,1,0:T(8,128)(2,1)}, u32[]{:S(2)}) copy-start(bf16[1,128,128]{2,1,0:T(8,128)(2,1)} %param.13) | copy-start | bytes 98308
  15.1 33.6 %all-to-all-start = ((f32[4,16,72,128]{3,2,1,0:T(8,128)}), f32[4,16,72,128]{3,2,1,0:T(8,128)S(1)}, u32[]{:S(2)}, u32[]{:S(2)}) async-start(f32[4,16,72,128]{3,2,1,0:T(8,128)} %bitcast.152), calls=%async_computation | async-start | bytes 4718592 | tf_op jit(solution)/shard_map/all_to_all | solution.py:64
  19.6 75.7 %all-gather.5.cloned.1.call-start = ((), (), s32[]{:S(2)}) async-start(), calls=%async_computation.2 | async-start | bytes 1179648 | tf_op jit(solution)/shard_map/all_gather | solution.py:100
  20.3 156.1 %all-gather.7.cloned.1.call-start = ((), (), s32[]{:S(2)}) async-start(), calls=%async_computation.3 | async-start | bytes 2621440 | tf_op jit(solution)/shard_map/all_gather | solution.py:102
  48.7 1.4 copy-start.1
  53.0 27.1 %copy-start.11 = (f32[16]{0:T(128)}, f32[16]{0:T(128)S(1)}, u32[]{:S(2)}) copy-start(f32[16]{0:T(128)S(1)} %get-tuple-element.72) | copy-start | bytes 196
  53.1 29.2 %copy-start.12 = (f32[16]{0:T(128)}, f32[16]{0:T(128)S(1)}, u32[]{:S(2)}) copy-start(f32[16]{0:T(128)S(1)} %broadcast_multiply_fusion.1) | copy-start | bytes 196
  54.2 25.9 %collective-permute-start = (f32[16,72,128]{2,1,0:T(8,128)S(1)}, f32[16,72,128]{2,1,0:T(8,128)S(1)}, u32[]{:S(2)}, u32[]{:S(2)}) collective-permute-start(f32[16,72,128]{2,1,0:T(8,128)S(1)} %pad_maximum_fusion.2), channel_id=1, source_target_pairs={{0,4},{1,5},{4,8},{5,9},{6,2},{7,3},{8,12},{9,13},{10,6},{11,7},{1... | collective-permute-start | bytes 1769480 | tf_op jit(solution)/shard_map/ppermute | solution.py:85
  80.2 0.8 copy-start.3
  83.2 18.4 %collective-permute-start.1 = (f32[16,72,128]{2,1,0:T(8,128)}, f32[16,72,128]{2,1,0:T(8,128)}, u32[]{:S(2)}, u32[]{:S(2)}) collective-permute-start(f32[16,72,128]{2,1,0:T(8,128)} %pad_maximum_fusion.3), channel_id=1, source_target_pairs={{0,8},{1,9},{4,12},{5,13},{8,16},{9,17},{10,2},{11,3},{12,20},{13,... | collective-permute-start | bytes 1769480 | tf_op jit(solution)/shard_map/ppermute | solution.py:85
  97.1 38.0 %copy-start.4 = (f32[16,72,128]{2,1,0:T(8,128)S(1)}, f32[16,72,128]{2,1,0:T(8,128)}, u32[]{:S(2)}) copy-start(f32[16,72,128]{2,1,0:T(8,128)} %copy-done.3) | copy-start | bytes 1769476
  103.7 32.7 %copy-start.2 = (f32[16,64,128]{2,1,0:T(8,128)S(1)}, f32[16,64,128]{2,1,0:T(8,128)}, u32[]{:S(2)}) copy-start(f32[16,64,128]{2,1,0:T(8,128)} %get-tuple-element.89) | copy-start | bytes 1572868
  103.9 31.3 %collective-permute-start.2 = (f32[16,72,128]{2,1,0:T(8,128)S(1)}, f32[16,72,128]{2,1,0:T(8,128)S(1)}, u32[]{:S(2)}, u32[]{:S(2)}) collective-permute-start(f32[16,72,128]{2,1,0:T(8,128)S(1)} %pad_maximum_fusion.4), channel_id=1, source_target_pairs={{0,16},{1,17},{4,20},{5,21},{8,24},{9,25},{12,28},{13,29},{18,2},{... | collective-permute-start | bytes 1769480 | tf_op jit(solution)/shard_map/ppermute | solution.py:85
  138.4 37.3 %copy-start.13 = (s32[16]{0:T(128)S(1)}, s32[16]{0:T(128)}, u32[]{:S(2)}) copy-start(s32[16]{0:T(128)} %param.19) | copy-start | bytes 196
  138.4 63.9 %all-to-all-start.1 = ((f32[4,16,64,128]{3,2,1,0:T(8,128)}), f32[4,16,64,128]{3,2,1,0:T(8,128)S(1)}, u32[]{:S(2)}, u32[]{:S(2)}) async-start(f32[4,16,64,128]{3,2,1,0:T(8,128)} %reverse_select_fusion.1), calls=%async_computation.1 | async-start | bytes 4194304 | tf_op jit(solution)/shard_map/all_to_all | solution.py:92
  180.9 6.3 %copy-start.8 = (f32[128,32]{1,0:T(8,128)S(1)}, f32[128,32]{1,0:T(8,128)}, u32[]{:S(2)}) copy-start(f32[128,32]{1,0:T(8,128)} %get-tuple-element.96) | copy-start | bytes 49156
  180.9 6.4 %copy-start.7 = (bf16[1,128,2048]{2,1,0:T(8,128)(2,1)S(1)}, bf16[1,128,2048]{2,1,0:T(8,128)(2,1)}, u32[]{:S(2)}) copy-start(bf16[1,128,2048]{2,1,0:T(8,128)(2,1)} %param.12) | copy-start | bytes 1572868
  184.6 20.5 %collective-permute-start.3 = (bf16[1024,1024]{0,1:T(8,128)(2,1)}, bf16[1024,1024]{0,1:T(8,128)(2,1)}, u32[]{:S(2)}, u32[]{:S(2)}) collective-permute-start(bf16[1024,1024]{0,1:T(8,128)(2,1)} %bitcast.43), channel_id=1, source_target_pairs={{0,32},{32,0},{64,96},{96,64},{128,160},{160,128},{192,224},{224,1... | collective-permute-start | bytes 6291464 | tf_op jit(solution)/shard_map/ppermute | solution.py:106
  188.5 14.0 %copy-start.5 = (f32[8,128,4,64]{1,3,2,0:T(8,128)S(1)}, f32[8,128,4,64]{1,3,2,0:T(8,128)}, u32[]{:S(2)}) copy-start(f32[8,128,4,64]{1,3,2,0:T(8,128)} %get-tuple-element.44) | copy-start | bytes 3145732
  202.5 1.2 copy-start.6
  203.7 1.0 copy-start.10
  210.1 16.3 %collective-permute-start.4 = (bf16[128,1024]{1,0:T(8,128)(2,1)S(1)}, bf16[128,1024]{1,0:T(8,128)(2,1)S(1)}, u32[]{:S(2)}, u32[]{:S(2)}) collective-permute-start(bf16[128,1024]{1,0:T(8,128)(2,1)S(1)} %fusion.24), channel_id=1, source_target_pairs={{28,32},{32,28},{60,64},{64,60},{92,96},{96,92},{124,128},{128,124... | collective-permute-start | bytes 786440 | tf_op jit(solution)/shard_map/ppermute | solution.py:203
Sparse Core Ops, SparseCore 0:
  22.5 72.7 all-gather.4
  98.4 37.3 all-gather.6

commit v8 on v7

--- a/solution.py
+++ b/solution.py
@@ -61,9 +61,12 @@
     parts = lax.axis_size("x")
     per_part = 2 * H // parts
     packed = packed.reshape(parts, per_part, P_SIZE + PAD_ROWS, N)
-    mine = lax.all_to_all(packed, "x", 0, 0, tiled=True)
+    half = parts // 2
+    odd = lax.axis_index("win") % 2 == 1
+    send = jnp.where(odd, jnp.concatenate([packed[half:], packed[:half]]), packed)
+    mine = lax.all_to_all(send, "x", 0, 0, tiled=True)
     mine, hold = lax.optimization_barrier((mine, hold))
-    is_bwd = lax.axis_index("x") >= parts // 2
+    is_bwd = jnp.logical_xor(lax.axis_index("x") >= half, odd)
     ordered = jnp.where(is_bwd, mine[::-1], mine)
     logs, states = split_packed(ordered)
     acc = (jnp.zeros_like(logs[0]), jnp.zeros_like(states[0]))
@@ -72,17 +75,19 @@
         pre.append(acc)
         acc = combine(acc, (logs[k], states[k]))
     rows = lax.axis_size("z")
+    wins = lax.axis_size("win")
     total = acc
     entering = (jnp.zeros_like(acc[0]), jnp.zeros_like(acc[1]))
     d = 1
     while d < rows:
         pairs = []
-        for z in range(rows):
-            for x in range(parts):
-                to = z + d if x < parts // 2 else z - d
-                if 0 <= to < rows:
-                    pairs.append((z * parts + x, to * parts + x))
-        got = split_packed(lax.ppermute(pack(*total), ("z", "x"), pairs))
+        for w in range(wins):
+            for z in range(rows):
+                for x in range(parts):
+                    to = z - d if (x >= half) != (w % 2 == 1) else z + d
+                    if 0 <= to < rows:
+                        pairs.append(((w * rows + z) * parts + x, (w * rows + to) * parts + x))
+        got = split_packed(lax.ppermute(pack(*total), ("win", "z", "x"), pairs))
         entering = combine(got, entering)
         if d * 2 < rows:
             total = combine(got, total)
@@ -90,6 +95,7 @@
     out = jnp.stack([combine(entering, pre[k])[1] for k in range(ROW)])
     out = jnp.where(is_bwd, out[::-1], out)
     back = lax.all_to_all(out, "x", 0, 0, tiled=True)
+    back = jnp.where(odd, jnp.concatenate([back[half:], back[:half]]), back)
     back = back.reshape(2, H, P_SIZE, N)
     return back[0], back[1], hold
 

time: 239 us -> 203 us (0.85); the launches traced: 234 us -> 202 us
  starting transfers between devices: 76.9 us -> 55.8 us
  waiting for transfers between devices: 89.9 us -> 76 us
    ppermute x3, waiting for transfers between devices: 36.1 us -> 15.5 us  [scan_states(): got = split_packed(lax.ppermute(pack(*total), ('win', 'z', 'x'), pairs))]
    all_to_all x1, starting transfers between devices: 37.3 us -> 21.1 us  [scan_states(): back = lax.all_to_all(out, 'x', 0, 0, tiled=True)]
    ppermute x3, starting transfers between devices: 31.3 us -> 19.2 us  [scan_states(): got = split_packed(lax.ppermute(pack(*total), ('win', 'z', 'x'), pairs))]
    all_gather x1, waiting for transfers between devices: 5.19 us -> 16.9 us  [gather_weight(): column = lax.all_gather(output_weight, 'z', axis=0)]
    ppermute x1, starting transfers between devices: 1.92 us -> 8.92 us  [per_device(): partner = lax.ppermute(projected_rows, ('win', 'z'), pairs)]
    ppermute x1, waiting for transfers between devices: 14.2 us -> 8.94 us  [per_device(): partner = lax.ppermute(projected_rows, ('win', 'z'), pairs)]
    all_gather x1, waiting for transfers between devices: 0.01 us -> 4.4 us  [gather_weight(): row = lax.all_gather(mine, 'x', axis=1)]
    all_to_all x1, waiting for transfers between devices: 13.7 us -> 9.7 us  [scan_states(): back = lax.all_to_all(out, 'x', 0, 0, tiled=True)]
  transfers between devices with their start and end apart: 9 -> 9, of which waited for: 7 -> 7; matrix products, arithmetic and copies ran while one was open for 15% -> 18% of each run, Pallas kernels for 0% -> 0%
where the time goes in v8:
time: 203 us; the launch traced here: 202 us
  waiting for transfers between devices  76 us (37%)
  starting transfers between devices  55.8 us (27%)
  local copies, waits for them, and re-layouts  20.9 us (10%)
  other arithmetic  18.9 us (9%)
  matrix products  16.3 us (8%)
  between operations  13.8 us (7%)
    all_to_all x1, starting transfers between devices, scan_states(): back = lax.all_to_all(out, 'x', 0, 0, tiled=True)  21.1 us
    all_to_all x1, waiting for transfers between devices, scan_states(): mine = lax.all_to_all(send, 'x', 0, 0, tiled=True)  19.9 us
    ppermute x3, starting transfers between devices, scan_states(): got = split_packed(lax.ppermute(pack(*total), ('win', 'z', 'x'), pairs))  19.2 us
    all_gather x1, waiting for transfers between devices, gather_weight(): column = lax.all_gather(output_weight, 'z', axis=0)  16.9 us
    ppermute x3, waiting for transfers between devices, scan_states(): got = split_packed(lax.ppermute(pack(*total), ('win', 'z', 'x'), pairs))  15.5 us
    all_to_all x1, waiting for transfers between devices, scan_states(): back = lax.all_to_all(out, 'x', 0, 0, tiled=True)  9.7 us
    unnamed x41, local copies, waits for them, and re-layouts  9.5 us
    ppermute x1, waiting for transfers between devices, per_device(): partner = lax.ppermute(projected_rows, ('win', 'z'), pairs)  8.94 us
  transfers between devices with their start and end apart: 9, of which 7 were waited for; matrix products, arithmetic and copies ran while one was open for 18% of the time, Pallas kernels for 0%

profile of v8, /device:TPU:24, one launch (start us, length us, event | category | flops | bytes accessed | tf_op | source)
XLA Modules:
  0.0 201.9 jit_solution(14033504211552547546)
XLA Ops:
  6.5 0.8 compare_select_fusion
  7.3 0.7 multiply_bitcast_fusion
  8.3 0.2 reduce_window_sum.17
  8.5 0.2 reduce_window_sum.18
  8.7 0.7 fusion.54
  9.5 1.3 copy.96
  10.8 0.8 bitcast_convert_fusion
  11.7 0.8 convolution_bitcast_fusion.4
  12.5 0.8 convolution_bitcast_fusion.3
  13.5 0.2 pad_maximum_fusion
  13.9 1.7 maximum_select_fusion.2
  15.5 4.4 %all-to-all-start = ((f32[4,16,72,128]{3,2,1,0:T(8,128)}), f32[4,16,72,128]{3,2,1,0:T(8,128)S(1)}, u32[]{:S(2)}, u32[]{:S(2)}) async-start(f32[4,16,72,128]{3,2,1,0:T(8,128)} %maximum_select_fusion.2), calls=%async_computation | async-start | bytes 4718592 | tf_op jit(solution)/shard_map/all_to_all | solution.py:67
  20.0 0.7 all-gather.5.cloned.1.call-update
  20.9 8.2 %while.11 = (s32[]{:T(128)}, f32[8,128,4,64]{1,3,2,0:T(8,128)}, bf16[8,128,4,64]{1,3,2,0:T(8,128)(2,1)S(1)}, f32[128,128]{1,0:T(8,128)S(1)}, f32[8,4,128]{2,1,0:...) while((s32[]{:T(128)}, f32[8,128,4,64]{1,3,2,0:T(8,128)}, ...), condition=%wide.region_4.5_spmd.clone, body=%wide.region_3.4_spmd.clone.sunk | while | flops 8732674 | bytes 312401 | solution.py:177
  21.0 1.0 fusion.64
  22.0 1.0 fusion.64
  23.1 1.0 fusion.64
  24.1 1.0 fusion.64
  25.1 1.0 fusion.64
  26.1 1.0 fusion.64
  27.2 1.0 fusion.64
  28.2 1.0 fusion.64
  29.2 19.9 %all-to-all-done = f32[4,16,72,128]{3,2,1,0:T(8,128)S(1)} async-done(((f32[4,16,72,128]{3,2,1,0:T(8,128)}), f32[4,16,72,128]{3,2,1,0:T(8,128)S(1)}, u32[]{:S(2)}, u32[]{:S(2)}) %all-to-all-start) | async-done | bytes 2359328 | tf_op jit(solution)/shard_map/all_to_all | solution.py:67
  49.1 1.4 copy-done.1
  50.5 2.6 %reverse_select_fusion = f32[4,16,72,128]{3,2,1,0:T(8,128)S(1)} fusion(f32[4,16,72,128]{3,2,1,0:T(8,128)} %copy-done.1, pred[]{:T(512)S(6)} %xor.3), kind=kLoop, calls=%fused_computation.24 | loop fusion | flops 589824 | bytes 4718593 | tf_op jit(solution)/shard_map/jit(_where)/select_n | solution.py:70
  53.2 0.3 exponential_reduce_fusion
  53.5 1.0 fusion.35
  54.7 3.9 %collective-permute-start = (f32[16,72,128]{2,1,0:T(8,128)S(1)}, f32[16,72,128]{2,1,0:T(8,128)S(1)}, u32[]{:S(2)}, u32[]{:S(2)}) collective-permute-start(f32[16,72,128]{2,1,0:T(8,128)S(1)} %pad_maximum_fusion.2), channel_id=1, source_target_pairs={{0,4},{1,5},{4,8},{5,9},{6,2},{7,3},{8,12},{9,13},{10,6},{11,7},{1... | collective-permute-start | bytes 1769480 | tf_op jit(solution)/shard_map/ppermute | solution.py:90
  58.5 9.7 %collective-permute-done = f32[16,72,128]{2,1,0:T(8,128)S(1)} collective-permute-done((f32[16,72,128]{2,1,0:T(8,128)S(1)}, f32[16,72,128]{2,1,0:T(8,128)S(1)}, u32[]{:S(2)}, u32[]{:S(2)}) %collective-permute-start) | collective-permute-done | bytes 589856 | tf_op jit(solution)/shard_map/ppermute | solution.py:90
  68.2 0.8 copy-done.4
  69.1 1.2 multiply_add_fusion.1
  70.4 0.9 pad_maximum_fusion.3
  71.3 7.5 %collective-permute-start.1 = (f32[16,72,128]{2,1,0:T(8,128)}, f32[16,72,128]{2,1,0:T(8,128)S(1)}, u32[]{:S(2)}, u32[]{:S(2)}) collective-permute-start(f32[16,72,128]{2,1,0:T(8,128)} %pad_maximum_fusion.3), channel_id=1, source_target_pairs={{0,8},{1,9},{4,12},{5,13},{8,16},{9,17},{10,2},{11,3},{12,20},{13,... | collective-permute-start | bytes 1769480 | tf_op jit(solution)/shard_map/ppermute | solution.py:90
  78.8 16.9 %all-gather.5.cloned.1.call-done = bf16[16384,32]{0,1:T(8,128)(2,1)} async-done(((bf16[2048,32]{0,1:T(8,128)(2,1)}), bf16[16384,32]{0,1:T(8,128)(2,1)}) %all-gather.5.cloned.1.call-update) | async-done | bytes 1048592 | tf_op jit(solution)/shard_map/all_gather | solution.py:106
  95.7 2.8 %copy.110 = bf16[4,8,8,2048]{3,2,1,0:T(8,128)(2,1)} copy(bf16[4,8,8,2048]{3,1,2,0:T(8,128)(2,1)} %bitcast.166) | data formatting | bytes 2097152
  98.6 0.5 exponential_bitcast_fusion.2
  99.1 0.2 copy-done.6
  99.5 0.9 pad_maximum_fusion.4
  100.4 7.8 %collective-permute-start.2 = (f32[16,72,128]{2,1,0:T(8,128)}, f32[16,72,128]{2,1,0:T(8,128)}, u32[]{:S(2)}, u32[]{:S(2)}) collective-permute-start(f32[16,72,128]{2,1,0:T(8,128)} %pad_maximum_fusion.4), channel_id=1, source_target_pairs={{0,16},{1,17},{4,20},{5,21},{8,24},{9,25},{12,28},{13,29},{18,2},{... | collective-permute-start | bytes 1769480 | tf_op jit(solution)/shard_map/ppermute | solution.py:90
  108.2 1.1 copy.109
  109.4 5.8 %collective-permute-done.2 = f32[16,72,128]{2,1,0:T(8,128)} collective-permute-done((f32[16,72,128]{2,1,0:T(8,128)}, f32[16,72,128]{2,1,0:T(8,128)}, u32[]{:S(2)}, u32[]{:S(2)}) %collective-permute-start.2) | collective-permute-done | bytes 589856 | tf_op jit(solution)/shard_map/ppermute | solution.py:90
  115.2 1.4 add_bitcast_fusion.2
  116.7 0.2 add_bitcast_fusion.1
  116.9 0.2 pad_maximum_fusion.1
  117.1 1.5 reverse_select_fusion.1
  118.6 21.1 %all-to-all-start.1 = ((f32[4,16,64,128]{3,2,1,0:T(8,128)}), f32[4,16,64,128]{3,2,1,0:T(8,128)S(1)}, u32[]{:S(2)}, u32[]{:S(2)}) async-start(f32[4,16,64,128]{3,2,1,0:T(8,128)} %reverse_select_fusion.1), calls=%async_computation.1 | async-start | bytes 4194304 | tf_op jit(solution)/shard_map/all_to_all | solution.py:97
  139.8 1.3 copy.104
  141.1 0.6 dynamic_slice.17
  141.7 0.6 iota_compare_fusion.1
  142.4 4.4 %all-gather.7.cloned.1.call-done = bf16[8,4096,32]{1,2,0:T(8,128)(2,1)} async-done(((bf16[8,1024,32]{1,2,0:T(8,128)(2,1)}), bf16[8,4096,32]{1,2,0:T(8,128)(2,1)}) %all-gather.7.cloned.1.call-update) | async-done | bytes 2097168 | tf_op jit(solution)/shard_map/all_gather | solution.py:108
  146.8 4.5 %reshape.289 = bf16[8,4,1024,32]{2,1,3,0:T(4,128)(2,1)} reshape(bf16[8,4096,32]{1,2,0:T(8,128)(2,1)} %all-gather.7.cloned.1.call-done) | data formatting | bytes 4194304 | tf_op jit(solution)/shard_map/all_gather | solution.py:108
  151.3 3.6 %copy.106 = bf16[1024,8,4,32]{0,3,2,1:T(8,128)(2,1)} copy(bf16[1024,8,4,32]{0,2,3,1:T(4,128)(2,1)} %bitcast.155) | data formatting | bytes 4194304 | tf_op jit(solution)/shard_map/transpose | solution.py:109
  155.0 2.1 %collective-permute-start.3 = (bf16[1024,1024]{0,1:T(8,128)(2,1)}, bf16[1024,1024]{0,1:T(8,128)(2,1)}, u32[]{:S(2)}, u32[]{:S(2)}) collective-permute-start(bf16[1024,1024]{0,1:T(8,128)(2,1)} %bitcast.45), channel_id=1, source_target_pairs={{0,32},{32,0},{64,96},{96,64},{128,160},{160,128},{192,224},{224,1... | collective-permute-start | bytes 6291464 | tf_op jit(solution)/shard_map/ppermute | solution.py:112
  157.1 9.7 %all-to-all-done.1 = f32[4,16,64,128]{3,2,1,0:T(8,128)S(1)} async-done(((f32[4,16,64,128]{3,2,1,0:T(8,128)}), f32[4,16,64,128]{3,2,1,0:T(8,128)S(1)}, u32[]{:S(2)}, u32[]{:S(2)}) %all-to-all-start.1) | async-done | bytes 2097184 | tf_op jit(solution)/shard_map/all_to_all | solution.py:97
  166.9 0.4 maximum_select_fusion.3
  167.5 1.1 copy-done.7
  168.5 0.6 fusion.22
  169.2 0.8 multiply_reduce_fusion
  170.2 0.5 copy-done.10
  170.7 0.3 fusion.25
  171.1 5.0 %fusion.24 = bf16[128,1024]{1,0:T(8,128)(2,1)S(1)} fusion(bf16[128,2048]{0,1:T(8,128)(2,1)S(1)} %fusion.25, bf16[1024,1024]{0,1:T(8,128)(2,1)} %collective-permute-done.3, bf16[1024,1024]{0,1:T(8,128)(2,1)} %bitcast.45, pred[]{:T(512)S(6)} %eq.36), kind=kOutput, calls=%fused_computation.41 | convolution fusion | flops 555876352 | bytes 4980737 | tf_op jit(solution)/shard_map/dot_general | solution.py:197
  176.1 8.9 %collective-permute-start.4 = (bf16[128,1024]{1,0:T(8,128)(2,1)S(1)}, bf16[128,1024]{1,0:T(8,128)(2,1)S(1)}, u32[]{:S(2)}, u32[]{:S(2)}) collective-permute-start(bf16[128,1024]{1,0:T(8,128)(2,1)S(1)} %fusion.24), channel_id=1, source_target_pairs={{28,32},{32,28},{60,64},{64,60},{92,96},{96,92},{124,128},{128,124... | collective-permute-start | bytes 786440 | tf_op jit(solution)/shard_map/ppermute | solution.py:209
  185.1 8.9 %collective-permute-done.4 = bf16[128,1024]{1,0:T(8,128)(2,1)S(1)} collective-permute-done((bf16[128,1024]{1,0:T(8,128)(2,1)S(1)}, bf16[128,1024]{1,0:T(8,128)(2,1)S(1)}, u32[]{:S(2)}, u32[]{:S(2)}) %collective-permute-start.4) | collective-permute-done | bytes 262176 | tf_op jit(solution)/shard_map/ppermute | solution.py:209
  194.1 0.9 fusion.39
  (90 shorter events, 2.6 us)
Async XLA Ops:
  6.5 14.3 %copy-start = (bf16[1,128,128]{2,1,0:T(8,128)(2,1)S(1)}, bf16[1,128,128]{2,1,0:T(8,128)(2,1)}, u32[]{:S(2)}) copy-start(bf16[1,128,128]{2,1,0:T(8,128)(2,1)} %param.14) | copy-start | bytes 98308
  15.5 5.3 %copy-start.9 = (bf16[1,128,128]{2,1,0:T(8,128)(2,1)S(1)}, bf16[1,128,128]{2,1,0:T(8,128)(2,1)}, u32[]{:S(2)}) copy-start(bf16[1,128,128]{2,1,0:T(8,128)(2,1)} %param.13) | copy-start | bytes 98308
  15.5 33.6 %all-to-all-start = ((f32[4,16,72,128]{3,2,1,0:T(8,128)}), f32[4,16,72,128]{3,2,1,0:T(8,128)S(1)}, u32[]{:S(2)}, u32[]{:S(2)}) async-start(f32[4,16,72,128]{3,2,1,0:T(8,128)} %maximum_select_fusion.2), calls=%async_computation | async-start | bytes 4718592 | tf_op jit(solution)/shard_map/all_to_all | solution.py:67
  20.0 75.7 %all-gather.5.cloned.1.call-start = ((), (), s32[]{:S(2)}) async-start(), calls=%async_computation.2 | async-start | bytes 1179648 | tf_op jit(solution)/shard_map/all_gather | solution.py:106
  20.7 126.1 %all-gather.7.cloned.1.call-start = ((), (), s32[]{:S(2)}) async-start(), calls=%async_computation.3 | async-start | bytes 2621440 | tf_op jit(solution)/shard_map/all_gather | solution.py:108
  49.1 1.4 copy-start.1
  53.5 1.2 copy-start.11
  53.5 1.2 copy-start.15
  54.7 13.6 %collective-permute-start = (f32[16,72,128]{2,1,0:T(8,128)S(1)}, f32[16,72,128]{2,1,0:T(8,128)S(1)}, u32[]{:S(2)}, u32[]{:S(2)}) collective-permute-start(f32[16,72,128]{2,1,0:T(8,128)S(1)} %pad_maximum_fusion.2), channel_id=1, source_target_pairs={{0,4},{1,5},{4,8},{5,9},{6,2},{7,3},{8,12},{9,13},{10,6},{11,7},{1... | collective-permute-start | bytes 1769480 | tf_op jit(solution)/shard_map/ppermute | solution.py:90
  68.2 0.8 copy-start.4
  71.3 27.2 %collective-permute-start.1 = (f32[16,72,128]{2,1,0:T(8,128)}, f32[16,72,128]{2,1,0:T(8,128)S(1)}, u32[]{:S(2)}, u32[]{:S(2)}) collective-permute-start(f32[16,72,128]{2,1,0:T(8,128)} %pad_maximum_fusion.3), channel_id=1, source_target_pairs={{0,8},{1,9},{4,12},{5,13},{8,16},{9,17},{10,2},{11,3},{12,20},{13,... | collective-permute-start | bytes 1769480 | tf_op jit(solution)/shard_map/ppermute | solution.py:90
  98.5 0.8 copy-start.6
  98.6 9.6 %copy-start.2 = (bf16[4,8,8,2048]{3,2,1,0:T(8,128)(2,1)S(1)}, bf16[4,8,8,2048]{3,2,1,0:T(8,128)(2,1)}, u32[]{:S(2)}) copy-start(bf16[4,8,8,2048]{3,2,1,0:T(8,128)(2,1)} %copy.110) | copy-start | bytes 3145732
  99.4 15.8 %copy-start.5 = (f32[16,72,128]{2,1,0:T(8,128)S(1)}, f32[16,72,128]{2,1,0:T(8,128)}, u32[]{:S(2)}) copy-start(f32[16,72,128]{2,1,0:T(8,128)} %copy-done.4) | copy-start | bytes 1769476
  99.4 15.8 %copy-start.12 = (f32[16]{0:T(128)S(1)}, f32[16]{0:T(128)}, u32[]{:S(2)}) copy-start(f32[16]{0:T(128)} %copy-done.11) | copy-start | bytes 196
  99.4 15.8 %copy-start.13 = (f32[16]{0:T(128)S(1)}, f32[16]{0:T(128)}, u32[]{:S(2)}) copy-start(f32[16]{0:T(128)} %get-tuple-element.108) | copy-start | bytes 196
  99.4 15.8 %copy-start.14 = (f32[16]{0:T(128)S(1)}, f32[16]{0:T(128)}, u32[]{:S(2)}) copy-start(f32[16]{0:T(128)} %get-tuple-element.113) | copy-start | bytes 196
  99.4 15.8 %copy-start.16 = (f32[16]{0:T(128)S(1)}, f32[16]{0:T(128)}, u32[]{:S(2)}) copy-start(f32[16]{0:T(128)} %copy-done.15) | copy-start | bytes 196
  100.4 14.8 %collective-permute-start.2 = (f32[16,72,128]{2,1,0:T(8,128)}, f32[16,72,128]{2,1,0:T(8,128)}, u32[]{:S(2)}, u32[]{:S(2)}) collective-permute-start(f32[16,72,128]{2,1,0:T(8,128)} %pad_maximum_fusion.4), channel_id=1, source_target_pairs={{0,16},{1,17},{4,20},{5,21},{8,24},{9,25},{12,28},{13,29},{18,2},{... | collective-permute-start | bytes 1769480 | tf_op jit(solution)/shard_map/ppermute | solution.py:90
  109.4 7.3 %copy-start.3 = (f32[16,64,128]{2,1,0:T(8,128)S(1)}, f32[16,64,128]{2,1,0:T(8,128)}, u32[]{:S(2)}) copy-start(f32[16,64,128]{2,1,0:T(8,128)} %get-tuple-element.89) | copy-start | bytes 1572868
  118.6 21.2 %copy-start.8 = (f32[128,32]{1,0:T(8,128)S(1)}, f32[128,32]{1,0:T(8,128)}, u32[]{:S(2)}) copy-start(f32[128,32]{1,0:T(8,128)} %get-tuple-element.100) | copy-start | bytes 49156
  118.6 22.5 %copy-start.17 = (s32[16]{0:T(128)S(1)}, s32[16]{0:T(128)}, u32[]{:S(2)}) copy-start(s32[16]{0:T(128)} %param.19) | copy-start | bytes 196
  118.6 48.1 %all-to-all-start.1 = ((f32[4,16,64,128]{3,2,1,0:T(8,128)}), f32[4,16,64,128]{3,2,1,0:T(8,128)S(1)}, u32[]{:S(2)}, u32[]{:S(2)}) async-start(f32[4,16,64,128]{3,2,1,0:T(8,128)} %reverse_select_fusion.1), calls=%async_computation.1 | async-start | bytes 4194304 | tf_op jit(solution)/shard_map/all_to_all | solution.py:97
  155.0 16.1 %collective-permute-start.3 = (bf16[1024,1024]{0,1:T(8,128)(2,1)}, bf16[1024,1024]{0,1:T(8,128)(2,1)}, u32[]{:S(2)}, u32[]{:S(2)}) collective-permute-start(bf16[1024,1024]{0,1:T(8,128)(2,1)} %bitcast.45), channel_id=1, source_target_pairs={{0,32},{32,0},{64,96},{96,64},{128,160},{160,128},{192,224},{224,1... | collective-permute-start | bytes 6291464 | tf_op jit(solution)/shard_map/ppermute | solution.py:112
  167.3 1.2 copy-start.7
  170.0 0.7 copy-start.10
  176.1 18.0 %collective-permute-start.4 = (bf16[128,1024]{1,0:T(8,128)(2,1)S(1)}, bf16[128,1024]{1,0:T(8,128)(2,1)S(1)}, u32[]{:S(2)}, u32[]{:S(2)}) collective-permute-start(bf16[128,1024]{1,0:T(8,128)(2,1)S(1)} %fusion.24), channel_id=1, source_target_pairs={{28,32},{32,28},{60,64},{64,60},{92,96},{96,92},{124,128},{128,124... | collective-permute-start | bytes 786440 | tf_op jit(solution)/shard_map/ppermute | solution.py:209
Sparse Core Ops, SparseCore 0:
  22.9 72.7 all-gather.4
  109.5 37.2 all-gather.6

commit v9 on v8

--- a/solution.py
+++ b/solution.py
@@ -48,19 +48,29 @@
 
 
 def split_packed(packed):
-    return packed[..., P_SIZE, 0], packed[..., :P_SIZE, :]
+    lead = packed.shape[:-2]
+    state_rows = packed.shape[-2] - PAD_ROWS
+    heads = state_rows // P_SIZE
+    states = packed[..., :state_rows, :].reshape(lead + (heads, P_SIZE, N))
+    return packed[..., state_rows, :heads], states
 
 
 def pack(logs, states):
-    rows = jnp.broadcast_to(logs[..., None, None], logs.shape + (PAD_ROWS, N))
-    return jnp.concatenate([states, rows], axis=-2)
+    lead = states.shape[:-3]
+    heads = logs.shape[-1]
+    flat = states.reshape(lead + (heads * P_SIZE, N))
+    widths = [(0, 0)] * len(lead) + [(0, PAD_ROWS * N - heads)]
+    block = jnp.pad(logs, widths).reshape(lead + (PAD_ROWS, N))
+    return jnp.concatenate([flat, block], axis=-2)
 
 
 def scan_states(log_fwd, log_bwd, fresh_fwd, fresh_bwd, hold):
-    packed = pack(jnp.stack([log_fwd, log_bwd]), jnp.stack([fresh_fwd, fresh_bwd]))
     parts = lax.axis_size("x")
     per_part = 2 * H // parts
-    packed = packed.reshape(parts, per_part, P_SIZE + PAD_ROWS, N)
+    packed = pack(
+        jnp.stack([log_fwd, log_bwd]).reshape(parts, per_part),
+        jnp.stack([fresh_fwd, fresh_bwd]).reshape(parts, per_part, P_SIZE, N),
+    )
     half = parts // 2
     odd = lax.axis_index("win") % 2 == 1
     send = jnp.where(odd, jnp.concatenate([packed[half:], packed[:half]]), packed)

time: 203 us -> 223 us (1.099)
  waiting for transfers between devices: 76 us -> 106 us
  starting transfers between devices: 55.8 us -> 48.8 us
  matrix products: 16.3 us -> 13 us
    all_to_all x1, waiting for transfers between devices: 9.7 us -> 35.3 us  [scan_states(): back = lax.all_to_all(out, 'x', 0, 0, tiled=True)]
    all_to_all x1, starting transfers between devices: 21.1 us -> 9.4 us  [scan_states(): back = lax.all_to_all(out, 'x', 0, 0, tiled=True)]
    all_gather x1, waiting for transfers between devices: 16.9 us -> 25 us  [gather_weight(): column = lax.all_gather(output_weight, 'z', axis=0)]
    ppermute x3, starting transfers between devices: 19.2 us -> 24.7 us  [scan_states(): got = split_packed(lax.ppermute(pack(*total), ('win', 'z', 'x'), pairs))]
    dot_general x1, matrix products: 5.03 us -> 1.73 us  [per_device(): jnp.dot(normed, gather_weight(output_weight), preferred_element_type=jnp....]
    add x3 -> x5, other arithmetic: 2.28 us -> 5.21 us  [combine(): jnp.exp(later[0])[..., None, None] * earlier[1] + later[1]]
    unnamed x41 -> x27, local copies, waits for them, and re-layouts: 9.5 us -> 8.04 us
  transfers between devices with their start and end apart: 9 -> 9, of which waited for: 7 -> 7; matrix products, arithmetic and copies ran while one was open for 18% -> 13% of each run, Pallas kernels for 0% -> 0%
where the time goes in v9:
time: 223 us; the launch traced here: 221 us
  waiting for transfers between devices  106 us (48%)
  starting transfers between devices  48.8 us (22%)
  local copies, waits for them, and re-layouts  20.9 us (9%)
  other arithmetic  19.3 us (9%)
  between operations  13.8 us (6%)
  matrix products  13 us (6%)
    all_to_all x1, waiting for transfers between devices, scan_states(): back = lax.all_to_all(out, 'x', 0, 0, tiled=True)  35.3 us
    all_gather x1, waiting for transfers between devices, gather_weight(): column = lax.all_gather(output_weight, 'z', axis=0)  25 us
    ppermute x3, starting transfers between devices, scan_states(): got = split_packed(lax.ppermute(pack(*total), ('win', 'z', 'x'), pairs))  24.7 us
    all_to_all x1, waiting for transfers between devices, scan_states(): mine = lax.all_to_all(send, 'x', 0, 0, tiled=True)  18.1 us
    ppermute x3, waiting for transfers between devices, scan_states(): got = split_packed(lax.ppermute(pack(*total), ('win', 'z', 'x'), pairs))  15.4 us
    ppermute x1, waiting for transfers between devices, per_device(): partner = lax.ppermute(projected_rows, ('win', 'z'), pairs)  9.54 us
    all_to_all x1, starting transfers between devices, scan_states(): back = lax.all_to_all(out, 'x', 0, 0, tiled=True)  9.4 us
    ppermute x1, starting transfers between devices, per_device(): partner = lax.ppermute(projected_rows, ('win', 'z'), pairs)  8.14 us
  transfers between devices with their start and end apart: 9, of which 7 were waited for; matrix products, arithmetic and copies ran while one was open for 13% of the time, Pallas kernels for 0%

profile of v9, /device:TPU:24, one launch (start us, length us, event | category | flops | bytes accessed | tf_op | source)
XLA Modules:
  0.0 221.3 jit_solution(1602721294572059025)
XLA Ops:
  6.5 0.8 compare_select_fusion
  7.3 0.7 multiply_bitcast_fusion
  8.3 0.2 reduce_window_sum.17
  8.5 0.2 reduce_window_sum.18
  8.8 1.3 copy.53
  10.2 0.8 bitcast_convert_fusion
  11.1 0.8 convolution_bitcast_fusion.4
  11.9 0.8 convolution_bitcast_fusion.3
  13.0 0.1 fusion.26
  13.1 1.6 fusion.19
  14.8 4.4 %all-to-all-start = ((f32[4,1032,128]{2,1,0:T(8,128)}), f32[4,1032,128]{2,1,0:T(8,128)S(1)}, u32[]{:S(2)}, u32[]{:S(2)}) async-start(f32[4,1032,128]{2,1,0:T(8,128)} %fusion.19), calls=%async_computation | async-start | bytes 4227072 | tf_op jit(solution)/shard_map/all_to_all | solution.py:77
  19.4 8.2 %while.11 = (s32[]{:T(128)}, f32[8,128,4,64]{1,3,2,0:T(8,128)}, bf16[8,128,4,64]{1,3,2,0:T(8,128)(2,1)S(1)}, f32[128,128]{1,0:T(8,128)S(1)}, f32[8,4,128]{2,1,0:...) while((s32[]{:T(128)}, f32[8,128,4,64]{1,3,2,0:T(8,128)}, ...), condition=%wide.region_4.5_spmd.clone, body=%wide.region_3.4_spmd.clone.sunk | while | flops 8732674 | bytes 312401 | solution.py:187
  19.5 1.0 fusion.69
  20.5 1.0 fusion.69
  21.5 1.0 fusion.69
  22.5 1.0 fusion.69
  23.6 1.0 fusion.69
  24.6 1.0 fusion.69
  25.6 1.0 fusion.69
  26.6 1.0 fusion.69
  27.6 18.1 %all-to-all-done = f32[4,1032,128]{2,1,0:T(8,128)S(1)} async-done(((f32[4,1032,128]{2,1,0:T(8,128)}), f32[4,1032,128]{2,1,0:T(8,128)S(1)}, u32[]{:S(2)}, u32[]{:S(2)}) %all-to-all-start) | async-done | bytes 2113568 | tf_op jit(solution)/shard_map/all_to_all | solution.py:77
  45.7 1.4 copy-done.1
  47.1 2.4 %reverse_select_fusion = f32[4,1032,128]{2,1,0:T(8,128)S(1)} fusion(f32[4,1032,128]{2,1,0:T(8,128)} %copy-done.1, pred[]{:T(512)S(6)} %xor.3), kind=kLoop, calls=%fused_computation.27 | loop fusion | flops 528384 | bytes 4227073 | tf_op jit(solution)/shard_map/jit(_where)/select_n | solution.py:80
  50.1 0.9 fusion.37
  51.0 3.9 %collective-permute-start = (f32[1032,128]{1,0:T(8,128)S(1)}, f32[1032,128]{1,0:T(8,128)S(1)}, u32[]{:S(2)}, u32[]{:S(2)}) collective-permute-start(f32[1032,128]{1,0:T(8,128)S(1)} %pad_maximum_fusion.3), channel_id=1, source_target_pairs={{0,4},{1,5},{4,8},{5,9},{6,2},{7,3},{8,12},{9,13},{10,6},{11,7},{1... | collective-permute-start | bytes 1585160 | tf_op jit(solution)/shard_map/ppermute | solution.py:100
  55.1 6.5 %collective-permute-done = f32[1032,128]{1,0:T(8,128)S(1)} collective-permute-done((f32[1032,128]{1,0:T(8,128)S(1)}, f32[1032,128]{1,0:T(8,128)S(1)}, u32[]{:S(2)}, u32[]{:S(2)}) %collective-permute-start) | collective-permute-done | bytes 528416 | tf_op jit(solution)/shard_map/ppermute | solution.py:100
  61.6 0.8 copy-done.7
  62.4 1.9 multiply_add_fusion.4
  64.3 0.8 pad_maximum_fusion.4
  65.1 6.5 %collective-permute-start.1 = (f32[1032,128]{1,0:T(8,128)}, f32[1032,128]{1,0:T(8,128)}, u32[]{:S(2)}, u32[]{:S(2)}) collective-permute-start(f32[1032,128]{1,0:T(8,128)} %pad_maximum_fusion.4), channel_id=1, source_target_pairs={{0,8},{1,9},{4,12},{5,13},{8,16},{9,17},{10,2},{11,3},{12,20},{13,... | collective-permute-start | bytes 1585160 | tf_op jit(solution)/shard_map/ppermute | solution.py:100
  71.8 8.9 %collective-permute-done.1 = f32[1032,128]{1,0:T(8,128)} collective-permute-done((f32[1032,128]{1,0:T(8,128)}, f32[1032,128]{1,0:T(8,128)}, u32[]{:S(2)}, u32[]{:S(2)}) %collective-permute-start.1) | collective-permute-done | bytes 528416 | tf_op jit(solution)/shard_map/ppermute | solution.py:100
  80.7 0.7 add_exponential_fusion
  81.4 2.0 multiply_add_fusion.3
  83.4 0.8 pad_maximum_fusion.5
  84.2 14.3 %collective-permute-start.2 = (f32[1032,128]{1,0:T(8,128)}, f32[1032,128]{1,0:T(8,128)}, u32[]{:S(2)}, u32[]{:S(2)}) collective-permute-start(f32[1032,128]{1,0:T(8,128)} %pad_maximum_fusion.5), channel_id=1, source_target_pairs={{0,16},{1,17},{4,20},{5,21},{8,24},{9,25},{12,28},{13,29},{18,2},{... | collective-permute-start | bytes 1585160 | tf_op jit(solution)/shard_map/ppermute | solution.py:100
  98.6 25.0 %all-gather.5.cloned.1.call-done = bf16[16384,32]{0,1:T(8,128)(2,1)} async-done(((bf16[2048,32]{0,1:T(8,128)(2,1)}), bf16[16384,32]{0,1:T(8,128)(2,1)}) %all-gather.5.cloned.1.call-update) | async-done | bytes 1048592 | tf_op jit(solution)/shard_map/all_gather | solution.py:116
  123.5 1.8 copy.64
  125.4 1.1 copy.62
  126.7 1.1 slice.133
  127.8 0.2 multiply_add_fusion.2
  128.0 0.3 multiply_add_fusion.1
  128.3 0.2 pad_maximum_fusion.2
  128.5 1.5 reverse_select_fusion.1
  130.0 9.4 %all-to-all-start.1 = ((f32[4,16,64,128]{3,2,1,0:T(8,128)}), f32[4,16,64,128]{3,2,1,0:T(8,128)S(1)}, u32[]{:S(2)}, u32[]{:S(2)}) async-start(f32[4,16,64,128]{3,2,1,0:T(8,128)} %reverse_select_fusion.1), calls=%async_computation.1 | async-start | bytes 4194304 | tf_op jit(solution)/shard_map/all_to_all | solution.py:107
  139.5 1.3 copy.59
  140.8 0.6 dynamic_slice.17
  141.3 0.6 iota_compare_fusion.1
  142.1 35.3 %all-to-all-done.1 = f32[4,16,64,128]{3,2,1,0:T(8,128)S(1)} async-done(((f32[4,16,64,128]{3,2,1,0:T(8,128)}), f32[4,16,64,128]{3,2,1,0:T(8,128)S(1)}, u32[]{:S(2)}, u32[]{:S(2)}) %all-to-all-start.1) | async-done | bytes 2097184 | tf_op jit(solution)/shard_map/all_to_all | solution.py:107
  177.4 1.2 fusion.58
  178.6 2.3 %all-gather.7.cloned.1.call-done = bf16[8,4096,32]{1,2,0:T(8,128)(2,1)} async-done(((bf16[8,1024,32]{1,2,0:T(8,128)(2,1)}), bf16[8,4096,32]{1,2,0:T(8,128)(2,1)}) %all-gather.7.cloned.1.call-update) | async-done | bytes 2097168 | tf_op jit(solution)/shard_map/all_gather | solution.py:118
  180.8 4.5 %reshape.472 = bf16[8,4,1024,32]{2,1,3,0:T(4,128)(2,1)} reshape(bf16[8,4096,32]{1,2,0:T(8,128)(2,1)} %all-gather.7.cloned.1.call-done) | data formatting | bytes 4194304 | tf_op jit(solution)/shard_map/all_gather | solution.py:118
  185.3 2.4 %copy.61 = bf16[1024,8,4,32]{0,3,2,1:T(8,128)(2,1)S(1)} copy(bf16[1024,8,4,32]{0,2,3,1:T(4,128)(2,1)} %bitcast.182) | data formatting | bytes 4194304 | tf_op jit(solution)/shard_map/transpose | solution.py:119
  187.7 2.1 collective-permute-start.3
  189.9 0.4 maximum_select_fusion.2
  190.3 0.1 fusion.57
  190.4 1.1 copy-done.4
  191.5 0.6 fusion.23
  192.1 0.8 multiply_reduce_fusion
  193.1 0.5 copy-done.9
  193.7 0.3 fusion.28
  194.0 1.7 fusion.25
  195.8 8.1 %collective-permute-start.4 = (bf16[128,1024]{1,0:T(8,128)(2,1)S(1)}, bf16[128,1024]{1,0:T(8,128)(2,1)S(1)}, u32[]{:S(2)}, u32[]{:S(2)}) collective-permute-start(bf16[128,1024]{1,0:T(8,128)(2,1)S(1)} %fusion.25), channel_id=1, source_target_pairs={{28,32},{32,28},{60,64},{64,60},{92,96},{96,92},{124,128},{128,124... | collective-permute-start | bytes 786440 | tf_op jit(solution)/shard_map/ppermute | solution.py:219
  204.0 9.5 %collective-permute-done.4 = bf16[128,1024]{1,0:T(8,128)(2,1)S(1)} collective-permute-done((bf16[128,1024]{1,0:T(8,128)(2,1)S(1)}, bf16[128,1024]{1,0:T(8,128)(2,1)S(1)}, u32[]{:S(2)}, u32[]{:S(2)}) %collective-permute-start.4) | collective-permute-done | bytes 262176 | tf_op jit(solution)/shard_map/ppermute | solution.py:219
  213.5 0.9 fusion.41
  (87 shorter events, 2.8 us)
Async XLA Ops:
  6.5 12.7 %copy-start = (bf16[1,128,128]{2,1,0:T(8,128)(2,1)S(1)}, bf16[1,128,128]{2,1,0:T(8,128)(2,1)}, u32[]{:S(2)}) copy-start(bf16[1,128,128]{2,1,0:T(8,128)(2,1)} %param.14) | copy-start | bytes 98308
  14.8 4.5 %copy-start.8 = (bf16[1,128,128]{2,1,0:T(8,128)(2,1)S(1)}, bf16[1,128,128]{2,1,0:T(8,128)(2,1)}, u32[]{:S(2)}) copy-start(bf16[1,128,128]{2,1,0:T(8,128)(2,1)} %param.13) | copy-start | bytes 98308
  14.8 30.9 %all-to-all-start = ((f32[4,1032,128]{2,1,0:T(8,128)}), f32[4,1032,128]{2,1,0:T(8,128)S(1)}, u32[]{:S(2)}, u32[]{:S(2)}) async-start(f32[4,1032,128]{2,1,0:T(8,128)} %fusion.19), calls=%async_computation | async-start | bytes 4227072 | tf_op jit(solution)/shard_map/all_to_all | solution.py:77
  19.2 104.3 %all-gather.5.cloned.1.call-start = ((), (), s32[]{:S(2)}) async-start(), calls=%async_computation.2 | async-start | bytes 1179648 | tf_op jit(solution)/shard_map/all_gather | solution.py:116
  45.7 1.4 copy-start.1
  51.0 10.6 %collective-permute-start = (f32[1032,128]{1,0:T(8,128)S(1)}, f32[1032,128]{1,0:T(8,128)S(1)}, u32[]{:S(2)}, u32[]{:S(2)}) collective-permute-start(f32[1032,128]{1,0:T(8,128)S(1)} %pad_maximum_fusion.3), channel_id=1, source_target_pairs={{0,4},{1,5},{4,8},{5,9},{6,2},{7,3},{8,12},{9,13},{10,6},{11,7},{1... | collective-permute-start | bytes 1585160 | tf_op jit(solution)/shard_map/ppermute | solution.py:100
  54.9 125.9 %all-gather.7.cloned.1.call-start = ((), (), s32[]{:S(2)}) async-start(), calls=%async_computation.3 | async-start | bytes 2621440 | tf_op jit(solution)/shard_map/all_gather | solution.py:118
  61.6 0.8 copy-start.7
  65.1 15.6 %collective-permute-start.1 = (f32[1032,128]{1,0:T(8,128)}, f32[1032,128]{1,0:T(8,128)}, u32[]{:S(2)}, u32[]{:S(2)}) collective-permute-start(f32[1032,128]{1,0:T(8,128)} %pad_maximum_fusion.4), channel_id=1, source_target_pairs={{0,8},{1,9},{4,12},{5,13},{8,16},{9,17},{10,2},{11,3},{12,20},{13,... | collective-permute-start | bytes 1585160 | tf_op jit(solution)/shard_map/ppermute | solution.py:100
  84.2 42.4 %collective-permute-start.2 = (f32[1032,128]{1,0:T(8,128)}, f32[1032,128]{1,0:T(8,128)}, u32[]{:S(2)}, u32[]{:S(2)}) collective-permute-start(f32[1032,128]{1,0:T(8,128)} %pad_maximum_fusion.5), channel_id=1, source_target_pairs={{0,16},{1,17},{4,20},{5,21},{8,24},{9,25},{12,28},{13,29},{18,2},{... | collective-permute-start | bytes 1585160 | tf_op jit(solution)/shard_map/ppermute | solution.py:100
  126.5 1.2 copy-start.3
  130.0 9.5 %copy-start.6 = (bf16[1,128,2048]{2,1,0:T(8,128)(2,1)S(1)}, bf16[1,128,2048]{2,1,0:T(8,128)(2,1)}, u32[]{:S(2)}) copy-start(bf16[1,128,2048]{2,1,0:T(8,128)(2,1)} %param.12) | copy-start | bytes 1572868
  130.0 10.7 %copy-start.10 = (s32[16]{0:T(128)S(1)}, s32[16]{0:T(128)}, u32[]{:S(2)}) copy-start(s32[16]{0:T(128)} %param.19) | copy-start | bytes 196
  130.0 47.3 %all-to-all-start.1 = ((f32[4,16,64,128]{3,2,1,0:T(8,128)}), f32[4,16,64,128]{3,2,1,0:T(8,128)S(1)}, u32[]{:S(2)}, u32[]{:S(2)}) async-start(f32[4,16,64,128]{3,2,1,0:T(8,128)} %reverse_select_fusion.1), calls=%async_computation.1 | async-start | bytes 4194304 | tf_op jit(solution)/shard_map/all_to_all | solution.py:107
  185.3 4.5 %copy-start.2 = (f32[2,16,64,128]{3,2,1,0:T(8,128)S(1)}, f32[2,16,64,128]{3,2,1,0:T(8,128)}, u32[]{:S(2)}) copy-start(f32[2,16,64,128]{3,2,1,0:T(8,128)} %get-tuple-element.102) | copy-start | bytes 3145732
  187.7 6.3 %collective-permute-start.3 = (bf16[1024,1024]{0,1:T(8,128)(2,1)S(1)}, bf16[1024,1024]{0,1:T(8,128)(2,1)S(1)}, u32[]{:S(2)}, u32[]{:S(2)}) collective-permute-start(bf16[1024,1024]{0,1:T(8,128)(2,1)S(1)} %bitcast.190), channel_id=1, source_target_pairs={{0,32},{32,0},{64,96},{96,64},{128,160},{160,128},{192,224},{224,1... | collective-permute-start | bytes 6291464 | tf_op jit(solution)/shard_map/ppermute | solution.py:122
  190.3 1.2 copy-start.4
  190.4 1.7 copy-start.5
  193.0 0.7 copy-start.9
  195.8 17.8 %collective-permute-start.4 = (bf16[128,1024]{1,0:T(8,128)(2,1)S(1)}, bf16[128,1024]{1,0:T(8,128)(2,1)S(1)}, u32[]{:S(2)}, u32[]{:S(2)}) collective-permute-start(bf16[128,1024]{1,0:T(8,128)(2,1)S(1)} %fusion.25), channel_id=1, source_target_pairs={{28,32},{32,28},{60,64},{64,60},{92,96},{96,92},{124,128},{128,124... | collective-permute-start | bytes 786440 | tf_op jit(solution)/shard_map/ppermute | solution.py:219
Sparse Core Ops, SparseCore 0:
  55.0 68.4 all-gather.4
  126.6 54.1 all-gather.6

commit v10 on v8

--- a/solution.py
+++ b/solution.py
@@ -106,15 +106,20 @@
     column = lax.all_gather(output_weight, "z", axis=0)
     mine = lax.dynamic_slice_in_dim(column, half * half_rows, half_rows, axis=1)
     row = lax.all_gather(mine, "x", axis=1)
-    gathered = row.transpose(2, 0, 1, 3).reshape(half_rows, -1)
     wins = lax.axis_size("win")
     pairs = [(w, w ^ 1) for w in range(wins)]
-    other = lax.ppermute(gathered, "win", pairs)
-    return jnp.where(
-        half == 0,
-        jnp.concatenate([gathered, other], axis=0),
-        jnp.concatenate([other, gathered], axis=0),
-    )
+    other = lax.ppermute(row, "win", pairs)
+    return row, other, half
+
+
+def project(normed, gathered):
+    row, other, half = gathered
+    half_rows = row.shape[2]
+    mine_cols = lax.dynamic_slice_in_dim(normed, half * half_rows, half_rows, axis=1)
+    other_cols = lax.dynamic_slice_in_dim(normed, (1 - half) * half_rows, half_rows, axis=1)
+    out = jnp.einsum("tr,zxrc->tzxc", mine_cols, row, preferred_element_type=jnp.float32)
+    out = out + jnp.einsum("tr,zxrc->tzxc", other_cols, other, preferred_element_type=jnp.float32)
+    return out.reshape(normed.shape[0], -1)
 
 
 def per_device(
@@ -194,11 +199,7 @@
     normed = (
         (gated_rows * inverse_rms).reshape(frame_count, H * P_SIZE) * gated_norm_gain[None, :]
     ).astype(jnp.bfloat16)
-    projected_rows = jnp.dot(
-        normed,
-        gather_weight(output_weight),
-        preferred_element_type=jnp.float32,
-    ).astype(jnp.bfloat16)
+    projected_rows = project(normed, gather_weight(output_weight)).astype(jnp.bfloat16)
     window_index = lax.axis_index("win")
     window_total = lax.axis_size("win")
     row_index = lax.axis_index("z")

time: 203 us -> 203 us (level)
  waiting for transfers between devices: 76 us -> 81.5 us
  local copies, waits for them, and re-layouts: 20.9 us -> 16.1 us
    all_to_all x1, waiting for transfers between devices: 9.7 us -> 14.9 us  [scan_states(): back = lax.all_to_all(out, 'x', 0, 0, tiled=True)]
    transpose x1 -> x0, local copies, waits for them, and re-layouts: 3.63 us -> none  [gather_weight(): gathered = row.transpose(2, 0, 1, 3).reshape(half_rows, -1)]
    dot_general x1 -> x2, matrix products: 5.03 us -> 4.64 us  [the longest x1 2.32 us: project(): jnp.einsum('tr,zxrc->tzxc', other_cols, other, preferred_element_type=jnp...]
  transfers between devices with their start and end apart: 9 -> 9, of which waited for: 7 -> 7; matrix products, arithmetic and copies ran while one was open for 18% -> 16% of each run, Pallas kernels for 0% -> 0%
where the time goes in v10:
time: 203 us; the launch traced here: 201 us
  waiting for transfers between devices  81.5 us (40%)
  starting transfers between devices  55.3 us (27%)
  other arithmetic  18.7 us (9%)
  local copies, waits for them, and re-layouts  16.1 us (8%)
  matrix products  15.9 us (8%)
  between operations  13.9 us (7%)
    all_to_all x1, starting transfers between devices, scan_states(): back = lax.all_to_all(out, 'x', 0, 0, tiled=True)  21 us
    all_to_all x1, waiting for transfers between devices, scan_states(): mine = lax.all_to_all(send, 'x', 0, 0, tiled=True)  19.9 us
    ppermute x3, starting transfers between devices, scan_states(): got = split_packed(lax.ppermute(pack(*total), ('win', 'z', 'x'), pairs))  19.1 us
    all_gather x1, waiting for transfers between devices, gather_weight(): column = lax.all_gather(output_weight, 'z', axis=0)  16.9 us
    ppermute x3, waiting for transfers between devices, scan_states(): got = split_packed(lax.ppermute(pack(*total), ('win', 'z', 'x'), pairs))  15.5 us
    all_to_all x1, waiting for transfers between devices, scan_states(): back = lax.all_to_all(out, 'x', 0, 0, tiled=True)  14.9 us
    unnamed x41, local copies, waits for them, and re-layouts  9.18 us
    ppermute x1, waiting for transfers between devices, per_device(): partner = lax.ppermute(projected_rows, ('win', 'z'), pairs)  8.98 us
  transfers between devices with their start and end apart: 9, of which 7 were waited for; matrix products, arithmetic and copies ran while one was open for 16% of the time, Pallas kernels for 0%

profile of v10, /device:TPU:24, one launch (start us, length us, event | category | flops | bytes accessed | tf_op | source)
XLA Modules:
  0.0 201.4 jit_solution(13652489499460684593)
XLA Ops:
  6.5 0.8 compare_select_fusion
  7.3 0.7 multiply_bitcast_fusion
  8.3 0.2 reduce_window_sum.17
  8.5 0.2 reduce_window_sum.18
  8.7 0.7 fusion.52
  9.5 1.3 copy.101
  10.8 0.8 bitcast_convert_fusion
  11.7 0.8 convolution_bitcast_fusion.4
  12.5 0.8 convolution_bitcast_fusion.3
  13.5 0.2 pad_maximum_fusion
  13.9 1.7 maximum_select_fusion
  15.5 4.4 %all-to-all-start = ((f32[4,16,72,128]{3,2,1,0:T(8,128)}), f32[4,16,72,128]{3,2,1,0:T(8,128)S(1)}, u32[]{:S(2)}, u32[]{:S(2)}) async-start(f32[4,16,72,128]{3,2,1,0:T(8,128)} %maximum_select_fusion), calls=%async_computation | async-start | bytes 4718592 | tf_op jit(solution)/shard_map/all_to_all | solution.py:67
  20.0 0.7 all-gather.5.cloned.1.call-update
  20.9 8.2 %while.11 = (s32[]{:T(128)}, f32[8,128,4,64]{1,3,2,0:T(8,128)}, bf16[8,128,4,64]{1,3,2,0:T(8,128)(2,1)S(1)}, f32[128,128]{1,0:T(8,128)S(1)}, f32[8,4,128]{2,1,0:...) while((s32[]{:T(128)}, f32[8,128,4,64]{1,3,2,0:T(8,128)}, ...), condition=%wide.region_4.5_spmd.clone, body=%wide.region_3.4_spmd.clone.sunk | while | flops 8732674 | bytes 312401 | solution.py:182
  21.0 1.0 fusion.62
  22.0 1.0 fusion.62
  23.1 1.0 fusion.62
  24.1 1.0 fusion.62
  25.1 1.0 fusion.62
  26.1 1.0 fusion.62
  27.1 1.0 fusion.62
  28.2 1.0 fusion.62
  29.2 19.9 %all-to-all-done = f32[4,16,72,128]{3,2,1,0:T(8,128)S(1)} async-done(((f32[4,16,72,128]{3,2,1,0:T(8,128)}), f32[4,16,72,128]{3,2,1,0:T(8,128)S(1)}, u32[]{:S(2)}, u32[]{:S(2)}) %all-to-all-start) | async-done | bytes 2359328 | tf_op jit(solution)/shard_map/all_to_all | solution.py:67
  49.1 1.4 copy-done.1
  50.5 2.6 %reverse_select_fusion = f32[4,16,72,128]{3,2,1,0:T(8,128)S(1)} fusion(f32[4,16,72,128]{3,2,1,0:T(8,128)} %copy-done.1, pred[]{:T(512)S(6)} %xor.3), kind=kLoop, calls=%fused_computation.16 | loop fusion | flops 589824 | bytes 4718593 | tf_op jit(solution)/shard_map/jit(_where)/select_n | solution.py:70
  53.2 0.3 exponential_reduce_fusion
  53.5 1.0 fusion.27
  54.7 3.9 %collective-permute-start = (f32[16,72,128]{2,1,0:T(8,128)S(1)}, f32[16,72,128]{2,1,0:T(8,128)S(1)}, u32[]{:S(2)}, u32[]{:S(2)}) collective-permute-start(f32[16,72,128]{2,1,0:T(8,128)S(1)} %pad_maximum_fusion.2), channel_id=1, source_target_pairs={{0,4},{1,5},{4,8},{5,9},{6,2},{7,3},{8,12},{9,13},{10,6},{11,7},{1... | collective-permute-start | bytes 1769480 | tf_op jit(solution)/shard_map/ppermute | solution.py:90
  58.5 9.7 %collective-permute-done = f32[16,72,128]{2,1,0:T(8,128)S(1)} collective-permute-done((f32[16,72,128]{2,1,0:T(8,128)S(1)}, f32[16,72,128]{2,1,0:T(8,128)S(1)}, u32[]{:S(2)}, u32[]{:S(2)}) %collective-permute-start) | collective-permute-done | bytes 589856 | tf_op jit(solution)/shard_map/ppermute | solution.py:90
  68.2 0.8 copy-done.4
  69.1 1.2 multiply_add_fusion.1
  70.4 0.9 pad_maximum_fusion.3
  71.3 7.5 %collective-permute-start.1 = (f32[16,72,128]{2,1,0:T(8,128)}, f32[16,72,128]{2,1,0:T(8,128)S(1)}, u32[]{:S(2)}, u32[]{:S(2)}) collective-permute-start(f32[16,72,128]{2,1,0:T(8,128)} %pad_maximum_fusion.3), channel_id=1, source_target_pairs={{0,8},{1,9},{4,12},{5,13},{8,16},{9,17},{10,2},{11,3},{12,20},{13,... | collective-permute-start | bytes 1769480 | tf_op jit(solution)/shard_map/ppermute | solution.py:90
  78.8 16.9 %all-gather.5.cloned.1.call-done = bf16[16384,32]{0,1:T(8,128)(2,1)} async-done(((bf16[2048,32]{0,1:T(8,128)(2,1)}), bf16[16384,32]{0,1:T(8,128)(2,1)}) %all-gather.5.cloned.1.call-update) | async-done | bytes 1048592 | tf_op jit(solution)/shard_map/all_gather | solution.py:106
  95.7 2.8 %copy.122 = bf16[4,8,8,2048]{3,2,1,0:T(8,128)(2,1)} copy(bf16[4,8,8,2048]{3,1,2,0:T(8,128)(2,1)} %bitcast.177) | data formatting | bytes 2097152
  98.6 0.5 exponential_bitcast_fusion.2
  99.2 0.2 copy-done.6
  99.6 0.9 pad_maximum_fusion.4
  100.5 7.7 %collective-permute-start.2 = (f32[16,72,128]{2,1,0:T(8,128)}, f32[16,72,128]{2,1,0:T(8,128)}, u32[]{:S(2)}, u32[]{:S(2)}) collective-permute-start(f32[16,72,128]{2,1,0:T(8,128)} %pad_maximum_fusion.4), channel_id=1, source_target_pairs={{0,16},{1,17},{4,20},{5,21},{8,24},{9,25},{12,28},{13,29},{18,2},{... | collective-permute-start | bytes 1769480 | tf_op jit(solution)/shard_map/ppermute | solution.py:90
  108.2 1.1 copy.120
  109.3 5.8 %collective-permute-done.2 = f32[16,72,128]{2,1,0:T(8,128)} collective-permute-done((f32[16,72,128]{2,1,0:T(8,128)}, f32[16,72,128]{2,1,0:T(8,128)}, u32[]{:S(2)}, u32[]{:S(2)}) %collective-permute-start.2) | collective-permute-done | bytes 589856 | tf_op jit(solution)/shard_map/ppermute | solution.py:90
  115.2 1.4 add_bitcast_fusion.2
  116.6 0.2 add_bitcast_fusion.1
  116.8 0.2 pad_maximum_fusion.1
  117.1 1.5 reverse_select_fusion.1
  118.6 21.0 %all-to-all-start.1 = ((f32[4,16,64,128]{3,2,1,0:T(8,128)}), f32[4,16,64,128]{3,2,1,0:T(8,128)S(1)}, u32[]{:S(2)}, u32[]{:S(2)}) async-start(f32[4,16,64,128]{3,2,1,0:T(8,128)} %reverse_select_fusion.1), calls=%async_computation.1 | async-start | bytes 4194304 | tf_op jit(solution)/shard_map/all_to_all | solution.py:97
  139.6 1.3 copy.109
  140.9 0.6 dynamic_slice.23
  141.5 0.6 iota_compare_fusion.1
  142.3 4.5 %all-gather.7.cloned.1.call-done = bf16[8,4096,32]{1,2,0:T(8,128)(2,1)} async-done(((bf16[8,1024,32]{1,2,0:T(8,128)(2,1)}), bf16[8,4096,32]{1,2,0:T(8,128)(2,1)}) %all-gather.7.cloned.1.call-update) | async-done | bytes 2097168 | tf_op jit(solution)/shard_map/all_gather | solution.py:108
  146.8 3.2 %copy.125 = bf16[8,4,4,8,1024]{4,3,1,2,0:T(8,128)(2,1)} copy(bf16[8,4,4,8,1024]{4,3,2,1,0:T(8,128)(2,1)} %bitcast.173) | data formatting | bytes 4194304 | tf_op jit(solution)/shard_map/all_gather | solution.py:108
  149.9 1.9 collective-permute-start.3
  151.9 14.9 %all-to-all-done.1 = f32[4,16,64,128]{3,2,1,0:T(8,128)S(1)} async-done(((f32[4,16,64,128]{3,2,1,0:T(8,128)}), f32[4,16,64,128]{3,2,1,0:T(8,128)S(1)}, u32[]{:S(2)}, u32[]{:S(2)}) %all-to-all-start.1) | async-done | bytes 2097184 | tf_op jit(solution)/shard_map/all_to_all | solution.py:97
  166.9 0.4 maximum_select_fusion.1
  167.4 1.1 copy-done.7
  168.5 0.6 fusion.15
  169.2 0.8 multiply_reduce_fusion
  170.2 0.3 copy.110
  170.5 0.2 copy-done.10
  170.8 2.3 %fusion.33 = f32[128,8,4,32]{0,3,2,1:T(8,128)S(1)} fusion(bf16[128,2048]{1,0:T(8,128)(2,1)S(1)} %multiply_convert_fusion.6, s32[]{:T(128)S(6)} %select_n.86, bf16[8,4,4,8,1024]{4,3,2,1,0:T(8,128)(2,1)} %bitcast.174), kind=kOutput, calls=%fused_computation.72 | convolution fusion | flops 268435456 | bytes 2883588 | tf_op jit(solution)/shard_map/tr,zxrc->tzxc/dot_general | solution.py:120
  173.1 2.3 %fusion.17 = bf16[128,8,4,32]{0,3,2,1:T(8,128)(2,1)S(1)} fusion(f32[128,8,4,32]{0,3,2,1:T(8,128)S(1)} %fusion.33, bf16[8,4,1024,32]{2,3,1,0:T(8,128)(2,1)} %collective-permute-done.3, bf16[128,2048]{1,0:T(8,128)(2,1)S(1)} %multiply_convert_fusion.6, s32[]{:T(128)S(6)} %select_n.87), kind=kOutput, calls=%fused_computation.35 | convolution fusion | flops 268697600 | bytes 3145732 | tf_op jit(solution)/shard_map/tr,zxrc->tzxc/dot_general | solution.py:121
  175.6 8.9 %collective-permute-start.4 = (bf16[128,1024]{1,0:T(8,128)(2,1)S(1)}, bf16[128,1024]{1,0:T(8,128)(2,1)S(1)}, u32[]{:S(2)}, u32[]{:S(2)}) collective-permute-start(bf16[128,1024]{1,0:T(8,128)(2,1)S(1)} %copy.114), channel_id=1, source_target_pairs={{28,32},{32,28},{60,64},{64,60},{92,96},{96,92},{124,128},{128,124... | collective-permute-start | bytes 786440 | tf_op jit(solution)/shard_map/ppermute | solution.py:210
  184.6 9.0 %collective-permute-done.4 = bf16[128,1024]{1,0:T(8,128)(2,1)S(1)} collective-permute-done((bf16[128,1024]{1,0:T(8,128)(2,1)S(1)}, bf16[128,1024]{1,0:T(8,128)(2,1)S(1)}, u32[]{:S(2)}, u32[]{:S(2)}) %collective-permute-start.4) | collective-permute-done | bytes 262176 | tf_op jit(solution)/shard_map/ppermute | solution.py:210
  193.6 0.9 fusion.31
  (92 shorter events, 2.8 us)
Async XLA Ops:
  6.5 14.3 %copy-start = (bf16[1,128,128]{2,1,0:T(8,128)(2,1)S(1)}, bf16[1,128,128]{2,1,0:T(8,128)(2,1)}, u32[]{:S(2)}) copy-start(bf16[1,128,128]{2,1,0:T(8,128)(2,1)} %param.14) | copy-start | bytes 98308
  15.5 5.3 %copy-start.9 = (bf16[1,128,128]{2,1,0:T(8,128)(2,1)S(1)}, bf16[1,128,128]{2,1,0:T(8,128)(2,1)}, u32[]{:S(2)}) copy-start(bf16[1,128,128]{2,1,0:T(8,128)(2,1)} %param.13) | copy-start | bytes 98308
  15.5 33.6 %all-to-all-start = ((f32[4,16,72,128]{3,2,1,0:T(8,128)}), f32[4,16,72,128]{3,2,1,0:T(8,128)S(1)}, u32[]{:S(2)}, u32[]{:S(2)}) async-start(f32[4,16,72,128]{3,2,1,0:T(8,128)} %maximum_select_fusion), calls=%async_computation | async-start | bytes 4718592 | tf_op jit(solution)/shard_map/all_to_all | solution.py:67
  20.0 75.8 %all-gather.5.cloned.1.call-start = ((), (), s32[]{:S(2)}) async-start(), calls=%async_computation.2 | async-start | bytes 1179648 | tf_op jit(solution)/shard_map/all_gather | solution.py:106
  20.7 126.1 %all-gather.7.cloned.1.call-start = ((), (), s32[]{:S(2)}) async-start(), calls=%async_computation.3 | async-start | bytes 2621440 | tf_op jit(solution)/shard_map/all_gather | solution.py:108
  49.1 1.4 copy-start.1
  53.5 1.2 copy-start.11
  53.5 1.2 copy-start.15
  54.7 13.6 %collective-permute-start = (f32[16,72,128]{2,1,0:T(8,128)S(1)}, f32[16,72,128]{2,1,0:T(8,128)S(1)}, u32[]{:S(2)}, u32[]{:S(2)}) collective-permute-start(f32[16,72,128]{2,1,0:T(8,128)S(1)} %pad_maximum_fusion.2), channel_id=1, source_target_pairs={{0,4},{1,5},{4,8},{5,9},{6,2},{7,3},{8,12},{9,13},{10,6},{11,7},{1... | collective-permute-start | bytes 1769480 | tf_op jit(solution)/shard_map/ppermute | solution.py:90
  68.2 0.8 copy-start.4
  71.3 27.3 %collective-permute-start.1 = (f32[16,72,128]{2,1,0:T(8,128)}, f32[16,72,128]{2,1,0:T(8,128)S(1)}, u32[]{:S(2)}, u32[]{:S(2)}) collective-permute-start(f32[16,72,128]{2,1,0:T(8,128)} %pad_maximum_fusion.3), channel_id=1, source_target_pairs={{0,8},{1,9},{4,12},{5,13},{8,16},{9,17},{10,2},{11,3},{12,20},{13,... | collective-permute-start | bytes 1769480 | tf_op jit(solution)/shard_map/ppermute | solution.py:90
  98.5 0.8 copy-start.6
  98.6 9.5 %copy-start.2 = (bf16[4,8,8,2048]{3,2,1,0:T(8,128)(2,1)S(1)}, bf16[4,8,8,2048]{3,2,1,0:T(8,128)(2,1)}, u32[]{:S(2)}) copy-start(bf16[4,8,8,2048]{3,2,1,0:T(8,128)(2,1)} %copy.122) | copy-start | bytes 3145732
  99.5 15.7 %copy-start.5 = (f32[16,72,128]{2,1,0:T(8,128)S(1)}, f32[16,72,128]{2,1,0:T(8,128)}, u32[]{:S(2)}) copy-start(f32[16,72,128]{2,1,0:T(8,128)} %copy-done.4) | copy-start | bytes 1769476
  99.5 15.7 %copy-start.12 = (f32[16]{0:T(128)S(1)}, f32[16]{0:T(128)}, u32[]{:S(2)}) copy-start(f32[16]{0:T(128)} %copy-done.11) | copy-start | bytes 196
  99.5 15.7 %copy-start.13 = (f32[16]{0:T(128)S(1)}, f32[16]{0:T(128)}, u32[]{:S(2)}) copy-start(f32[16]{0:T(128)} %get-tuple-element.108) | copy-start | bytes 196
  99.5 15.7 %copy-start.14 = (f32[16]{0:T(128)S(1)}, f32[16]{0:T(128)}, u32[]{:S(2)}) copy-start(f32[16]{0:T(128)} %get-tuple-element.113) | copy-start | bytes 196
  99.5 15.7 %copy-start.16 = (f32[16]{0:T(128)S(1)}, f32[16]{0:T(128)}, u32[]{:S(2)}) copy-start(f32[16]{0:T(128)} %copy-done.15) | copy-start | bytes 196
  100.5 14.7 %collective-permute-start.2 = (f32[16,72,128]{2,1,0:T(8,128)}, f32[16,72,128]{2,1,0:T(8,128)}, u32[]{:S(2)}, u32[]{:S(2)}) collective-permute-start(f32[16,72,128]{2,1,0:T(8,128)} %pad_maximum_fusion.4), channel_id=1, source_target_pairs={{0,16},{1,17},{4,20},{5,21},{8,24},{9,25},{12,28},{13,29},{18,2},{... | collective-permute-start | bytes 1769480 | tf_op jit(solution)/shard_map/ppermute | solution.py:90
  109.3 7.3 %copy-start.3 = (f32[16,64,128]{2,1,0:T(8,128)S(1)}, f32[16,64,128]{2,1,0:T(8,128)}, u32[]{:S(2)}) copy-start(f32[16,64,128]{2,1,0:T(8,128)} %get-tuple-element.89) | copy-start | bytes 1572868
  118.6 21.0 %copy-start.8 = (f32[128,32]{1,0:T(8,128)S(1)}, f32[128,32]{1,0:T(8,128)}, u32[]{:S(2)}) copy-start(f32[128,32]{1,0:T(8,128)} %get-tuple-element.100) | copy-start | bytes 49156
  118.6 22.3 %copy-start.17 = (s32[16]{0:T(128)S(1)}, s32[16]{0:T(128)}, u32[]{:S(2)}) copy-start(s32[16]{0:T(128)} %param.19) | copy-start | bytes 196
  118.6 48.1 %all-to-all-start.1 = ((f32[4,16,64,128]{3,2,1,0:T(8,128)}), f32[4,16,64,128]{3,2,1,0:T(8,128)S(1)}, u32[]{:S(2)}, u32[]{:S(2)}) async-start(f32[4,16,64,128]{3,2,1,0:T(8,128)} %reverse_select_fusion.1), calls=%async_computation.1 | async-start | bytes 4194304 | tf_op jit(solution)/shard_map/all_to_all | solution.py:97
  149.9 23.2 %collective-permute-start.3 = (bf16[8,4,1024,32]{2,3,1,0:T(8,128)(2,1)}, bf16[8,4,1024,32]{2,3,1,0:T(8,128)(2,1)}, u32[]{:S(2)}, u32[]{:S(2)}) collective-permute-start(bf16[8,4,1024,32]{2,3,1,0:T(8,128)(2,1)} %bitcast.156), channel_id=1, source_target_pairs={{0,32},{32,0},{64,96},{96,64},{128,160},{160,128},{192,224},{224,1... | collective-permute-start | bytes 6291464 | tf_op jit(solution)/shard_map/ppermute | solution.py:111
  167.3 1.2 copy-start.7
  170.0 0.7 copy-start.10
  175.6 18.0 %collective-permute-start.4 = (bf16[128,1024]{1,0:T(8,128)(2,1)S(1)}, bf16[128,1024]{1,0:T(8,128)(2,1)S(1)}, u32[]{:S(2)}, u32[]{:S(2)}) collective-permute-start(bf16[128,1024]{1,0:T(8,128)(2,1)S(1)} %copy.114), channel_id=1, source_target_pairs={{28,32},{32,28},{60,64},{64,60},{92,96},{96,92},{124,128},{128,124... | collective-permute-start | bytes 786440 | tf_op jit(solution)/shard_map/ppermute | solution.py:210
Sparse Core Ops, SparseCore 0:
  22.9 72.7 all-gather.4
  109.5 37.2 all-gather.6

commit v11 on v10

--- a/solution.py
+++ b/solution.py
@@ -56,7 +56,7 @@
     return jnp.concatenate([states, rows], axis=-2)
 
 
-def scan_states(log_fwd, log_bwd, fresh_fwd, fresh_bwd, hold):
+def scan_states(log_fwd, log_bwd, fresh_fwd, fresh_bwd, hold, anchor):
     packed = pack(jnp.stack([log_fwd, log_bwd]), jnp.stack([fresh_fwd, fresh_bwd]))
     parts = lax.axis_size("x")
     per_part = 2 * H // parts
@@ -87,7 +87,10 @@
                     to = z - d if (x >= half) != (w % 2 == 1) else z + d
                     if 0 <= to < rows:
                         pairs.append(((w * rows + z) * parts + x, (w * rows + to) * parts + x))
-        got = split_packed(lax.ppermute(pack(*total), ("win", "z", "x"), pairs))
+        moved = lax.ppermute(pack(*total), ("win", "z", "x"), pairs)
+        if d * 2 >= rows:
+            moved, anchor = lax.optimization_barrier((moved, anchor))
+        got = split_packed(moved)
         entering = combine(got, entering)
         if d * 2 < rows:
             total = combine(got, total)
@@ -97,13 +100,12 @@
     back = lax.all_to_all(out, "x", 0, 0, tiled=True)
     back = jnp.where(odd, jnp.concatenate([back[half:], back[:half]]), back)
     back = back.reshape(2, H, P_SIZE, N)
-    return back[0], back[1], hold
-
-
-def gather_weight(output_weight):
+    return back[0], back[1], hold, anchor
+
+
+def gather_weight(column):
     half = lax.axis_index("win") % 2
-    half_rows = output_weight.shape[0] // 2
-    column = lax.all_gather(output_weight, "z", axis=0)
+    half_rows = column.shape[1] // 2
     mine = lax.dynamic_slice_in_dim(column, half * half_rows, half_rows, axis=1)
     row = lax.all_gather(mine, "x", axis=1)
     wins = lax.axis_size("win")
@@ -181,8 +183,9 @@
     grouped_frames = head_frames.reshape(frame_count, group_count, 4, P_SIZE).transpose(1, 0, 2, 3)
     local_groups = lax.map(group_mix, (grouped_fwd, grouped_bwd, grouped_frames))
     local_part = local_groups.transpose(1, 0, 2, 3).reshape(frame_count, H, P_SIZE)
-    state_fwd, state_bwd, local_part = scan_states(
-        running_fwd[-1], running_bwd[0], fresh_fwd, fresh_bwd, local_part
+    column = lax.all_gather(output_weight, "z", axis=0)
+    state_fwd, state_bwd, local_part, column = scan_states(
+        running_fwd[-1], running_bwd[0], fresh_fwd, fresh_bwd, local_part, column
     )
     c_float = c_rows.astype(jnp.float32)
     carried_fwd = jnp.exp(running_fwd)[:, :, None] * jnp.einsum(
@@ -199,7 +202,7 @@
     normed = (
         (gated_rows * inverse_rms).reshape(frame_count, H * P_SIZE) * gated_norm_gain[None, :]
     ).astype(jnp.bfloat16)
-    projected_rows = project(normed, gather_weight(output_weight)).astype(jnp.bfloat16)
+    projected_rows = project(normed, gather_weight(column)).astype(jnp.bfloat16)
     window_index = lax.axis_index("win")
     window_total = lax.axis_size("win")
     row_index = lax.axis_index("z")

time: 203 us -> 229 us (1.13)
  waiting for transfers between devices: 81.5 us -> 102 us
  starting transfers between devices: 55.3 us -> 59.3 us
    all_to_all x1, waiting for transfers between devices: 14.9 us -> 34.3 us  [scan_states(): back = lax.all_to_all(out, 'x', 0, 0, tiled=True)]
    ppermute x3, starting transfers between devices: 19.1 us -> 30.1 us  [scan_states(): moved = lax.ppermute(pack(*total), ('win', 'z', 'x'), pairs)]
    all_to_all x1, starting transfers between devices: 21 us -> 13.8 us  [scan_states(): back = lax.all_to_all(out, 'x', 0, 0, tiled=True)]
    unnamed x41 -> x32, local copies, waits for them, and re-layouts: 9.18 us -> 6.55 us
    all_gather x1, waiting for transfers between devices: 4.53 us -> 2.01 us  [gather_weight(): row = lax.all_gather(mine, 'x', axis=1)]
    all_gather x1, waiting for transfers between devices: 16.9 us -> 19.3 us  [per_device(): column = lax.all_gather(output_weight, 'z', axis=0)]
  transfers between devices with their start and end apart: 9 -> 9, of which waited for: 7 -> 7; matrix products, arithmetic and copies ran while one was open for 16% -> 12% of each run, Pallas kernels for 0% -> 0%
where the time goes in v11:
time: 229 us; the launch traced here: 228 us
  waiting for transfers between devices  102 us (45%)
  starting transfers between devices  59.3 us (26%)
  other arithmetic  20.6 us (9%)
  matrix products  15.9 us (7%)
  local copies, waits for them, and re-layouts  15.7 us (7%)
  between operations  13.8 us (6%)
    all_to_all x1, waiting for transfers between devices, scan_states(): back = lax.all_to_all(out, 'x', 0, 0, tiled=True)  34.3 us
    ppermute x3, starting transfers between devices, scan_states(): moved = lax.ppermute(pack(*total), ('win', 'z', 'x'), pairs)  30.1 us
    all_to_all x1, waiting for transfers between devices, scan_states(): mine = lax.all_to_all(send, 'x', 0, 0, tiled=True)  20.7 us
    all_gather x1, waiting for transfers between devices, per_device(): column = lax.all_gather(output_weight, 'z', axis=0)  19.3 us
    ppermute x3, waiting for transfers between devices, scan_states(): moved = lax.ppermute(pack(*total), ('win', 'z', 'x'), pairs)  17.2 us
    all_to_all x1, starting transfers between devices, scan_states(): back = lax.all_to_all(out, 'x', 0, 0, tiled=True)  13.8 us
    ppermute x1, starting transfers between devices, per_device(): partner = lax.ppermute(projected_rows, ('win', 'z'), pairs)  8.99 us
    ppermute x1, waiting for transfers between devices, per_device(): partner = lax.ppermute(projected_rows, ('win', 'z'), pairs)  8.65 us
  transfers between devices with their start and end apart: 9, of which 7 were waited for; matrix products, arithmetic and copies ran while one was open for 12% of the time, Pallas kernels for 0%

profile of v11, /device:TPU:24, one launch (start us, length us, event | category | flops | bytes accessed | tf_op | source)
XLA Modules:
  0.0 227.6 jit_solution(5813146741264229512)
XLA Ops:
  6.5 0.8 compare_select_fusion
  7.3 0.7 multiply_bitcast_fusion
  8.3 0.2 reduce_window_sum.17
  8.7 0.7 fusion.50
  9.5 1.3 copy.101
  10.8 0.8 bitcast_convert_fusion
  11.7 0.8 convolution_bitcast_fusion.4
  12.5 0.8 convolution_bitcast_fusion.3
  13.5 0.2 pad_maximum_fusion
  13.9 1.7 maximum_select_fusion
  15.5 4.4 %all-to-all-start = ((f32[4,16,72,128]{3,2,1,0:T(8,128)}), f32[4,16,72,128]{3,2,1,0:T(8,128)S(1)}, u32[]{:S(2)}, u32[]{:S(2)}) async-start(f32[4,16,72,128]{3,2,1,0:T(8,128)} %maximum_select_fusion), calls=%async_computation | async-start | bytes 4718592 | tf_op jit(solution)/shard_map/all_to_all | solution.py:67
  20.2 8.3 %while.11 = (s32[]{:T(128)}, f32[8,128,4,64]{1,3,2,0:T(8,128)}, bf16[8,128,4,64]{1,3,2,0:T(8,128)(2,1)S(1)}, f32[128,128]{1,0:T(8,128)S(1)}, f32[8,4,128]{2,1,0:...) while((s32[]{:T(128)}, f32[8,128,4,64]{1,3,2,0:T(8,128)}, ...), condition=%wide.region_4.5_spmd.clone, body=%wide.region_3.4_spmd.clone.sunk | while | flops 8732674 | bytes 312401 | solution.py:184
  20.2 1.0 fusion.60
  21.3 1.0 fusion.60
  22.3 1.0 fusion.60
  23.3 1.0 fusion.60
  24.3 1.0 fusion.60
  25.4 1.0 fusion.60
  26.4 1.0 fusion.60
  27.4 1.0 fusion.60
  28.4 20.7 %all-to-all-done = f32[4,16,72,128]{3,2,1,0:T(8,128)S(1)} async-done(((f32[4,16,72,128]{3,2,1,0:T(8,128)}), f32[4,16,72,128]{3,2,1,0:T(8,128)S(1)}, u32[]{:S(2)}, u32[]{:S(2)}) %all-to-all-start) | async-done | bytes 2359328 | tf_op jit(solution)/shard_map/all_to_all | solution.py:67
  49.1 1.4 copy-done.1
  50.5 2.6 %reverse_select_fusion = f32[4,16,72,128]{3,2,1,0:T(8,128)S(1)} fusion(f32[4,16,72,128]{3,2,1,0:T(8,128)} %copy-done.1, pred[]{:T(512)S(6)} %xor.3), kind=kLoop, calls=%fused_computation.16 | loop fusion | flops 589824 | bytes 4718593 | tf_op jit(solution)/shard_map/jit(_where)/select_n | solution.py:70
  53.2 0.3 exponential_reduce_fusion
  53.5 1.0 fusion.26
  54.6 0.9 pad_maximum_fusion.2
  55.5 3.8 %collective-permute-start = (f32[16,72,128]{2,1,0:T(8,128)}, f32[16,72,128]{2,1,0:T(8,128)S(1)}, u32[]{:S(2)}, u32[]{:S(2)}) collective-permute-start(f32[16,72,128]{2,1,0:T(8,128)} %pad_maximum_fusion.2), channel_id=1, source_target_pairs={{0,4},{1,5},{4,8},{5,9},{6,2},{7,3},{8,12},{9,13},{10,6},{11,7},{1... | collective-permute-start | bytes 1769480 | tf_op jit(solution)/shard_map/ppermute | solution.py:90
  59.4 0.6 exp.111
  60.0 7.0 %collective-permute-done = f32[16,72,128]{2,1,0:T(8,128)S(1)} collective-permute-done((f32[16,72,128]{2,1,0:T(8,128)}, f32[16,72,128]{2,1,0:T(8,128)S(1)}, u32[]{:S(2)}, u32[]{:S(2)}) %collective-permute-start) | collective-permute-done | bytes 589856 | tf_op jit(solution)/shard_map/ppermute | solution.py:90
  67.1 0.7 copy-done.4
  67.8 1.2 multiply_add_fusion.1
  69.1 5.7 %collective-permute-start.1 = (f32[16,72,128]{2,1,0:T(8,128)S(1)}, f32[16,72,128]{2,1,0:T(8,128)S(1)}, u32[]{:S(2)}, u32[]{:S(2)}) collective-permute-start(f32[16,72,128]{2,1,0:T(8,128)S(1)} %pad_maximum_fusion.3), channel_id=1, source_target_pairs={{0,8},{1,9},{4,12},{5,13},{8,16},{9,17},{10,2},{11,3},{12,20},{13,... | collective-permute-start | bytes 1769480 | tf_op jit(solution)/shard_map/ppermute | solution.py:90
  74.8 10.2 %collective-permute-done.1 = f32[16,72,128]{2,1,0:T(8,128)S(1)} collective-permute-done((f32[16,72,128]{2,1,0:T(8,128)S(1)}, f32[16,72,128]{2,1,0:T(8,128)S(1)}, u32[]{:S(2)}, u32[]{:S(2)}) %collective-permute-start.1) | collective-permute-done | bytes 589856 | tf_op jit(solution)/shard_map/ppermute | solution.py:90
  85.0 0.8 copy-done.6
  85.9 1.2 multiply_add_fusion
  87.1 0.9 pad_maximum_fusion.4
  88.0 20.5 %collective-permute-start.2 = (f32[16,72,128]{2,1,0:T(8,128)}, f32[16,72,128]{2,1,0:T(8,128)}, u32[]{:S(2)}, u32[]{:S(2)}) collective-permute-start(f32[16,72,128]{2,1,0:T(8,128)} %pad_maximum_fusion.4), channel_id=1, source_target_pairs={{0,16},{1,17},{4,20},{5,21},{8,24},{9,25},{12,28},{13,29},{18,2},{... | collective-permute-start | bytes 1769480 | tf_op jit(solution)/shard_map/ppermute | solution.py:90
  108.6 19.3 %all-gather.5.cloned.1.call-done = bf16[16384,32]{0,1:T(8,128)(2,1)} async-done(((bf16[2048,32]{0,1:T(8,128)(2,1)}), bf16[16384,32]{0,1:T(8,128)(2,1)}) %all-gather.5.cloned.1.call-update) | async-done | bytes 1048592 | tf_op jit(solution)/shard_map/all_gather | solution.py:186
  127.9 1.8 copy.121
  129.7 0.6 copy.111
  130.3 0.9 constant_dynamic-slice_fusion
  131.2 1.5 add_bitcast_fusion.2
  132.7 0.2 add_bitcast_fusion.1
  132.9 0.2 pad_maximum_fusion.1
  133.2 1.5 reverse_select_fusion.1
  134.7 13.8 %all-to-all-start.1 = ((f32[4,16,64,128]{3,2,1,0:T(8,128)}), f32[4,16,64,128]{3,2,1,0:T(8,128)S(1)}, u32[]{:S(2)}, u32[]{:S(2)}) async-start(f32[4,16,64,128]{3,2,1,0:T(8,128)} %reverse_select_fusion.1), calls=%async_computation.1 | async-start | bytes 4194304 | tf_op jit(solution)/shard_map/all_to_all | solution.py:100
  148.5 1.3 copy.109
  149.8 0.6 dynamic_slice.23
  150.4 0.6 iota_compare_fusion.1
  151.1 34.3 %all-to-all-done.1 = f32[4,16,64,128]{3,2,1,0:T(8,128)S(1)} async-done(((f32[4,16,64,128]{3,2,1,0:T(8,128)}), f32[4,16,64,128]{3,2,1,0:T(8,128)S(1)}, u32[]{:S(2)}, u32[]{:S(2)}) %all-to-all-start.1) | async-done | bytes 2097184 | tf_op jit(solution)/shard_map/all_to_all | solution.py:100
  185.5 1.7 maximum_select_fusion.1
  187.3 2.0 all-gather.7.cloned.1.call-done
  189.3 3.3 %copy.124 = bf16[8,4,4,8,1024]{4,3,1,2,0:T(8,128)(2,1)} copy(bf16[8,4,4,8,1024]{4,3,2,1,0:T(8,128)(2,1)} %bitcast.173) | data formatting | bytes 4194304 | tf_op jit(solution)/shard_map/all_gather | solution.py:110
  192.6 2.0 collective-permute-start.3
  194.7 0.2 fusion.48
  194.9 0.6 fusion.15
  195.6 0.8 multiply_reduce_fusion
  196.6 0.3 copy.110
  196.9 0.2 copy-done.10
  197.2 2.3 %fusion.32 = f32[128,8,4,32]{0,3,2,1:T(8,128)S(1)} fusion(bf16[128,2048]{1,0:T(8,128)(2,1)S(1)} %multiply_convert_fusion.6, s32[]{:T(128)S(6)} %select_n.86, bf16[8,4,4,8,1024]{4,3,2,1,0:T(8,128)(2,1)} %bitcast.174), kind=kOutput, calls=%fused_computation.71 | convolution fusion | flops 268435456 | bytes 2883588 | tf_op jit(solution)/shard_map/tr,zxrc->tzxc/dot_general | solution.py:122
  199.5 2.3 %fusion.17 = bf16[128,8,4,32]{0,3,2,1:T(8,128)(2,1)S(1)} fusion(f32[128,8,4,32]{0,3,2,1:T(8,128)S(1)} %fusion.32, bf16[8,4,1024,32]{2,3,1,0:T(8,128)(2,1)} %collective-permute-done.3, bf16[128,2048]{1,0:T(8,128)(2,1)S(1)} %multiply_convert_fusion.6, s32[]{:T(128)S(6)} %select_n.87), kind=kOutput, calls=%fused_computation.35 | convolution fusion | flops 268697600 | bytes 3145732 | tf_op jit(solution)/shard_map/tr,zxrc->tzxc/dot_general | solution.py:123
  202.0 9.0 %collective-permute-start.4 = (bf16[128,1024]{1,0:T(8,128)(2,1)S(1)}, bf16[128,1024]{1,0:T(8,128)(2,1)S(1)}, u32[]{:S(2)}, u32[]{:S(2)}) collective-permute-start(bf16[128,1024]{1,0:T(8,128)(2,1)S(1)} %copy.114), channel_id=1, source_target_pairs={{28,32},{32,28},{60,64},{64,60},{92,96},{96,92},{124,128},{128,124... | collective-permute-start | bytes 786440 | tf_op jit(solution)/shard_map/ppermute | solution.py:213
  211.1 8.6 %collective-permute-done.4 = bf16[128,1024]{1,0:T(8,128)(2,1)S(1)} collective-permute-done((bf16[128,1024]{1,0:T(8,128)(2,1)S(1)}, bf16[128,1024]{1,0:T(8,128)(2,1)S(1)}, u32[]{:S(2)}, u32[]{:S(2)}) %collective-permute-start.4) | collective-permute-done | bytes 262176 | tf_op jit(solution)/shard_map/ppermute | solution.py:213
  219.8 0.9 fusion.30
  (84 shorter events, 2.7 us)
Async XLA Ops:
  6.5 13.5 %copy-start = (bf16[1,128,128]{2,1,0:T(8,128)(2,1)S(1)}, bf16[1,128,128]{2,1,0:T(8,128)(2,1)}, u32[]{:S(2)}) copy-start(bf16[1,128,128]{2,1,0:T(8,128)(2,1)} %param.14) | copy-start | bytes 98308
  15.5 4.5 %copy-start.9 = (bf16[1,128,128]{2,1,0:T(8,128)(2,1)S(1)}, bf16[1,128,128]{2,1,0:T(8,128)(2,1)}, u32[]{:S(2)}) copy-start(bf16[1,128,128]{2,1,0:T(8,128)(2,1)} %param.13) | copy-start | bytes 98308
  15.5 33.6 %all-to-all-start = ((f32[4,16,72,128]{3,2,1,0:T(8,128)}), f32[4,16,72,128]{3,2,1,0:T(8,128)S(1)}, u32[]{:S(2)}, u32[]{:S(2)}) async-start(f32[4,16,72,128]{3,2,1,0:T(8,128)} %maximum_select_fusion), calls=%async_computation | async-start | bytes 4718592 | tf_op jit(solution)/shard_map/all_to_all | solution.py:67
  20.0 107.9 %all-gather.5.cloned.1.call-start = ((), (), s32[]{:S(2)}) async-start(), calls=%async_computation.2 | async-start | bytes 1179648 | tf_op jit(solution)/shard_map/all_gather | solution.py:186
  49.1 1.4 copy-start.1
  53.5 1.1 copy-start.11
  55.5 11.5 %collective-permute-start = (f32[16,72,128]{2,1,0:T(8,128)}, f32[16,72,128]{2,1,0:T(8,128)S(1)}, u32[]{:S(2)}, u32[]{:S(2)}) collective-permute-start(f32[16,72,128]{2,1,0:T(8,128)} %pad_maximum_fusion.2), channel_id=1, source_target_pairs={{0,4},{1,5},{4,8},{5,9},{6,2},{7,3},{8,12},{9,13},{10,6},{11,7},{1... | collective-permute-start | bytes 1769480 | tf_op jit(solution)/shard_map/ppermute | solution.py:90
  59.3 130.0 %all-gather.7.cloned.1.call-start = ((), (), s32[]{:S(2)}) async-start(), calls=%async_computation.3 | async-start | bytes 2621440 | tf_op jit(solution)/shard_map/all_gather | solution.py:110
  67.0 0.8 copy-start.4
  69.1 15.8 %collective-permute-start.1 = (f32[16,72,128]{2,1,0:T(8,128)S(1)}, f32[16,72,128]{2,1,0:T(8,128)S(1)}, u32[]{:S(2)}, u32[]{:S(2)}) collective-permute-start(f32[16,72,128]{2,1,0:T(8,128)S(1)} %pad_maximum_fusion.3), channel_id=1, source_target_pairs={{0,8},{1,9},{4,12},{5,13},{8,16},{9,17},{10,2},{11,3},{12,20},{13,... | collective-permute-start | bytes 1769480 | tf_op jit(solution)/shard_map/ppermute | solution.py:90
  84.9 0.8 copy-start.6
  88.0 41.7 %collective-permute-start.2 = (f32[16,72,128]{2,1,0:T(8,128)}, f32[16,72,128]{2,1,0:T(8,128)}, u32[]{:S(2)}, u32[]{:S(2)}) collective-permute-start(f32[16,72,128]{2,1,0:T(8,128)} %pad_maximum_fusion.4), channel_id=1, source_target_pairs={{0,16},{1,17},{4,20},{5,21},{8,24},{9,25},{12,28},{13,29},{18,2},{... | collective-permute-start | bytes 1769480 | tf_op jit(solution)/shard_map/ppermute | solution.py:90
  129.7 1.5 copy-start.5
  129.7 1.5 copy-start.12
  131.2 1.5 copy-start.3
  134.7 13.8 %copy-start.8 = (f32[128,32]{1,0:T(8,128)S(1)}, f32[128,32]{1,0:T(8,128)}, u32[]{:S(2)}) copy-start(f32[128,32]{1,0:T(8,128)} %get-tuple-element.104) | copy-start | bytes 49156
  134.7 15.1 %copy-start.13 = (s32[16]{0:T(128)S(1)}, s32[16]{0:T(128)}, u32[]{:S(2)}) copy-start(s32[16]{0:T(128)} %param.19) | copy-start | bytes 196
  134.7 50.7 %all-to-all-start.1 = ((f32[4,16,64,128]{3,2,1,0:T(8,128)}), f32[4,16,64,128]{3,2,1,0:T(8,128)S(1)}, u32[]{:S(2)}, u32[]{:S(2)}) async-start(f32[4,16,64,128]{3,2,1,0:T(8,128)} %reverse_select_fusion.1), calls=%async_computation.1 | async-start | bytes 4194304 | tf_op jit(solution)/shard_map/all_to_all | solution.py:100
  189.3 5.4 %copy-start.2 = (f32[4,16,64,128]{3,2,1,0:T(8,128)S(1)}, f32[4,16,64,128]{3,2,1,0:T(8,128)}, u32[]{:S(2)}) copy-start(f32[4,16,64,128]{3,2,1,0:T(8,128)} %maximum_select_fusion.1) | copy-start | bytes 6291460
  192.6 2.3 %copy-start.7 = (f32[8,128,4,64]{1,3,2,0:T(8,128)S(1)}, f32[8,128,4,64]{1,3,2,0:T(8,128)}, u32[]{:S(2)}) copy-start(f32[8,128,4,64]{1,3,2,0:T(8,128)} %get-tuple-element.46) | copy-start | bytes 3145732
  192.6 6.9 %collective-permute-start.3 = (bf16[8,4,1024,32]{2,3,1,0:T(8,128)(2,1)}, bf16[8,4,1024,32]{2,3,1,0:T(8,128)(2,1)}, u32[]{:S(2)}, u32[]{:S(2)}) collective-permute-start(bf16[8,4,1024,32]{2,3,1,0:T(8,128)(2,1)} %bitcast.156), channel_id=1, source_target_pairs={{0,32},{32,0},{64,96},{96,64},{128,160},{160,128},{192,224},{224,1... | collective-permute-start | bytes 6291464 | tf_op jit(solution)/shard_map/ppermute | solution.py:113
  196.4 0.7 copy-start.10
  202.0 17.7 %collective-permute-start.4 = (bf16[128,1024]{1,0:T(8,128)(2,1)S(1)}, bf16[128,1024]{1,0:T(8,128)(2,1)S(1)}, u32[]{:S(2)}, u32[]{:S(2)}) collective-permute-start(bf16[128,1024]{1,0:T(8,128)(2,1)S(1)} %copy.114), channel_id=1, source_target_pairs={{28,32},{32,28},{60,64},{64,60},{92,96},{96,92},{124,128},{128,124... | collective-permute-start | bytes 786440 | tf_op jit(solution)/shard_map/ppermute | solution.py:213
Sparse Core Ops, SparseCore 0:
  59.5 68.3 all-gather.4
  131.3 57.9 all-gather.6

commit v12 on v10

--- a/solution.py
+++ b/solution.py
@@ -74,7 +74,7 @@
     for k in range(ROW):
         pre.append(acc)
         acc = combine(acc, (logs[k], states[k]))
-    rows = lax.axis_size("z")
+    rows = lax.axis_size("zh") * lax.axis_size("zl")
     wins = lax.axis_size("win")
     total = acc
     entering = (jnp.zeros_like(acc[0]), jnp.zeros_like(acc[1]))
@@ -87,7 +87,7 @@
                     to = z - d if (x >= half) != (w % 2 == 1) else z + d
                     if 0 <= to < rows:
                         pairs.append(((w * rows + z) * parts + x, (w * rows + to) * parts + x))
-        got = split_packed(lax.ppermute(pack(*total), ("win", "z", "x"), pairs))
+        got = split_packed(lax.ppermute(pack(*total), ("win", "zh", "zl", "x"), pairs))
         entering = combine(got, entering)
         if d * 2 < rows:
             total = combine(got, total)
@@ -103,7 +103,8 @@
 def gather_weight(output_weight):
     half = lax.axis_index("win") % 2
     half_rows = output_weight.shape[0] // 2
-    column = lax.all_gather(output_weight, "z", axis=0)
+    far = lax.all_gather(output_weight, "zh", axis=0)
+    column = lax.all_gather(far, "zl", axis=1).reshape((-1,) + output_weight.shape)
     mine = lax.dynamic_slice_in_dim(column, half * half_rows, half_rows, axis=1)
     row = lax.all_gather(mine, "x", axis=1)
     wins = lax.axis_size("win")
@@ -135,7 +136,7 @@
 ):
     frames = frame_inputs[0]
     frame_count = frames.shape[0]
-    rows = lax.axis_size("z")
+    rows = lax.axis_size("zh") * lax.axis_size("zl")
     row_len = lax.axis_size("x")
     chain_length = rows * row_len
     window_length = frame_count * chain_length
@@ -202,12 +203,12 @@
     projected_rows = project(normed, gather_weight(output_weight)).astype(jnp.bfloat16)
     window_index = lax.axis_index("win")
     window_total = lax.axis_size("win")
-    row_index = lax.axis_index("z")
+    row_index = lax.axis_index("zh") * lax.axis_size("zl") + lax.axis_index("zl")
     pairs = []
     for w in range(1, window_total):
         pairs.append(((w - 1) * rows + rows - 1, w * rows))
         pairs.append((w * rows, (w - 1) * rows + rows - 1))
-    partner = lax.ppermute(projected_rows, ("win", "z"), pairs)
+    partner = lax.ppermute(projected_rows, ("win", "zh", "zl"), pairs)
     seam_pos = lax.axis_index("x") * frame_count + jnp.arange(frame_count)
     is_tail = row_index == rows - 1
     fade_window = jnp.minimum(window_index + is_tail.astype(jnp.int32), window_total - 1)
@@ -225,8 +226,8 @@
 def solution(mesh):
     wins, chain = mesh.devices.shape
     rows = chain // ROW
-    grid = Mesh(mesh.devices.reshape(wins, rows, ROW), ("win", "z", "x"))
-    blocks = ("z", "x")
+    grid = Mesh(mesh.devices.reshape(wins, 2, rows // 2, ROW), ("win", "zh", "zl", "x"))
+    blocks = ("zh", "zl", "x")
     in_specs = (
         P("win", blocks, None),
         P("win", blocks, None),

time: 203 us -> 232 us (1.14)
  blocking collectives: 0 us -> 16.5 us
  local copies, waits for them, and re-layouts: 16.1 us -> 24.3 us
  waiting for transfers between devices: 81.5 us -> 85.5 us
  other arithmetic: 18.7 us -> 21.8 us
    all_gather x1, waiting for transfers between devices: 16.9 us -> 37.7 us  [gather_weight(): lax.all_gather(far, 'zl', axis=1).reshape((-1,) + output_weight.shape)]
    all_gather x0 -> x1, blocking collectives: none -> 16.5 us  [gather_weight(): far = lax.all_gather(output_weight, 'zh', axis=0)]
    ppermute x4, waiting for transfers between devices: 24.5 us -> 15.7 us  [the longest x1 9.6 us: per_device(): partner = lax.ppermute(projected_rows, ('win', 'zh', 'zl'), pairs)]
    all_gather x1 -> x2, local copies, waits for them, and re-layouts: 3.16 us -> 8.61 us  [gather_weight(): row = lax.all_gather(mine, 'x', axis=1)]
    all_gather x1, waiting for transfers between devices: 4.53 us -> 0.02 us  [gather_weight(): row = lax.all_gather(mine, 'x', axis=1)]
    unnamed x41 -> x37, local copies, waits for them, and re-layouts: 9.18 us -> 4.78 us
    all_to_all x1, waiting for transfers between devices: 14.9 us -> 11.3 us  [scan_states(): back = lax.all_to_all(out, 'x', 0, 0, tiled=True)]
    ppermute x4, starting transfers between devices: 28 us -> 24.7 us  [the longest x3 17.8 us: scan_states(): lax.ppermute(pack(*total), ('win', 'zh', 'zl', 'x'), pairs)]
  transfers between devices with their start and end apart: 9 -> 9, of which waited for: 7 -> 5; matrix products, arithmetic and copies ran while one was open for 16% -> 16% of each run, Pallas kernels for 0% -> 0%
where the time goes in v12:
time: 232 us; the launch traced here: 231 us
  waiting for transfers between devices  85.5 us (37%)
  starting transfers between devices  54.2 us (23%)
  local copies, waits for them, and re-layouts  24.3 us (10%)
  other arithmetic  21.8 us (9%)
  blocking collectives  16.5 us (7%)
  matrix products  15.1 us (7%)
  between operations  13.8 us (6%)
    all_gather x1, waiting for transfers between devices, gather_weight(): lax.all_gather(far, 'zl', axis=1).reshape((-1,) + output_weight.shape)  37.7 us
    all_to_all x1, starting transfers between devices, scan_states(): back = lax.all_to_all(out, 'x', 0, 0, tiled=True)  22.9 us
    all_to_all x1, waiting for transfers between devices, scan_states(): mine = lax.all_to_all(send, 'x', 0, 0, tiled=True)  20.7 us
    ppermute x3, starting transfers between devices, scan_states(): lax.ppermute(pack(*total), ('win', 'zh', 'zl', 'x'), pairs)  17.8 us
    all_gather x1, blocking collectives, gather_weight(): far = lax.all_gather(output_weight, 'zh', axis=0)  16.5 us
    all_to_all x1, waiting for transfers between devices, scan_states(): back = lax.all_to_all(out, 'x', 0, 0, tiled=True)  11.3 us
    ppermute x1, waiting for transfers between devices, per_device(): partner = lax.ppermute(projected_rows, ('win', 'zh', 'zl'), pairs)  9.6 us
    all_gather x2, local copies, waits for them, and re-layouts, gather_weight(): row = lax.all_gather(mine, 'x', axis=1)  8.61 us
  transfers between devices with their start and end apart: 9, of which 5 were waited for; matrix products, arithmetic and copies ran while one was open for 16% of the time, Pallas kernels for 0%

profile of v12, /device:TPU:24, one launch (start us, length us, event | category | flops | bytes accessed | tf_op | source)
XLA Modules:
  0.0 231.2 jit_solution(8742488787730141454)
XLA Ops:
  6.5 0.8 compare_select_fusion
  7.3 0.7 multiply_bitcast_fusion
  8.7 0.7 fusion.53
  9.4 1.3 copy.120
  10.8 0.8 bitcast_convert_fusion
  11.7 0.8 convolution_bitcast_fusion.4
  12.5 0.8 convolution_bitcast_fusion.3
  13.9 1.7 maximum_select_fusion
  15.5 4.4 %all-to-all-start = ((f32[4,16,72,128]{3,2,1,0:T(8,128)}), f32[4,16,72,128]{3,2,1,0:T(8,128)S(1)}, u32[]{:S(2)}, u32[]{:S(2)}) async-start(f32[4,16,72,128]{3,2,1,0:T(8,128)} %maximum_select_fusion), calls=%async_computation | async-start | bytes 4718592 | tf_op jit(solution)/shard_map/all_to_all | solution.py:67
  20.2 8.2 %while.11 = (s32[]{:T(128)}, f32[8,128,4,64]{1,3,2,0:T(8,128)}, bf16[8,128,4,64]{1,3,2,0:T(8,128)(2,1)S(1)}, f32[128,128]{1,0:T(8,128)S(1)}, f32[8,4,128]{2,1,0:...) while((s32[]{:T(128)}, f32[8,128,4,64]{1,3,2,0:T(8,128)}, ...), condition=%wide.region_4.5_spmd.clone, body=%wide.region_3.4_spmd.clone.sunk | while | flops 8732674 | bytes 312401 | solution.py:183
  20.2 1.0 fusion.63
  21.2 1.0 fusion.63
  22.3 1.0 fusion.63
  23.3 1.0 fusion.63
  24.3 1.0 fusion.63
  25.3 1.0 fusion.63
  26.3 1.0 fusion.63
  27.4 1.0 fusion.63
  28.4 20.7 %all-to-all-done = f32[4,16,72,128]{3,2,1,0:T(8,128)S(1)} async-done(((f32[4,16,72,128]{3,2,1,0:T(8,128)}), f32[4,16,72,128]{3,2,1,0:T(8,128)S(1)}, u32[]{:S(2)}, u32[]{:S(2)}) %all-to-all-start) | async-done | bytes 2359328 | tf_op jit(solution)/shard_map/all_to_all | solution.py:67
  49.1 1.4 copy-done.1
  50.5 2.6 %reverse_select_fusion = f32[4,16,72,128]{3,2,1,0:T(8,128)S(1)} fusion(f32[4,16,72,128]{3,2,1,0:T(8,128)} %copy-done.1, pred[]{:T(512)S(6)} %xor.3), kind=kLoop, calls=%fused_computation.16 | loop fusion | flops 589824 | bytes 4718593 | tf_op jit(solution)/shard_map/jit(_where)/select_n | solution.py:70
  53.1 0.3 exponential_reduce_fusion
  53.5 1.0 fusion.27
  54.6 0.9 pad_maximum_fusion.2
  55.5 3.8 %collective-permute-start = (f32[16,72,128]{2,1,0:T(8,128)}, f32[16,72,128]{2,1,0:T(8,128)S(1)}, u32[]{:S(2)}, u32[]{:S(2)}) collective-permute-start(f32[16,72,128]{2,1,0:T(8,128)} %pad_maximum_fusion.2), channel_id=1, source_target_pairs={{0,4},{1,5},{4,8},{5,9},{6,2},{7,3},{8,12},{9,13},{10,6},{11,7},{1... | collective-permute-start | bytes 1769480 | tf_op jit(solution)/shard_map/ppermute | solution.py:90
  59.3 16.5 %all-gather = bf16[4096,32]{0,1:T(8,128)(2,1)} all-gather(bf16[2048,32]{0,1:T(8,128)(2,1)S(1)} %copy-done.9), channel_id=2, replica_groups=mesh['win'=16,'zh'=2,'zl'=4,'x'=4] {'zh'}, dimensions={0}, use_global_device_ids=true | all-gather | bytes 393216 | tf_op jit(solution)/shard_map/all_gather | solution.py:106
  75.9 1.8 reshape.290
  77.8 0.5 exp.111
  78.4 0.7 copy-done.5
  79.2 1.2 multiply_add_fusion.1
  80.4 0.9 pad_maximum_fusion.3
  81.3 5.5 %collective-permute-start.1 = (f32[16,72,128]{2,1,0:T(8,128)}, f32[16,72,128]{2,1,0:T(8,128)}, u32[]{:S(2)}, u32[]{:S(2)}) collective-permute-start(f32[16,72,128]{2,1,0:T(8,128)} %pad_maximum_fusion.3), channel_id=1, source_target_pairs={{0,8},{1,9},{4,12},{5,13},{8,16},{9,17},{10,2},{11,3},{12,20},{13,... | collective-permute-start | bytes 1769480 | tf_op jit(solution)/shard_map/ppermute | solution.py:90
  86.7 37.7 %all-gather.6.cloned.1.call-done = bf16[2,8192,32]{1,0,2:T(2,128)(2,1)} async-done(((bf16[2,2048,32]{1,0,2:T(2,128)(2,1)}), bf16[2,8192,32]{1,0,2:T(2,128)(2,1)}) %all-gather.6.cloned.1.call-update) | async-done | bytes 1048592 | tf_op jit(solution)/shard_map/all_gather | solution.py:107
  124.4 2.2 reshape.288
  126.6 0.8 slice.133
  127.5 0.5 exponential_bitcast_fusion.2
  128.0 1.2 multiply_add_fusion
  129.3 0.9 pad_maximum_fusion.4
  130.2 8.5 %collective-permute-start.2 = (f32[16,72,128]{2,1,0:T(8,128)}, f32[16,72,128]{2,1,0:T(8,128)}, u32[]{:S(2)}, u32[]{:S(2)}) collective-permute-start(f32[16,72,128]{2,1,0:T(8,128)} %pad_maximum_fusion.4), channel_id=1, source_target_pairs={{0,16},{1,17},{4,20},{5,21},{8,24},{9,25},{12,28},{13,29},{18,2},{... | collective-permute-start | bytes 1769480 | tf_op jit(solution)/shard_map/ppermute | solution.py:90
  138.6 0.8 constant_dynamic-slice_fusion
  139.5 6.1 %collective-permute-done.2 = f32[16,72,128]{2,1,0:T(8,128)} collective-permute-done((f32[16,72,128]{2,1,0:T(8,128)}, f32[16,72,128]{2,1,0:T(8,128)}, u32[]{:S(2)}, u32[]{:S(2)}) %collective-permute-start.2) | collective-permute-done | bytes 589856 | tf_op jit(solution)/shard_map/ppermute | solution.py:90
  145.6 1.4 add_bitcast_fusion.2
  147.1 0.2 add_bitcast_fusion.1
  147.3 0.2 pad_maximum_fusion.1
  147.5 1.5 reverse_select_fusion.1
  149.1 22.9 %all-to-all-start.1 = ((f32[4,16,64,128]{3,2,1,0:T(8,128)}), f32[4,16,64,128]{3,2,1,0:T(8,128)S(1)}, u32[]{:S(2)}, u32[]{:S(2)}) async-start(f32[4,16,64,128]{3,2,1,0:T(8,128)} %reverse_select_fusion.1), calls=%async_computation.1 | async-start | bytes 4194304 | tf_op jit(solution)/shard_map/all_to_all | solution.py:97
  172.0 1.3 copy.128
  173.3 0.6 dynamic_slice.23
  173.9 0.6 iota_compare_fusion.1
  174.6 4.5 %reshape.297 = bf16[8,4,1024,32]{2,1,0,3:T(4,128)(2,1)} reshape(bf16[8,4096,32]{1,0,2:T(8,128)(2,1)} %all-gather.8.cloned.1.call-done) | data formatting | bytes 4194304 | tf_op jit(solution)/shard_map/all_gather | solution.py:109
  179.1 4.1 %copy.131 = bf16[8,4,1024,32]{2,3,1,0:T(8,128)(2,1)} copy(bf16[8,4,1024,32]{2,1,0,3:T(4,128)(2,1)} %reshape.297) | data formatting | bytes 4194304 | tf_op jit(solution)/shard_map/all_gather | solution.py:109
  183.2 2.1 collective-permute-start.3
  185.3 11.3 %all-to-all-done.1 = f32[4,16,64,128]{3,2,1,0:T(8,128)S(1)} async-done(((f32[4,16,64,128]{3,2,1,0:T(8,128)}), f32[4,16,64,128]{3,2,1,0:T(8,128)S(1)}, u32[]{:S(2)}, u32[]{:S(2)}) %all-to-all-start.1) | async-done | bytes 2097184 | tf_op jit(solution)/shard_map/all_to_all | solution.py:97
  196.8 0.4 maximum_select_fusion.1
  197.3 1.1 copy-done.7
  198.4 0.6 fusion.15
  199.1 0.8 multiply_reduce_fusion
  200.1 1.3 copy.129
  201.4 1.3 multiply_convert_fusion.6
  202.7 1.5 fusion.33
  204.2 2.3 %fusion.17 = bf16[128,8,4,32]{0,3,2,1:T(8,128)(2,1)S(1)} fusion(f32[128,8,4,32]{0,3,2,1:T(8,128)S(1)} %fusion.33, bf16[8,4,1024,32]{2,3,1,0:T(8,128)(2,1)} %collective-permute-done.3, bf16[128,2048]{1,0:T(8,128)(2,1)S(1)} %multiply_convert_fusion.6, s32[]{:T(128)S(6)} %select_n.87), kind=kOutput, calls=%fused_computation.34 | convolution fusion | flops 268697600 | bytes 3145732 | tf_op jit(solution)/shard_map/tr,zxrc->tzxc/dot_general | solution.py:122
  206.7 6.9 %collective-permute-start.4 = (bf16[128,1024]{1,0:T(8,128)(2,1)S(1)}, bf16[128,1024]{1,0:T(8,128)(2,1)S(1)}, u32[]{:S(2)}, u32[]{:S(2)}) collective-permute-start(bf16[128,1024]{1,0:T(8,128)(2,1)S(1)} %copy.133), channel_id=1, source_target_pairs={{28,32},{32,28},{60,64},{64,60},{92,96},{96,92},{124,128},{128,124... | collective-permute-start | bytes 786440 | tf_op jit(solution)/shard_map/ppermute | solution.py:211
  213.8 9.6 %collective-permute-done.4 = bf16[128,1024]{1,0:T(8,128)(2,1)S(1)} collective-permute-done((bf16[128,1024]{1,0:T(8,128)(2,1)S(1)}, bf16[128,1024]{1,0:T(8,128)(2,1)S(1)}, u32[]{:S(2)}, u32[]{:S(2)}) %collective-permute-start.4) | collective-permute-done | bytes 262176 | tf_op jit(solution)/shard_map/ppermute | solution.py:211
  223.4 0.9 fusion.31
  (92 shorter events, 3.1 us)
Async XLA Ops:
  6.5 13.5 %copy-start = (bf16[1,128,128]{2,1,0:T(8,128)(2,1)S(1)}, bf16[1,128,128]{2,1,0:T(8,128)(2,1)}, u32[]{:S(2)}) copy-start(bf16[1,128,128]{2,1,0:T(8,128)(2,1)} %param.14) | copy-start | bytes 98308
  15.5 4.5 %copy-start.10 = (bf16[1,128,128]{2,1,0:T(8,128)(2,1)S(1)}, bf16[1,128,128]{2,1,0:T(8,128)(2,1)}, u32[]{:S(2)}) copy-start(bf16[1,128,128]{2,1,0:T(8,128)(2,1)} %param.13) | copy-start | bytes 98308
  15.5 33.6 %all-to-all-start = ((f32[4,16,72,128]{3,2,1,0:T(8,128)}), f32[4,16,72,128]{3,2,1,0:T(8,128)S(1)}, u32[]{:S(2)}, u32[]{:S(2)}) async-start(f32[4,16,72,128]{3,2,1,0:T(8,128)} %maximum_select_fusion), calls=%async_computation | async-start | bytes 4718592 | tf_op jit(solution)/shard_map/all_to_all | solution.py:67
  20.0 104.4 %all-gather.6.cloned.1.call-start = ((), (), s32[]{:S(2)}) async-start(), calls=%async_computation.2 | async-start | bytes 1310720 | tf_op jit(solution)/shard_map/all_gather | solution.py:107
  49.1 1.4 copy-start.1
  53.5 1.1 copy-start.14
  53.5 5.9 %copy-start.9 = (bf16[2048,32]{0,1:T(8,128)(2,1)S(1)}, bf16[2048,32]{0,1:T(8,128)(2,1)}, u32[]{:S(2)}) copy-start(bf16[2048,32]{0,1:T(8,128)(2,1)} %param.18) | copy-start | bytes 393220
  55.5 22.9 %collective-permute-start = (f32[16,72,128]{2,1,0:T(8,128)}, f32[16,72,128]{2,1,0:T(8,128)S(1)}, u32[]{:S(2)}, u32[]{:S(2)}) collective-permute-start(f32[16,72,128]{2,1,0:T(8,128)} %pad_maximum_fusion.2), channel_id=1, source_target_pairs={{0,4},{1,5},{4,8},{5,9},{6,2},{7,3},{8,12},{9,13},{10,6},{11,7},{1... | collective-permute-start | bytes 1769480 | tf_op jit(solution)/shard_map/ppermute | solution.py:90
  77.8 96.9 %all-gather.8.cloned.1.call-start = ((), (), s32[]{:S(2)}) async-start(), calls=%async_computation.3 | async-start | bytes 2621440 | tf_op jit(solution)/shard_map/all_gather | solution.py:109
  78.3 0.8 copy-start.5
  81.3 45.3 %collective-permute-start.1 = (f32[16,72,128]{2,1,0:T(8,128)}, f32[16,72,128]{2,1,0:T(8,128)}, u32[]{:S(2)}, u32[]{:S(2)}) collective-permute-start(f32[16,72,128]{2,1,0:T(8,128)} %pad_maximum_fusion.3), channel_id=1, source_target_pairs={{0,8},{1,9},{4,12},{5,13},{8,16},{9,17},{10,2},{11,3},{12,20},{13,... | collective-permute-start | bytes 1769480 | tf_op jit(solution)/shard_map/ppermute | solution.py:90
  127.5 11.1 %copy-start.3 = (bf16[8,2048,32]{1,0,2:T(8,128)(2,1)S(1)}, bf16[8,2048,32]{1,0,2:T(8,128)(2,1)}, u32[]{:S(2)}) copy-start(bf16[8,2048,32]{1,0,2:T(8,128)(2,1)} %reshape.288) | copy-start | bytes 3145732
  128.0 17.6 %copy-start.12 = (f32[16]{0:T(128)S(1)}, f32[16]{0:T(128)}, u32[]{:S(2)}) copy-start(f32[16]{0:T(128)} %get-tuple-element.108) | copy-start | bytes 196
  128.0 17.6 %copy-start.13 = (f32[16]{0:T(128)S(1)}, f32[16]{0:T(128)}, u32[]{:S(2)}) copy-start(f32[16]{0:T(128)} %get-tuple-element.113) | copy-start | bytes 196
  129.2 16.4 %copy-start.6 = (f32[16,72,128]{2,1,0:T(8,128)S(1)}, f32[16,72,128]{2,1,0:T(8,128)}, u32[]{:S(2)}) copy-start(f32[16,72,128]{2,1,0:T(8,128)} %copy-done.5) | copy-start | bytes 1769476
  129.2 16.4 %copy-start.15 = (f32[16]{0:T(128)S(1)}, f32[16]{0:T(128)}, u32[]{:S(2)}) copy-start(f32[16]{0:T(128)} %copy-done.14) | copy-start | bytes 196
  130.2 15.4 %collective-permute-start.2 = (f32[16,72,128]{2,1,0:T(8,128)}, f32[16,72,128]{2,1,0:T(8,128)}, u32[]{:S(2)}, u32[]{:S(2)}) collective-permute-start(f32[16,72,128]{2,1,0:T(8,128)} %pad_maximum_fusion.4), channel_id=1, source_target_pairs={{0,16},{1,17},{4,20},{5,21},{8,24},{9,25},{12,28},{13,29},{18,2},{... | collective-permute-start | bytes 1769480 | tf_op jit(solution)/shard_map/ppermute | solution.py:90
  139.5 7.6 %copy-start.4 = (f32[16,64,128]{2,1,0:T(8,128)S(1)}, f32[16,64,128]{2,1,0:T(8,128)}, u32[]{:S(2)}) copy-start(f32[16,64,128]{2,1,0:T(8,128)} %get-tuple-element.89) | copy-start | bytes 1572868
  149.0 22.9 %copy-start.8 = (f32[128,32]{1,0:T(8,128)S(1)}, f32[128,32]{1,0:T(8,128)}, u32[]{:S(2)}) copy-start(f32[128,32]{1,0:T(8,128)} %get-tuple-element.100) | copy-start | bytes 49156
  149.1 24.2 %copy-start.16 = (s32[16]{0:T(128)S(1)}, s32[16]{0:T(128)}, u32[]{:S(2)}) copy-start(s32[16]{0:T(128)} %param.19) | copy-start | bytes 196
  149.1 47.6 %all-to-all-start.1 = ((f32[4,16,64,128]{3,2,1,0:T(8,128)}), f32[4,16,64,128]{3,2,1,0:T(8,128)S(1)}, u32[]{:S(2)}, u32[]{:S(2)}) async-start(f32[4,16,64,128]{3,2,1,0:T(8,128)} %reverse_select_fusion.1), calls=%async_computation.1 | async-start | bytes 4194304 | tf_op jit(solution)/shard_map/all_to_all | solution.py:97
  183.2 21.0 %collective-permute-start.3 = (bf16[8,4,1024,32]{2,3,1,0:T(8,128)(2,1)}, bf16[8,4,1024,32]{2,3,1,0:T(8,128)(2,1)}, u32[]{:S(2)}, u32[]{:S(2)}) collective-permute-start(bf16[8,4,1024,32]{2,3,1,0:T(8,128)(2,1)} %copy.131), channel_id=1, source_target_pairs={{0,32},{32,0},{64,96},{96,64},{128,160},{160,128},{192,224},{224,1... | collective-permute-start | bytes 6291464 | tf_op jit(solution)/shard_map/ppermute | solution.py:112
  197.2 1.2 copy-start.7
  199.9 1.5 copy-start.11
  200.1 2.6 %copy-start.2 = (bf16[8,4,1024,32]{2,1,0,3:T(4,128)(2,1)S(1)}, bf16[8,4,1024,32]{2,1,0,3:T(4,128)(2,1)}, u32[]{:S(2)}) copy-start(bf16[8,4,1024,32]{2,1,0,3:T(4,128)(2,1)} %reshape.297) | copy-start | bytes 6291460
  206.7 16.6 %collective-permute-start.4 = (bf16[128,1024]{1,0:T(8,128)(2,1)S(1)}, bf16[128,1024]{1,0:T(8,128)(2,1)S(1)}, u32[]{:S(2)}, u32[]{:S(2)}) collective-permute-start(bf16[128,1024]{1,0:T(8,128)(2,1)S(1)} %copy.133), channel_id=1, source_target_pairs={{28,32},{32,28},{60,64},{64,60},{92,96},{96,92},{124,128},{128,124... | collective-permute-start | bytes 786440 | tf_op jit(solution)/shard_map/ppermute | solution.py:211
Sparse Core Ops, SparseCore 0:
  77.9 46.4 all-gather.5
  139.6 32.3 all-gather.7

commit v13 on v12

--- a/solution.py
+++ b/solution.py
@@ -103,8 +103,11 @@
 def gather_weight(output_weight):
     half = lax.axis_index("win") % 2
     half_rows = output_weight.shape[0] // 2
-    far = lax.all_gather(output_weight, "zh", axis=0)
-    column = lax.all_gather(far, "zl", axis=1).reshape((-1,) + output_weight.shape)
+    width = output_weight.shape[1]
+    padded = jnp.concatenate([output_weight, jnp.zeros_like(output_weight)], axis=1)
+    near = lax.all_gather(padded, "zl", axis=0)
+    both = lax.all_gather(near, "zh", axis=0)
+    column = both.reshape((-1,) + padded.shape)[..., :width]
     mine = lax.dynamic_slice_in_dim(column, half * half_rows, half_rows, axis=1)
     row = lax.all_gather(mine, "x", axis=1)
     wins = lax.axis_size("win")

time: 232 us -> 304 us (1.31)
  waiting for transfers between devices: 85.5 us -> 144 us
  starting transfers between devices: 54.2 us -> 92.6 us
  blocking collectives: 16.5 us -> 0 us
  local copies, waits for them, and re-layouts: 24.3 us -> 16.2 us
    ppermute x3, starting transfers between devices: 17.8 us -> 73.9 us  [scan_states(): lax.ppermute(pack(*total), ('win', 'zh', 'zl', 'x'), pairs)]
    all_gather x1 -> x2, waiting for transfers between devices: 37.7 us -> 67.1 us  [the longest x1 58.9 us: gather_weight(): both = lax.all_gather(near, 'zh', axis=0)]
    all_to_all x1, waiting for transfers between devices: 11.3 us -> 39 us  [scan_states(): back = lax.all_to_all(out, 'x', 0, 0, tiled=True)]
    all_to_all x1, starting transfers between devices: 22.9 us -> 4.76 us  [scan_states(): back = lax.all_to_all(out, 'x', 0, 0, tiled=True)]
    all_gather x1 -> x0, blocking collectives: 16.5 us -> none  [gather_weight(): far = lax.all_gather(output_weight, 'zh', axis=0)]
    all_gather x2 -> x1, local copies, waits for them, and re-layouts: 8.61 us -> 3.29 us  [gather_weight(): row = lax.all_gather(mine, 'x', axis=1)]
  transfers between devices with their start and end apart: 9 -> 10, of which waited for: 5 -> 6; matrix products, arithmetic and copies ran while one was open for 16% -> 11% of each run, Pallas kernels for 0% -> 0%
where the time goes in v13:
time: 304 us; the launch traced here: 302 us
  waiting for transfers between devices  144 us (47%)
  starting transfers between devices  92.6 us (30%)
  other arithmetic  20.1 us (7%)
  local copies, waits for them, and re-layouts  16.2 us (5%)
  matrix products  15.9 us (5%)
  between operations  13.5 us (4%)
    ppermute x3, starting transfers between devices, scan_states(): lax.ppermute(pack(*total), ('win', 'zh', 'zl', 'x'), pairs)  73.9 us
    all_gather x1, waiting for transfers between devices, gather_weight(): both = lax.all_gather(near, 'zh', axis=0)  58.9 us
    all_to_all x1, waiting for transfers between devices, scan_states(): back = lax.all_to_all(out, 'x', 0, 0, tiled=True)  39 us
    all_to_all x1, waiting for transfers between devices, scan_states(): mine = lax.all_to_all(send, 'x', 0, 0, tiled=True)  19.9 us
    ppermute x1, waiting for transfers between devices, per_device(): partner = lax.ppermute(projected_rows, ('win', 'zh', 'zl'), pairs)  10.4 us
    all_gather x1, waiting for transfers between devices, gather_weight(): near = lax.all_gather(padded, 'zl', axis=0)  8.19 us
    dot_general x8, matrix products, group_mix(): jnp.einsum('hts,shp->thp', mixing, group_frames, preferred_element_type=j...  8.01 us
    ppermute x1, starting transfers between devices, per_device(): partner = lax.ppermute(projected_rows, ('win', 'zh', 'zl'), pairs)  7.42 us
  transfers between devices with their start and end apart: 10, of which 6 were waited for; matrix products, arithmetic and copies ran while one was open for 11% of the time, Pallas kernels for 0%

profile of v13, /device:TPU:24, one launch (start us, length us, event | category | flops | bytes accessed | tf_op | source)
XLA Modules:
  0.0 302.3 jit_solution(15053144008970689009)
XLA Ops:
  6.5 0.8 compare_select_fusion
  7.3 0.7 multiply_bitcast_fusion
  8.3 0.2 reduce_window_sum.17
  8.5 0.2 reduce_window_sum.18
  8.7 0.7 fusion.52
  9.5 1.3 copy.100
  10.8 0.8 bitcast_convert_fusion
  11.7 0.8 convolution_bitcast_fusion.4
  12.5 0.8 convolution_bitcast_fusion.3
  13.5 0.2 pad_maximum_fusion
  13.7 0.2 fusion.49
  13.9 1.7 maximum_select_fusion
  15.5 4.4 %all-to-all-start = ((f32[4,16,72,128]{3,2,1,0:T(8,128)}), f32[4,16,72,128]{3,2,1,0:T(8,128)S(1)}, u32[]{:S(2)}, u32[]{:S(2)}) async-start(f32[4,16,72,128]{3,2,1,0:T(8,128)} %maximum_select_fusion), calls=%async_computation | async-start | bytes 4718592 | tf_op jit(solution)/shard_map/all_to_all | solution.py:67
  20.0 0.7 concatenate.27
  21.0 8.2 %while.11 = (s32[]{:T(128)}, f32[8,128,4,64]{1,3,2,0:T(8,128)}, bf16[8,128,4,64]{1,3,2,0:T(8,128)(2,1)S(1)}, f32[128,128]{1,0:T(8,128)S(1)}, f32[8,4,128]{2,1,0:...) while((s32[]{:T(128)}, f32[8,128,4,64]{1,3,2,0:T(8,128)}, ...), condition=%wide.region_4.5_spmd.clone, body=%wide.region_3.4_spmd.clone.sunk | while | flops 8732674 | bytes 312401 | solution.py:186
  21.0 1.0 fusion.62
  22.1 1.0 fusion.62
  23.1 1.0 fusion.62
  24.1 1.0 fusion.62
  25.1 1.0 fusion.62
  26.1 1.0 fusion.62
  27.2 1.0 fusion.62
  28.2 1.0 fusion.62
  29.2 19.9 %all-to-all-done = f32[4,16,72,128]{3,2,1,0:T(8,128)S(1)} async-done(((f32[4,16,72,128]{3,2,1,0:T(8,128)}), f32[4,16,72,128]{3,2,1,0:T(8,128)S(1)}, u32[]{:S(2)}, u32[]{:S(2)}) %all-to-all-start) | async-done | bytes 2359328 | tf_op jit(solution)/shard_map/all_to_all | solution.py:67
  49.1 1.4 copy-done.1
  50.5 2.6 reverse_select_fusion
  53.2 0.3 exponential_reduce_fusion
  53.5 1.0 fusion.27
  54.6 0.9 pad_maximum_fusion.2
  55.5 4.6 %collective-permute-start = (f32[16,72,128]{2,1,0:T(8,128)}, f32[16,72,128]{2,1,0:T(8,128)}, u32[]{:S(2)}, u32[]{:S(2)}) collective-permute-start(f32[16,72,128]{2,1,0:T(8,128)} %pad_maximum_fusion.2), channel_id=1, source_target_pairs={{0,4},{1,5},{4,8},{5,9},{6,2},{7,3},{8,12},{9,13},{10,6},{11,7},{1... | collective-permute-start | bytes 1769480 | tf_op jit(solution)/shard_map/ppermute | solution.py:90
  60.2 8.2 %all-gather.7.cloned.1.call-done = bf16[8192,64]{0,1:T(8,128)(2,1)} async-done(((bf16[2048,64]{0,1:T(8,128)(2,1)}), bf16[8192,64]{0,1:T(8,128)(2,1)}) %all-gather.7.cloned.1.call-update) | async-done | bytes 1048592 | tf_op jit(solution)/shard_map/all_gather | solution.py:108
  68.3 2.3 copy.125
  70.8 0.8 slice.136
  71.7 1.2 multiply_add_fusion.1
  73.0 3.4 %collective-permute-start.1 = (f32[16,72,128]{2,1,0:T(8,128)S(1)}, f32[16,72,128]{2,1,0:T(8,128)S(1)}, u32[]{:S(2)}, u32[]{:S(2)}) collective-permute-start(f32[16,72,128]{2,1,0:T(8,128)S(1)} %pad_maximum_fusion.3), channel_id=1, source_target_pairs={{0,8},{1,9},{4,12},{5,13},{8,16},{9,17},{10,2},{11,3},{12,20},{13,... | collective-permute-start | bytes 1769480 | tf_op jit(solution)/shard_map/ppermute | solution.py:90
  76.4 7.4 %collective-permute-done.1 = f32[16,72,128]{2,1,0:T(8,128)S(1)} collective-permute-done((f32[16,72,128]{2,1,0:T(8,128)S(1)}, f32[16,72,128]{2,1,0:T(8,128)S(1)}, u32[]{:S(2)}, u32[]{:S(2)}) %collective-permute-start.1) | collective-permute-done | bytes 589856 | tf_op jit(solution)/shard_map/ppermute | solution.py:90
  83.9 0.5 exponential_bitcast_fusion.2
  84.6 0.9 pad_maximum_fusion.4
  85.5 65.8 %collective-permute-start.2 = (f32[16,72,128]{2,1,0:T(8,128)}, f32[16,72,128]{2,1,0:T(8,128)}, u32[]{:S(2)}, u32[]{:S(2)}) collective-permute-start(f32[16,72,128]{2,1,0:T(8,128)} %pad_maximum_fusion.4), channel_id=1, source_target_pairs={{0,16},{1,17},{4,20},{5,21},{8,24},{9,25},{12,28},{13,29},{18,2},{... | collective-permute-start | bytes 1769480 | tf_op jit(solution)/shard_map/ppermute | solution.py:90
  151.3 58.9 %all-gather.9.cloned.1.call-done = bf16[8,2048,64]{1,2,0:T(8,128)(2,1)} async-done(((bf16[4,2048,64]{1,2,0:T(8,128)(2,1)}), bf16[8,2048,64]{1,2,0:T(8,128)(2,1)}) %all-gather.9.cloned.1.call-update) | async-done | bytes 2097168 | tf_op jit(solution)/shard_map/all_gather | solution.py:109
  210.2 1.2 slice-done
  211.5 0.9 constant_dynamic-slice_fusion
  212.4 1.5 add_bitcast_fusion.2
  213.9 0.2 add_bitcast_fusion.1
  214.1 0.2 pad_maximum_fusion.1
  214.3 1.5 reverse_select_fusion.1
  215.8 4.8 %all-to-all-start.1 = ((f32[4,16,64,128]{3,2,1,0:T(8,128)}), f32[4,16,64,128]{3,2,1,0:T(8,128)S(1)}, u32[]{:S(2)}, u32[]{:S(2)}) async-start(f32[4,16,64,128]{3,2,1,0:T(8,128)} %reverse_select_fusion.1), calls=%async_computation.1 | async-start | bytes 4194304 | tf_op jit(solution)/shard_map/all_to_all | solution.py:97
  220.7 1.3 copy.108
  222.0 0.6 dynamic_slice.23
  222.5 0.6 iota_compare_fusion.1
  223.3 39.0 %all-to-all-done.1 = f32[4,16,64,128]{3,2,1,0:T(8,128)S(1)} async-done(((f32[4,16,64,128]{3,2,1,0:T(8,128)}), f32[4,16,64,128]{3,2,1,0:T(8,128)S(1)}, u32[]{:S(2)}, u32[]{:S(2)}) %all-to-all-start.1) | async-done | bytes 2097184 | tf_op jit(solution)/shard_map/all_to_all | solution.py:97
  262.4 1.8 maximum_select_fusion.1
  264.2 3.3 %copy.124 = bf16[8,4,4,8,1024]{4,3,1,2,0:T(8,128)(2,1)} copy(bf16[8,4,4,8,1024]{4,3,2,1,0:T(8,128)(2,1)} %bitcast.173) | data formatting | bytes 4194304 | tf_op jit(solution)/shard_map/all_gather | solution.py:112
  267.5 2.0 collective-permute-start.3
  269.5 0.2 fusion.50
  269.8 0.6 fusion.15
  270.4 0.8 multiply_reduce_fusion
  271.5 0.3 copy.109
  271.8 0.2 copy-done.8
  272.1 2.3 fusion.33
  274.4 2.3 fusion.17
  276.9 7.4 %collective-permute-start.4 = (bf16[128,1024]{1,0:T(8,128)(2,1)S(1)}, bf16[128,1024]{1,0:T(8,128)(2,1)S(1)}, u32[]{:S(2)}, u32[]{:S(2)}) collective-permute-start(bf16[128,1024]{1,0:T(8,128)(2,1)S(1)} %copy.113), channel_id=1, source_target_pairs={{28,32},{32,28},{60,64},{64,60},{92,96},{96,92},{124,128},{128,124... | collective-permute-start | bytes 786440 | tf_op jit(solution)/shard_map/ppermute | solution.py:214
  284.4 10.4 %collective-permute-done.4 = bf16[128,1024]{1,0:T(8,128)(2,1)S(1)} collective-permute-done((bf16[128,1024]{1,0:T(8,128)(2,1)S(1)}, bf16[128,1024]{1,0:T(8,128)(2,1)S(1)}, u32[]{:S(2)}, u32[]{:S(2)}) %collective-permute-start.4) | collective-permute-done | bytes 262176 | tf_op jit(solution)/shard_map/ppermute | solution.py:214
  294.8 0.9 fusion.31
  (93 shorter events, 2.6 us)
Async XLA Ops:
  6.5 14.3 %copy-start = (bf16[1,128,128]{2,1,0:T(8,128)(2,1)S(1)}, bf16[1,128,128]{2,1,0:T(8,128)(2,1)}, u32[]{:S(2)}) copy-start(bf16[1,128,128]{2,1,0:T(8,128)(2,1)} %param.14) | copy-start | bytes 98308
  15.5 4.4 %copy-start.6 = (bf16[2048,32]{0,1:T(8,128)(2,1)S(1)}, bf16[2048,32]{0,1:T(8,128)(2,1)}, u32[]{:S(2)}) copy-start(bf16[2048,32]{0,1:T(8,128)(2,1)} %param.18) | copy-start | bytes 393220
  15.5 5.3 %copy-start.7 = (bf16[1,128,128]{2,1,0:T(8,128)(2,1)S(1)}, bf16[1,128,128]{2,1,0:T(8,128)(2,1)}, u32[]{:S(2)}) copy-start(bf16[1,128,128]{2,1,0:T(8,128)(2,1)} %param.13) | copy-start | bytes 98308
  15.5 33.6 %all-to-all-start = ((f32[4,16,72,128]{3,2,1,0:T(8,128)}), f32[4,16,72,128]{3,2,1,0:T(8,128)S(1)}, u32[]{:S(2)}, u32[]{:S(2)}) async-start(f32[4,16,72,128]{3,2,1,0:T(8,128)} %maximum_select_fusion), calls=%async_computation | async-start | bytes 4718592 | tf_op jit(solution)/shard_map/all_to_all | solution.py:67
  20.0 48.4 %all-gather.7.cloned.1.call-start = ((), (), s32[]{:S(2)}) async-start(), calls=%async_computation.2 | async-start | bytes 1310720 | tf_op jit(solution)/shard_map/all_gather | solution.py:108
  20.7 189.5 %all-gather.9.cloned.1.call-start = ((), (), s32[]{:S(2)}) async-start(), calls=%async_computation.3 | async-start | bytes 3145728 | tf_op jit(solution)/shard_map/all_gather | solution.py:109
  49.1 1.4 copy-start.1
  53.5 2.0 copy-start.9
  53.5 2.0 copy-start.13
  55.5 15.2 %collective-permute-start = (f32[16,72,128]{2,1,0:T(8,128)}, f32[16,72,128]{2,1,0:T(8,128)}, u32[]{:S(2)}, u32[]{:S(2)}) collective-permute-start(f32[16,72,128]{2,1,0:T(8,128)} %pad_maximum_fusion.2), channel_id=1, source_target_pairs={{0,4},{1,5},{4,8},{5,9},{6,2},{7,3},{8,12},{9,13},{10,6},{11,7},{1... | collective-permute-start | bytes 1769480 | tf_op jit(solution)/shard_map/ppermute | solution.py:90
  70.7 193.5 %all-gather.11.cloned.1.call-start = ((), (), s32[]{:S(2)}) async-start(), calls=%async_computation.4 | async-start | bytes 2621440 | tf_op jit(solution)/shard_map/all_gather | solution.py:112
  73.0 10.8 %collective-permute-start.1 = (f32[16,72,128]{2,1,0:T(8,128)S(1)}, f32[16,72,128]{2,1,0:T(8,128)S(1)}, u32[]{:S(2)}, u32[]{:S(2)}) collective-permute-start(f32[16,72,128]{2,1,0:T(8,128)S(1)} %pad_maximum_fusion.3), channel_id=1, source_target_pairs={{0,8},{1,9},{4,12},{5,13},{8,16},{9,17},{10,2},{11,3},{12,20},{13,... | collective-permute-start | bytes 1769480 | tf_op jit(solution)/shard_map/ppermute | solution.py:90
  85.5 126.9 %copy-start.10 = (f32[16]{0:T(128)S(1)}, f32[16]{0:T(128)}, u32[]{:S(2)}) copy-start(f32[16]{0:T(128)} %copy-done.9) | copy-start | bytes 196
  85.5 126.9 %copy-start.11 = (f32[16]{0:T(128)S(1)}, f32[16]{0:T(128)}, u32[]{:S(2)}) copy-start(f32[16]{0:T(128)} %get-tuple-element.108) | copy-start | bytes 196
  85.5 126.9 %copy-start.12 = (f32[16]{0:T(128)S(1)}, f32[16]{0:T(128)}, u32[]{:S(2)}) copy-start(f32[16]{0:T(128)} %get-tuple-element.113) | copy-start | bytes 196
  85.5 126.9 %copy-start.14 = (f32[16]{0:T(128)S(1)}, f32[16]{0:T(128)}, u32[]{:S(2)}) copy-start(f32[16]{0:T(128)} %copy-done.13) | copy-start | bytes 196
  85.5 126.8 %collective-permute-start.2 = (f32[16,72,128]{2,1,0:T(8,128)}, f32[16,72,128]{2,1,0:T(8,128)}, u32[]{:S(2)}, u32[]{:S(2)}) collective-permute-start(f32[16,72,128]{2,1,0:T(8,128)} %pad_maximum_fusion.4), channel_id=1, source_target_pairs={{0,16},{1,17},{4,20},{5,21},{8,24},{9,25},{12,28},{13,29},{18,2},{... | collective-permute-start | bytes 1769480 | tf_op jit(solution)/shard_map/ppermute | solution.py:90
  210.2 1.2 slice-start
  212.3 1.5 copy-start.3
  215.8 4.8 %copy-start.5 = (f32[128,32]{1,0:T(8,128)S(1)}, f32[128,32]{1,0:T(8,128)}, u32[]{:S(2)}) copy-start(f32[128,32]{1,0:T(8,128)} %get-tuple-element.100) | copy-start | bytes 49156
  215.8 6.1 %copy-start.15 = (s32[16]{0:T(128)S(1)}, s32[16]{0:T(128)}, u32[]{:S(2)}) copy-start(s32[16]{0:T(128)} %param.19) | copy-start | bytes 196
  215.8 46.4 %all-to-all-start.1 = ((f32[4,16,64,128]{3,2,1,0:T(8,128)}), f32[4,16,64,128]{3,2,1,0:T(8,128)S(1)}, u32[]{:S(2)}, u32[]{:S(2)}) async-start(f32[4,16,64,128]{3,2,1,0:T(8,128)} %reverse_select_fusion.1), calls=%async_computation.1 | async-start | bytes 4194304 | tf_op jit(solution)/shard_map/all_to_all | solution.py:97
  264.2 5.3 %copy-start.2 = (f32[4,16,64,128]{3,2,1,0:T(8,128)S(1)}, f32[4,16,64,128]{3,2,1,0:T(8,128)}, u32[]{:S(2)}) copy-start(f32[4,16,64,128]{3,2,1,0:T(8,128)} %maximum_select_fusion.1) | copy-start | bytes 6291460
  267.5 2.3 copy-start.4
  267.5 6.9 %collective-permute-start.3 = (bf16[8,4,1024,32]{2,3,1,0:T(8,128)(2,1)}, bf16[8,4,1024,32]{2,3,1,0:T(8,128)(2,1)}, u32[]{:S(2)}, u32[]{:S(2)}) collective-permute-start(bf16[8,4,1024,32]{2,3,1,0:T(8,128)(2,1)} %bitcast.155), channel_id=1, source_target_pairs={{0,32},{32,0},{64,96},{96,64},{128,160},{160,128},{192,224},{224,1... | collective-permute-start | bytes 6291464 | tf_op jit(solution)/shard_map/ppermute | solution.py:115
  271.3 0.7 copy-start.8
  276.9 18.0 %collective-permute-start.4 = (bf16[128,1024]{1,0:T(8,128)(2,1)S(1)}, bf16[128,1024]{1,0:T(8,128)(2,1)S(1)}, u32[]{:S(2)}, u32[]{:S(2)}) collective-permute-start(bf16[128,1024]{1,0:T(8,128)(2,1)S(1)} %copy.113), channel_id=1, source_target_pairs={{28,32},{32,28},{60,64},{64,60},{92,96},{96,92},{124,128},{128,124... | collective-permute-start | bytes 786440 | tf_op jit(solution)/shard_map/ppermute | solution.py:214
Sparse Core Ops, SparseCore 0:
  22.9 45.4 all-gather.6
  70.8 139.3 all-gather.8
  212.5 51.5 all-gather.10

commit v14 on v10

--- a/solution.py
+++ b/solution.py
@@ -54,6 +54,18 @@
 def pack(logs, states):
     rows = jnp.broadcast_to(logs[..., None, None], logs.shape + (PAD_ROWS, N))
     return jnp.concatenate([states, rows], axis=-2)
+
+
+def pack_dense(logs, states):
+    heads = logs.shape[-1]
+    flat = states.reshape(heads * P_SIZE, N)
+    block = jnp.pad(logs, (0, PAD_ROWS * N - heads)).reshape(PAD_ROWS, N)
+    return jnp.concatenate([flat, block], axis=0)
+
+
+def split_dense(packed, heads):
+    state_rows = heads * P_SIZE
+    return packed[state_rows, :heads], packed[:state_rows].reshape(heads, P_SIZE, N)
 
 
 def scan_states(log_fwd, log_bwd, fresh_fwd, fresh_bwd, hold):
@@ -87,7 +99,11 @@
                     to = z - d if (x >= half) != (w % 2 == 1) else z + d
                     if 0 <= to < rows:
                         pairs.append(((w * rows + z) * parts + x, (w * rows + to) * parts + x))
-        got = split_packed(lax.ppermute(pack(*total), ("win", "z", "x"), pairs))
+        if d * 2 < rows:
+            got = split_packed(lax.ppermute(pack(*total), ("win", "z", "x"), pairs))
+        else:
+            moved = lax.ppermute(pack_dense(*total), ("win", "z", "x"), pairs)
+            got = split_dense(moved, per_part)
         entering = combine(got, entering)
         if d * 2 < rows:
             total = combine(got, total)

time: 203 us -> 202 us (level)
    ppermute x0 -> x1, starting transfers between devices: none -> 7.83 us  [scan_states(): moved = lax.ppermute(pack_dense(*total), ('win', 'z', 'x'), pairs)]
    ppermute x3 -> x2, starting transfers between devices: 19.1 us -> 11.7 us  [scan_states(): got = split_packed(lax.ppermute(pack(*total), ('win', 'z', 'x'), pairs))]
    ppermute x3 -> x2, waiting for transfers between devices: 15.5 us -> 9.19 us  [scan_states(): got = split_packed(lax.ppermute(pack(*total), ('win', 'z', 'x'), pairs))]
    ppermute x0 -> x1, waiting for transfers between devices: none -> 5.92 us  [scan_states(): moved = lax.ppermute(pack_dense(*total), ('win', 'z', 'x'), pairs)]
    all_gather x1, waiting for transfers between devices: 4.53 us -> 8.75 us  [gather_weight(): row = lax.all_gather(mine, 'x', axis=1)]
    all_to_all x1, starting transfers between devices: 21 us -> 18.4 us  [scan_states(): back = lax.all_to_all(out, 'x', 0, 0, tiled=True)]
    all_to_all x1, waiting for transfers between devices: 14.9 us -> 12.6 us  [scan_states(): back = lax.all_to_all(out, 'x', 0, 0, tiled=True)]
    unnamed x41 -> x37, local copies, waits for them, and re-layouts: 9.18 us -> 9.56 us
  transfers between devices with their start and end apart: 9 -> 9, of which waited for: 7 -> 7; matrix products, arithmetic and copies ran while one was open for 16% -> 17% of each run, Pallas kernels for 0% -> 0%
where the time goes in v14:
time: 202 us; the launch traced here: 201 us
  waiting for transfers between devices  82.2 us (41%)
  starting transfers between devices  53.7 us (27%)
  other arithmetic  18.5 us (9%)
  local copies, waits for them, and re-layouts  16.4 us (8%)
  matrix products  15.9 us (8%)
  between operations  13.8 us (7%)
    all_to_all x1, waiting for transfers between devices, scan_states(): mine = lax.all_to_all(send, 'x', 0, 0, tiled=True)  20 us
    all_to_all x1, starting transfers between devices, scan_states(): back = lax.all_to_all(out, 'x', 0, 0, tiled=True)  18.4 us
    all_gather x1, waiting for transfers between devices, gather_weight(): column = lax.all_gather(output_weight, 'z', axis=0)  16.5 us
    all_to_all x1, waiting for transfers between devices, scan_states(): back = lax.all_to_all(out, 'x', 0, 0, tiled=True)  12.6 us
    ppermute x2, starting transfers between devices, scan_states(): got = split_packed(lax.ppermute(pack(*total), ('win', 'z', 'x'), pairs))  11.7 us
    unnamed x37, local copies, waits for them, and re-layouts  9.56 us
    ppermute x1, starting transfers between devices, per_device(): partner = lax.ppermute(projected_rows, ('win', 'z'), pairs)  9.37 us
    ppermute x2, waiting for transfers between devices, scan_states(): got = split_packed(lax.ppermute(pack(*total), ('win', 'z', 'x'), pairs))  9.19 us
  transfers between devices with their start and end apart: 9, of which 7 were waited for; matrix products, arithmetic and copies ran while one was open for 17% of the time, Pallas kernels for 0%

profile of v14, /device:TPU:24, one launch (start us, length us, event | category | flops | bytes accessed | tf_op | source)
XLA Modules:
  0.0 200.5 jit_solution(16309955962915091265)
XLA Ops:
  6.5 0.8 compare_select_fusion
  7.3 0.7 multiply_bitcast_fusion
  8.3 0.2 reduce_window_sum.17
  8.5 0.2 reduce_window_sum.18
  8.7 0.7 fusion.51
  9.5 1.3 copy.103
  10.8 0.8 bitcast_convert_fusion
  11.7 0.8 convolution_bitcast_fusion.4
  12.5 0.8 convolution_bitcast_fusion.3
  13.5 0.2 pad_maximum_fusion
  13.7 0.2 fusion.48
  13.9 1.7 maximum_select_fusion
  15.5 4.4 %all-to-all-start = ((f32[4,16,72,128]{3,2,1,0:T(8,128)}), f32[4,16,72,128]{3,2,1,0:T(8,128)S(1)}, u32[]{:S(2)}, u32[]{:S(2)}) async-start(f32[4,16,72,128]{3,2,1,0:T(8,128)} %maximum_select_fusion), calls=%async_computation | async-start | bytes 4718592 | tf_op jit(solution)/shard_map/all_to_all | solution.py:79
  20.0 0.7 all-gather.5.cloned.1.call-update
  21.0 8.2 %while.11 = (s32[]{:T(128)}, f32[8,128,4,64]{1,3,2,0:T(8,128)}, bf16[8,128,4,64]{1,3,2,0:T(8,128)(2,1)S(1)}, f32[128,128]{1,0:T(8,128)S(1)}, f32[8,4,128]{2,1,0:...) while((s32[]{:T(128)}, f32[8,128,4,64]{1,3,2,0:T(8,128)}, ...), condition=%wide.region_4.5_spmd.clone, body=%wide.region_3.4_spmd.clone.sunk | while | flops 8732674 | bytes 312401 | solution.py:198
  21.0 1.0 fusion.61
  22.0 1.0 fusion.61
  23.1 1.0 fusion.61
  24.1 1.0 fusion.61
  25.1 1.0 fusion.61
  26.1 1.0 fusion.61
  27.1 1.0 fusion.61
  28.1 1.0 fusion.61
  29.2 20.0 %all-to-all-done = f32[4,16,72,128]{3,2,1,0:T(8,128)S(1)} async-done(((f32[4,16,72,128]{3,2,1,0:T(8,128)}), f32[4,16,72,128]{3,2,1,0:T(8,128)S(1)}, u32[]{:S(2)}, u32[]{:S(2)}) %all-to-all-start) | async-done | bytes 2359328 | tf_op jit(solution)/shard_map/all_to_all | solution.py:79
  49.1 1.4 copy-done.1
  50.5 2.6 %reverse_select_fusion = f32[4,16,72,128]{3,2,1,0:T(8,128)S(1)} fusion(f32[4,16,72,128]{3,2,1,0:T(8,128)} %copy-done.1, pred[]{:T(512)S(6)} %xor.3), kind=kLoop, calls=%fused_computation.16 | loop fusion | flops 589824 | bytes 4718593 | tf_op jit(solution)/shard_map/jit(_where)/select_n | solution.py:82
  53.2 0.8 exponential_reduce_fusion
  54.0 1.0 fusion.26
  55.1 3.9 %collective-permute-start = (f32[16,72,128]{2,1,0:T(8,128)S(1)}, f32[16,72,128]{2,1,0:T(8,128)S(1)}, u32[]{:S(2)}, u32[]{:S(2)}) collective-permute-start(f32[16,72,128]{2,1,0:T(8,128)S(1)} %pad_maximum_fusion.2), channel_id=1, source_target_pairs={{0,4},{1,5},{4,8},{5,9},{6,2},{7,3},{8,12},{9,13},{10,6},{11,7},{1... | collective-permute-start | bytes 1769480 | tf_op jit(solution)/shard_map/ppermute | solution.py:103
  59.0 9.2 %collective-permute-done = f32[16,72,128]{2,1,0:T(8,128)S(1)} collective-permute-done((f32[16,72,128]{2,1,0:T(8,128)S(1)}, f32[16,72,128]{2,1,0:T(8,128)S(1)}, u32[]{:S(2)}, u32[]{:S(2)}) %collective-permute-start) | collective-permute-done | bytes 589856 | tf_op jit(solution)/shard_map/ppermute | solution.py:103
  68.2 0.8 copy-done.4
  69.1 1.2 multiply_add_fusion.1
  70.4 0.9 pad_maximum_fusion.3
  71.3 7.8 %collective-permute-start.1 = (f32[16,72,128]{2,1,0:T(8,128)}, f32[16,72,128]{2,1,0:T(8,128)S(1)}, u32[]{:S(2)}, u32[]{:S(2)}) collective-permute-start(f32[16,72,128]{2,1,0:T(8,128)} %pad_maximum_fusion.3), channel_id=1, source_target_pairs={{0,8},{1,9},{4,12},{5,13},{8,16},{9,17},{10,2},{11,3},{12,20},{13,... | collective-permute-start | bytes 1769480 | tf_op jit(solution)/shard_map/ppermute | solution.py:103
  79.1 16.5 %all-gather.5.cloned.1.call-done = bf16[16384,32]{0,1:T(8,128)(2,1)} async-done(((bf16[2048,32]{0,1:T(8,128)(2,1)}), bf16[16384,32]{0,1:T(8,128)(2,1)}) %all-gather.5.cloned.1.call-update) | async-done | bytes 1048592 | tf_op jit(solution)/shard_map/all_gather | solution.py:122
  95.6 2.8 %copy.124 = bf16[4,8,8,2048]{3,2,1,0:T(8,128)(2,1)} copy(bf16[4,8,8,2048]{3,1,2,0:T(8,128)(2,1)} %bitcast.185) | data formatting | bytes 2097152
  98.6 0.6 copy-done.6
  99.2 0.8 pad_maximum_fusion.4
  100.0 7.8 %collective-permute-start.2 = (f32[1032,128]{1,0:T(8,128)}, f32[1032,128]{1,0:T(8,128)S(1)}, u32[]{:S(2)}, u32[]{:S(2)}) collective-permute-start(f32[1032,128]{1,0:T(8,128)} %pad_maximum_fusion.4), channel_id=1, source_target_pairs={{0,16},{1,17},{4,20},{5,21},{8,24},{9,25},{12,28},{13,29},{18,2},{... | collective-permute-start | bytes 1585160 | tf_op jit(solution)/shard_map/ppermute | solution.py:105
  108.0 1.1 copy.122
  109.1 5.9 %collective-permute-done.2 = f32[1032,128]{1,0:T(8,128)S(1)} collective-permute-done((f32[1032,128]{1,0:T(8,128)}, f32[1032,128]{1,0:T(8,128)S(1)}, u32[]{:S(2)}, u32[]{:S(2)}) %collective-permute-start.2) | collective-permute-done | bytes 528416 | tf_op jit(solution)/shard_map/ppermute | solution.py:105
  115.1 1.3 add_bitcast_fusion.2
  116.4 0.2 add_bitcast_fusion.1
  116.6 0.2 pad_maximum_fusion.1
  116.8 1.5 reverse_select_fusion.1
  118.4 18.4 %all-to-all-start.1 = ((f32[4,16,64,128]{3,2,1,0:T(8,128)}), f32[4,16,64,128]{3,2,1,0:T(8,128)S(1)}, u32[]{:S(2)}, u32[]{:S(2)}) async-start(f32[4,16,64,128]{3,2,1,0:T(8,128)} %reverse_select_fusion.1), calls=%async_computation.1 | async-start | bytes 4194304 | tf_op jit(solution)/shard_map/all_to_all | solution.py:113
  136.8 1.3 copy.111
  138.2 0.6 dynamic_slice.23
  138.7 0.7 iota_compare_fusion.1
  139.5 8.7 %all-gather.7.cloned.1.call-done = bf16[8,4096,32]{1,2,0:T(8,128)(2,1)} async-done(((bf16[8,1024,32]{1,2,0:T(8,128)(2,1)}), bf16[8,4096,32]{1,2,0:T(8,128)(2,1)}) %all-gather.7.cloned.1.call-update) | async-done | bytes 2097168 | tf_op jit(solution)/shard_map/all_gather | solution.py:124
  148.2 3.2 %copy.127 = bf16[8,4,4,8,1024]{4,3,1,2,0:T(8,128)(2,1)} copy(bf16[8,4,4,8,1024]{4,3,2,1,0:T(8,128)(2,1)} %bitcast.179) | data formatting | bytes 4194304 | tf_op jit(solution)/shard_map/all_gather | solution.py:124
  151.4 1.9 collective-permute-start.3
  153.3 12.6 %all-to-all-done.1 = f32[4,16,64,128]{3,2,1,0:T(8,128)S(1)} async-done(((f32[4,16,64,128]{3,2,1,0:T(8,128)}), f32[4,16,64,128]{3,2,1,0:T(8,128)S(1)}, u32[]{:S(2)}, u32[]{:S(2)}) %all-to-all-start.1) | async-done | bytes 2097184 | tf_op jit(solution)/shard_map/all_to_all | solution.py:113
  166.1 0.4 maximum_select_fusion.1
  166.6 1.1 copy-done.7
  167.7 0.6 fusion.15
  168.3 0.8 multiply_reduce_fusion
  169.4 0.3 copy.112
  169.7 0.2 copy-done.10
  170.0 2.3 %fusion.32 = f32[128,8,4,32]{0,3,2,1:T(8,128)S(1)} fusion(bf16[128,2048]{1,0:T(8,128)(2,1)S(1)} %multiply_convert_fusion.6, s32[]{:T(128)S(6)} %select_n.86, bf16[8,4,4,8,1024]{4,3,2,1,0:T(8,128)(2,1)} %bitcast.180), kind=kOutput, calls=%fused_computation.71 | convolution fusion | flops 268435456 | bytes 2883588 | tf_op jit(solution)/shard_map/tr,zxrc->tzxc/dot_general | solution.py:136
  172.3 2.3 %fusion.17 = bf16[128,8,4,32]{0,3,2,1:T(8,128)(2,1)S(1)} fusion(f32[128,8,4,32]{0,3,2,1:T(8,128)S(1)} %fusion.32, bf16[8,4,1024,32]{2,3,1,0:T(8,128)(2,1)} %collective-permute-done.3, bf16[128,2048]{1,0:T(8,128)(2,1)S(1)} %multiply_convert_fusion.6, s32[]{:T(128)S(6)} %select_n.87), kind=kOutput, calls=%fused_computation.35 | convolution fusion | flops 268697600 | bytes 3145732 | tf_op jit(solution)/shard_map/tr,zxrc->tzxc/dot_general | solution.py:137
  174.8 9.4 %collective-permute-start.4 = (bf16[128,1024]{1,0:T(8,128)(2,1)S(1)}, bf16[128,1024]{1,0:T(8,128)(2,1)S(1)}, u32[]{:S(2)}, u32[]{:S(2)}) collective-permute-start(bf16[128,1024]{1,0:T(8,128)(2,1)S(1)} %copy.116), channel_id=1, source_target_pairs={{28,32},{32,28},{60,64},{64,60},{92,96},{96,92},{124,128},{128,124... | collective-permute-start | bytes 786440 | tf_op jit(solution)/shard_map/ppermute | solution.py:226
  184.3 8.5 %collective-permute-done.4 = bf16[128,1024]{1,0:T(8,128)(2,1)S(1)} collective-permute-done((bf16[128,1024]{1,0:T(8,128)(2,1)S(1)}, bf16[128,1024]{1,0:T(8,128)(2,1)S(1)}, u32[]{:S(2)}, u32[]{:S(2)}) %collective-permute-start.4) | collective-permute-done | bytes 262176 | tf_op jit(solution)/shard_map/ppermute | solution.py:226
  192.8 0.9 fusion.30
  (90 shorter events, 2.7 us)
Async XLA Ops:
  6.5 14.3 %copy-start = (bf16[1,128,128]{2,1,0:T(8,128)(2,1)S(1)}, bf16[1,128,128]{2,1,0:T(8,128)(2,1)}, u32[]{:S(2)}) copy-start(bf16[1,128,128]{2,1,0:T(8,128)(2,1)} %param.14) | copy-start | bytes 98308
  15.5 5.3 %copy-start.9 = (bf16[1,128,128]{2,1,0:T(8,128)(2,1)S(1)}, bf16[1,128,128]{2,1,0:T(8,128)(2,1)}, u32[]{:S(2)}) copy-start(bf16[1,128,128]{2,1,0:T(8,128)(2,1)} %param.13) | copy-start | bytes 98308
  15.5 33.6 %all-to-all-start = ((f32[4,16,72,128]{3,2,1,0:T(8,128)}), f32[4,16,72,128]{3,2,1,0:T(8,128)S(1)}, u32[]{:S(2)}, u32[]{:S(2)}) async-start(f32[4,16,72,128]{3,2,1,0:T(8,128)} %maximum_select_fusion), calls=%async_computation | async-start | bytes 4718592 | tf_op jit(solution)/shard_map/all_to_all | solution.py:79
  20.0 75.6 %all-gather.5.cloned.1.call-start = ((), (), s32[]{:S(2)}) async-start(), calls=%async_computation.2 | async-start | bytes 1179648 | tf_op jit(solution)/shard_map/all_gather | solution.py:122
  20.7 127.5 %all-gather.7.cloned.1.call-start = ((), (), s32[]{:S(2)}) async-start(), calls=%async_computation.3 | async-start | bytes 2621440 | tf_op jit(solution)/shard_map/all_gather | solution.py:124
  49.1 1.4 copy-start.1
  54.0 1.2 copy-start.12
  54.0 1.2 copy-start.14
  55.1 13.1 %collective-permute-start = (f32[16,72,128]{2,1,0:T(8,128)S(1)}, f32[16,72,128]{2,1,0:T(8,128)S(1)}, u32[]{:S(2)}, u32[]{:S(2)}) collective-permute-start(f32[16,72,128]{2,1,0:T(8,128)S(1)} %pad_maximum_fusion.2), channel_id=1, source_target_pairs={{0,4},{1,5},{4,8},{5,9},{6,2},{7,3},{8,12},{9,13},{10,6},{11,7},{1... | collective-permute-start | bytes 1769480 | tf_op jit(solution)/shard_map/ppermute | solution.py:103
  68.2 0.8 copy-start.4
  71.3 27.1 %collective-permute-start.1 = (f32[16,72,128]{2,1,0:T(8,128)}, f32[16,72,128]{2,1,0:T(8,128)S(1)}, u32[]{:S(2)}, u32[]{:S(2)}) collective-permute-start(f32[16,72,128]{2,1,0:T(8,128)} %pad_maximum_fusion.3), channel_id=1, source_target_pairs={{0,8},{1,9},{4,12},{5,13},{8,16},{9,17},{10,2},{11,3},{12,20},{13,... | collective-permute-start | bytes 1769480 | tf_op jit(solution)/shard_map/ppermute | solution.py:103
  98.4 0.8 copy-start.6
  98.5 9.4 %copy-start.2 = (bf16[4,8,8,2048]{3,2,1,0:T(8,128)(2,1)S(1)}, bf16[4,8,8,2048]{3,2,1,0:T(8,128)(2,1)}, u32[]{:S(2)}) copy-start(bf16[4,8,8,2048]{3,2,1,0:T(8,128)(2,1)} %copy.124) | copy-start | bytes 3145732
  100.0 15.0 %copy-start.5 = (f32[16,72,128]{2,1,0:T(8,128)S(1)}, f32[16,72,128]{2,1,0:T(8,128)}, u32[]{:S(2)}) copy-start(f32[16,72,128]{2,1,0:T(8,128)} %copy-done.4) | copy-start | bytes 1769476
  100.0 15.0 %copy-start.13 = (f32[16]{0:T(128)S(1)}, f32[16]{0:T(128)}, u32[]{:S(2)}) copy-start(f32[16]{0:T(128)} %copy-done.12) | copy-start | bytes 196
  100.0 15.0 %collective-permute-start.2 = (f32[1032,128]{1,0:T(8,128)}, f32[1032,128]{1,0:T(8,128)S(1)}, u32[]{:S(2)}, u32[]{:S(2)}) collective-permute-start(f32[1032,128]{1,0:T(8,128)} %pad_maximum_fusion.4), channel_id=1, source_target_pairs={{0,16},{1,17},{4,20},{5,21},{8,24},{9,25},{12,28},{13,29},{18,2},{... | collective-permute-start | bytes 1585160 | tf_op jit(solution)/shard_map/ppermute | solution.py:105
  109.1 7.3 %copy-start.3 = (f32[16,64,128]{2,1,0:T(8,128)S(1)}, f32[16,64,128]{2,1,0:T(8,128)}, u32[]{:S(2)}) copy-start(f32[16,64,128]{2,1,0:T(8,128)} %get-tuple-element.89) | copy-start | bytes 1572868
  109.1 7.3 %copy-start.11 = (f32[16]{0:T(128)S(1)}, f32[16]{0:T(128)}, u32[]{:S(2)}) copy-start(f32[16]{0:T(128)} %get-tuple-element.73) | copy-start | bytes 196
  118.4 18.4 %copy-start.8 = (f32[128,32]{1,0:T(8,128)S(1)}, f32[128,32]{1,0:T(8,128)}, u32[]{:S(2)}) copy-start(f32[128,32]{1,0:T(8,128)} %get-tuple-element.100) | copy-start | bytes 49156
  118.4 19.8 %copy-start.15 = (s32[16]{0:T(128)S(1)}, s32[16]{0:T(128)}, u32[]{:S(2)}) copy-start(s32[16]{0:T(128)} %param.19) | copy-start | bytes 196
  118.4 47.6 %all-to-all-start.1 = ((f32[4,16,64,128]{3,2,1,0:T(8,128)}), f32[4,16,64,128]{3,2,1,0:T(8,128)S(1)}, u32[]{:S(2)}, u32[]{:S(2)}) async-start(f32[4,16,64,128]{3,2,1,0:T(8,128)} %reverse_select_fusion.1), calls=%async_computation.1 | async-start | bytes 4194304 | tf_op jit(solution)/shard_map/all_to_all | solution.py:113
  151.4 20.9 %collective-permute-start.3 = (bf16[8,4,1024,32]{2,3,1,0:T(8,128)(2,1)}, bf16[8,4,1024,32]{2,3,1,0:T(8,128)(2,1)}, u32[]{:S(2)}, u32[]{:S(2)}) collective-permute-start(bf16[8,4,1024,32]{2,3,1,0:T(8,128)(2,1)} %bitcast.162), channel_id=1, source_target_pairs={{0,32},{32,0},{64,96},{96,64},{128,160},{160,128},{192,224},{224,1... | collective-permute-start | bytes 6291464 | tf_op jit(solution)/shard_map/ppermute | solution.py:127
  166.5 1.2 copy-start.7
  169.2 0.7 copy-start.10
  174.8 18.0 %collective-permute-start.4 = (bf16[128,1024]{1,0:T(8,128)(2,1)S(1)}, bf16[128,1024]{1,0:T(8,128)(2,1)S(1)}, u32[]{:S(2)}, u32[]{:S(2)}) collective-permute-start(bf16[128,1024]{1,0:T(8,128)(2,1)S(1)} %copy.116), channel_id=1, source_target_pairs={{28,32},{32,28},{60,64},{64,60},{92,96},{96,92},{124,128},{128,124... | collective-permute-start | bytes 786440 | tf_op jit(solution)/shard_map/ppermute | solution.py:226
Sparse Core Ops, SparseCore 0:
  22.9 72.6 all-gather.4
  109.2 38.9 all-gather.6

commit v15 on v14

--- a/solution.py
+++ b/solution.py
@@ -121,7 +121,7 @@
     half_rows = output_weight.shape[0] // 2
     column = lax.all_gather(output_weight, "z", axis=0)
     mine = lax.dynamic_slice_in_dim(column, half * half_rows, half_rows, axis=1)
-    row = lax.all_gather(mine, "x", axis=1)
+    row = lax.all_gather(mine, "x", axis=2, tiled=True)
     wins = lax.axis_size("win")
     pairs = [(w, w ^ 1) for w in range(wins)]
     other = lax.ppermute(row, "win", pairs)
@@ -130,11 +130,11 @@
 
 def project(normed, gathered):
     row, other, half = gathered
-    half_rows = row.shape[2]
+    half_rows = row.shape[1]
     mine_cols = lax.dynamic_slice_in_dim(normed, half * half_rows, half_rows, axis=1)
     other_cols = lax.dynamic_slice_in_dim(normed, (1 - half) * half_rows, half_rows, axis=1)
-    out = jnp.einsum("tr,zxrc->tzxc", mine_cols, row, preferred_element_type=jnp.float32)
-    out = out + jnp.einsum("tr,zxrc->tzxc", other_cols, other, preferred_element_type=jnp.float32)
+    out = jnp.einsum("tr,zrk->tzk", mine_cols, row, preferred_element_type=jnp.float32)
+    out = out + jnp.einsum("tr,zrk->tzk", other_cols, other, preferred_element_type=jnp.float32)
     return out.reshape(normed.shape[0], -1)
 
 

time: 202 us -> 202 us (level)
  waiting for transfers between devices: 82.2 us -> 85.4 us
  local copies, waits for them, and re-layouts: 16.4 us -> 13.3 us
    dot_general x2 -> x0, matrix products: 4.63 us -> none  [the longest x1 2.32 us: project(): jnp.einsum('tr,zxrc->tzxc', other_cols, other, preferred_element_type=jnp...]
    unnamed x0 -> x2, matrix products: none -> 4.62 us
    all_to_all x1, waiting for transfers between devices: 12.6 us -> 15.8 us  [scan_states(): back = lax.all_to_all(out, 'x', 0, 0, tiled=True)]
    all_gather x1 -> x0, local copies, waits for them, and re-layouts: 3.16 us -> none  [gather_weight(): row = lax.all_gather(mine, 'x', axis=1)]
  transfers between devices with their start and end apart: 9 -> 9, of which waited for: 7 -> 7; matrix products, arithmetic and copies ran while one was open for 17% -> 15% of each run, Pallas kernels for 0% -> 0%
where the time goes in v15:
time: 202 us; the launch traced here: 201 us
  waiting for transfers between devices  85.4 us (42%)
  starting transfers between devices  53.6 us (27%)
  other arithmetic  18.6 us (9%)
  matrix products  15.9 us (8%)
  between operations  13.9 us (7%)
  local copies, waits for them, and re-layouts  13.3 us (7%)
    all_to_all x1, waiting for transfers between devices, scan_states(): mine = lax.all_to_all(send, 'x', 0, 0, tiled=True)  20 us
    all_to_all x1, starting transfers between devices, scan_states(): back = lax.all_to_all(out, 'x', 0, 0, tiled=True)  18.6 us
    all_gather x1, waiting for transfers between devices, gather_weight(): column = lax.all_gather(output_weight, 'z', axis=0)  16.6 us
    all_to_all x1, waiting for transfers between devices, scan_states(): back = lax.all_to_all(out, 'x', 0, 0, tiled=True)  15.8 us
    ppermute x2, starting transfers between devices, scan_states(): got = split_packed(lax.ppermute(pack(*total), ('win', 'z', 'x'), pairs))  11.6 us
    unnamed x37, local copies, waits for them, and re-layouts  9.54 us
    ppermute x1, starting transfers between devices, per_device(): partner = lax.ppermute(projected_rows, ('win', 'z'), pairs)  9.36 us
    ppermute x2, waiting for transfers between devices, scan_states(): got = split_packed(lax.ppermute(pack(*total), ('win', 'z', 'x'), pairs))  9.17 us
  transfers between devices with their start and end apart: 9, of which 7 were waited for; matrix products, arithmetic and copies ran while one was open for 15% of the time, Pallas kernels for 0%

profile of v15, /device:TPU:24, one launch (start us, length us, event | category | flops | bytes accessed | tf_op | source)
XLA Modules:
  0.0 200.6 jit_solution(15753105272997334633)
XLA Ops:
  6.5 0.8 compare_select_fusion
  7.3 0.7 multiply_bitcast_fusion
  8.3 0.2 reduce_window_sum.17
  8.5 0.2 reduce_window_sum.18
  8.7 0.7 fusion.49
  9.5 1.3 copy.95
  10.8 0.8 bitcast_convert_fusion
  11.7 0.8 convolution_bitcast_fusion.4
  12.5 0.8 convolution_bitcast_fusion.3
  13.5 0.2 pad_maximum_fusion
  13.7 0.2 fusion.46
  13.9 1.7 maximum_select_fusion
  15.5 4.4 %all-to-all-start = ((f32[4,16,72,128]{3,2,1,0:T(8,128)}), f32[4,16,72,128]{3,2,1,0:T(8,128)S(1)}, u32[]{:S(2)}, u32[]{:S(2)}) async-start(f32[4,16,72,128]{3,2,1,0:T(8,128)} %maximum_select_fusion), calls=%async_computation | async-start | bytes 4718592 | tf_op jit(solution)/shard_map/all_to_all | solution.py:79
  20.0 0.7 all-gather.6.cloned.1.call-update
  21.0 8.2 %while.11 = (s32[]{:T(128)}, f32[8,128,4,64]{1,3,2,0:T(8,128)}, bf16[8,128,4,64]{1,3,2,0:T(8,128)(2,1)S(1)}, f32[128,128]{1,0:T(8,128)S(1)}, f32[8,4,128]{2,1,0:...) while((s32[]{:T(128)}, f32[8,128,4,64]{1,3,2,0:T(8,128)}, ...), condition=%wide.region_4.5_spmd.clone, body=%wide.region_3.4_spmd.clone.sunk | while | flops 8732674 | bytes 312401 | solution.py:198
  21.0 1.0 fusion.60
  22.0 1.0 fusion.60
  23.1 1.0 fusion.60
  24.1 1.0 fusion.60
  25.1 1.0 fusion.60
  26.1 1.0 fusion.60
  27.1 1.0 fusion.60
  28.2 1.0 fusion.60
  29.2 20.0 %all-to-all-done = f32[4,16,72,128]{3,2,1,0:T(8,128)S(1)} async-done(((f32[4,16,72,128]{3,2,1,0:T(8,128)}), f32[4,16,72,128]{3,2,1,0:T(8,128)S(1)}, u32[]{:S(2)}, u32[]{:S(2)}) %all-to-all-start) | async-done | bytes 2359328 | tf_op jit(solution)/shard_map/all_to_all | solution.py:79
  49.1 1.4 copy-done.1
  50.5 2.6 %reverse_select_fusion = f32[4,16,72,128]{3,2,1,0:T(8,128)S(1)} fusion(f32[4,16,72,128]{3,2,1,0:T(8,128)} %copy-done.1, pred[]{:T(512)S(6)} %xor.3), kind=kLoop, calls=%fused_computation.16 | loop fusion | flops 589824 | bytes 4718593 | tf_op jit(solution)/shard_map/jit(_where)/select_n | solution.py:82
  53.2 0.8 exponential_reduce_fusion
  54.0 1.0 fusion.25
  55.2 3.9 %collective-permute-start = (f32[16,72,128]{2,1,0:T(8,128)S(1)}, f32[16,72,128]{2,1,0:T(8,128)S(1)}, u32[]{:S(2)}, u32[]{:S(2)}) collective-permute-start(f32[16,72,128]{2,1,0:T(8,128)S(1)} %pad_maximum_fusion.2), channel_id=1, source_target_pairs={{0,4},{1,5},{4,8},{5,9},{6,2},{7,3},{8,12},{9,13},{10,6},{11,7},{1... | collective-permute-start | bytes 1769480 | tf_op jit(solution)/shard_map/ppermute | solution.py:103
  59.0 9.2 %collective-permute-done = f32[16,72,128]{2,1,0:T(8,128)S(1)} collective-permute-done((f32[16,72,128]{2,1,0:T(8,128)S(1)}, f32[16,72,128]{2,1,0:T(8,128)S(1)}, u32[]{:S(2)}, u32[]{:S(2)}) %collective-permute-start) | collective-permute-done | bytes 589856 | tf_op jit(solution)/shard_map/ppermute | solution.py:103
  68.2 0.8 copy-done.4
  69.1 1.2 multiply_add_fusion.1
  70.4 0.9 pad_maximum_fusion.3
  71.3 7.8 %collective-permute-start.1 = (f32[16,72,128]{2,1,0:T(8,128)}, f32[16,72,128]{2,1,0:T(8,128)S(1)}, u32[]{:S(2)}, u32[]{:S(2)}) collective-permute-start(f32[16,72,128]{2,1,0:T(8,128)} %pad_maximum_fusion.3), channel_id=1, source_target_pairs={{0,8},{1,9},{4,12},{5,13},{8,16},{9,17},{10,2},{11,3},{12,20},{13,... | collective-permute-start | bytes 1769480 | tf_op jit(solution)/shard_map/ppermute | solution.py:103
  79.0 16.6 %all-gather.6.cloned.1.call-done = bf16[16384,32]{0,1:T(8,128)(2,1)} async-done(((bf16[2048,32]{0,1:T(8,128)(2,1)}), bf16[16384,32]{0,1:T(8,128)(2,1)}) %all-gather.6.cloned.1.call-update) | async-done | bytes 1048592 | tf_op jit(solution)/shard_map/all_gather | solution.py:122
  95.7 2.8 %copy.111 = bf16[4,8,8,2048]{3,2,1,0:T(8,128)(2,1)} copy(bf16[4,8,8,2048]{3,1,2,0:T(8,128)(2,1)} %bitcast.181) | data formatting | bytes 2097152
  98.7 0.6 copy-done.6
  99.3 0.8 pad_maximum_fusion.4
  100.1 7.7 %collective-permute-start.2 = (f32[1032,128]{1,0:T(8,128)}, f32[1032,128]{1,0:T(8,128)S(1)}, u32[]{:S(2)}, u32[]{:S(2)}) collective-permute-start(f32[1032,128]{1,0:T(8,128)} %pad_maximum_fusion.4), channel_id=1, source_target_pairs={{0,16},{1,17},{4,20},{5,21},{8,24},{9,25},{12,28},{13,29},{18,2},{... | collective-permute-start | bytes 1585160 | tf_op jit(solution)/shard_map/ppermute | solution.py:105
  107.9 1.1 copy.110
  109.0 5.9 %collective-permute-done.2 = f32[1032,128]{1,0:T(8,128)S(1)} collective-permute-done((f32[1032,128]{1,0:T(8,128)}, f32[1032,128]{1,0:T(8,128)S(1)}, u32[]{:S(2)}, u32[]{:S(2)}) %collective-permute-start.2) | collective-permute-done | bytes 528416 | tf_op jit(solution)/shard_map/ppermute | solution.py:105
  115.0 1.3 add_bitcast_fusion.2
  116.3 0.2 add_bitcast_fusion.1
  116.5 0.2 pad_maximum_fusion.1
  116.8 1.5 reverse_select_fusion.1
  118.3 18.6 %all-to-all-start.1 = ((f32[4,16,64,128]{3,2,1,0:T(8,128)}), f32[4,16,64,128]{3,2,1,0:T(8,128)S(1)}, u32[]{:S(2)}, u32[]{:S(2)}) async-start(f32[4,16,64,128]{3,2,1,0:T(8,128)} %reverse_select_fusion.1), calls=%async_computation.1 | async-start | bytes 4194304 | tf_op jit(solution)/shard_map/all_to_all | solution.py:113
  136.9 1.3 copy.103
  138.2 0.6 dynamic_slice.23
  138.8 0.7 iota_compare_fusion.1
  139.6 8.6 %all-gather.4.cloned.1.call-done = bf16[8,1024,128]{1,2,0:T(8,128)(2,1)} async-done(((bf16[8,1024,32]{1,2,0:T(8,128)(2,1)}), bf16[8,1024,128]{1,2,0:T(8,128)(2,1)}) %all-gather.4.cloned.1.call-update) | async-done | bytes 2097168 | tf_op jit(solution)/shard_map/all_gather | solution.py:124
  148.2 1.9 collective-permute-start.3
  150.1 15.8 %all-to-all-done.1 = f32[4,16,64,128]{3,2,1,0:T(8,128)S(1)} async-done(((f32[4,16,64,128]{3,2,1,0:T(8,128)}), f32[4,16,64,128]{3,2,1,0:T(8,128)S(1)}, u32[]{:S(2)}, u32[]{:S(2)}) %all-to-all-start.1) | async-done | bytes 2097184 | tf_op jit(solution)/shard_map/all_to_all | solution.py:113
  166.1 0.4 maximum_select_fusion.1
  166.6 1.1 copy-done.7
  167.7 0.6 fusion.15
  168.3 0.8 multiply_reduce_fusion
  169.3 0.3 copy.104
  169.7 0.2 copy-done.10
  170.0 2.3 %fusion.32 = f32[128,1024]{0,1:S(1)} fusion(bf16[1024,1024]{0,1:T(8,128)(2,1)} %bitcast.173, bf16[128,2048]{1,0:T(8,128)(2,1)S(1)} %multiply_convert_fusion.6, s32[]{:T(128)S(6)} %select_n.86), kind=kOutput, calls=%fused_computation.70 | convolution fusion | flops 268435456 | bytes 2883588
  172.3 2.3 %fusion.30 = f32[128,1024]{0,1:S(1)} fusion(bf16[1024,1024]{0,1:T(8,128)(2,1)} %bitcast.52, bf16[128,2048]{1,0:T(8,128)(2,1)S(1)} %multiply_convert_fusion.6, s32[]{:T(128)S(6)} %select_n.87), kind=kOutput, calls=%fused_computation.68 | convolution fusion | flops 268435456 | bytes 2883588
  174.7 0.1 copy.106
  174.8 9.4 %collective-permute-start.4 = (bf16[128,1024]{1,0:T(8,128)(2,1)S(1)}, bf16[128,1024]{1,0:T(8,128)(2,1)S(1)}, u32[]{:S(2)}, u32[]{:S(2)}) collective-permute-start(bf16[128,1024]{1,0:T(8,128)(2,1)S(1)} %copy.106), channel_id=1, source_target_pairs={{28,32},{32,28},{60,64},{64,60},{92,96},{96,92},{124,128},{128,124... | collective-permute-start | bytes 786440 | tf_op jit(solution)/shard_map/ppermute | solution.py:226
  184.3 8.5 %collective-permute-done.4 = bf16[128,1024]{1,0:T(8,128)(2,1)S(1)} collective-permute-done((bf16[128,1024]{1,0:T(8,128)(2,1)S(1)}, bf16[128,1024]{1,0:T(8,128)(2,1)S(1)}, u32[]{:S(2)}, u32[]{:S(2)}) %collective-permute-start.4) | collective-permute-done | bytes 262176 | tf_op jit(solution)/shard_map/ppermute | solution.py:226
  192.8 0.9 fusion.29
  (90 shorter events, 2.6 us)
Async XLA Ops:
  6.5 14.3 %copy-start = (bf16[1,128,128]{2,1,0:T(8,128)(2,1)S(1)}, bf16[1,128,128]{2,1,0:T(8,128)(2,1)}, u32[]{:S(2)}) copy-start(bf16[1,128,128]{2,1,0:T(8,128)(2,1)} %param.14) | copy-start | bytes 98308
  15.5 5.3 %copy-start.9 = (bf16[1,128,128]{2,1,0:T(8,128)(2,1)S(1)}, bf16[1,128,128]{2,1,0:T(8,128)(2,1)}, u32[]{:S(2)}) copy-start(bf16[1,128,128]{2,1,0:T(8,128)(2,1)} %param.13) | copy-start | bytes 98308
  15.5 33.6 %all-to-all-start = ((f32[4,16,72,128]{3,2,1,0:T(8,128)}), f32[4,16,72,128]{3,2,1,0:T(8,128)S(1)}, u32[]{:S(2)}, u32[]{:S(2)}) async-start(f32[4,16,72,128]{3,2,1,0:T(8,128)} %maximum_select_fusion), calls=%async_computation | async-start | bytes 4718592 | tf_op jit(solution)/shard_map/all_to_all | solution.py:79
  20.0 75.7 %all-gather.6.cloned.1.call-start = ((), (), s32[]{:S(2)}) async-start(), calls=%async_computation.3 | async-start | bytes 1179648 | tf_op jit(solution)/shard_map/all_gather | solution.py:122
  20.7 127.5 %all-gather.4.cloned.1.call-start = ((), (), s32[]{:S(2)}) async-start(), calls=%async_computation.2 | async-start | bytes 2621440 | tf_op jit(solution)/shard_map/all_gather | solution.py:124
  49.1 1.4 copy-start.1
  54.0 1.2 copy-start.12
  54.0 1.2 copy-start.14
  55.2 13.0 %collective-permute-start = (f32[16,72,128]{2,1,0:T(8,128)S(1)}, f32[16,72,128]{2,1,0:T(8,128)S(1)}, u32[]{:S(2)}, u32[]{:S(2)}) collective-permute-start(f32[16,72,128]{2,1,0:T(8,128)S(1)} %pad_maximum_fusion.2), channel_id=1, source_target_pairs={{0,4},{1,5},{4,8},{5,9},{6,2},{7,3},{8,12},{9,13},{10,6},{11,7},{1... | collective-permute-start | bytes 1769480 | tf_op jit(solution)/shard_map/ppermute | solution.py:103
  68.2 0.8 copy-start.4
  71.3 27.2 %collective-permute-start.1 = (f32[16,72,128]{2,1,0:T(8,128)}, f32[16,72,128]{2,1,0:T(8,128)S(1)}, u32[]{:S(2)}, u32[]{:S(2)}) collective-permute-start(f32[16,72,128]{2,1,0:T(8,128)} %pad_maximum_fusion.3), channel_id=1, source_target_pairs={{0,8},{1,9},{4,12},{5,13},{8,16},{9,17},{10,2},{11,3},{12,20},{13,... | collective-permute-start | bytes 1769480 | tf_op jit(solution)/shard_map/ppermute | solution.py:103
  98.5 0.8 copy-start.6
  98.6 9.2 %copy-start.2 = (bf16[4,8,8,2048]{3,2,1,0:T(8,128)(2,1)S(1)}, bf16[4,8,8,2048]{3,2,1,0:T(8,128)(2,1)}, u32[]{:S(2)}) copy-start(bf16[4,8,8,2048]{3,2,1,0:T(8,128)(2,1)} %copy.111) | copy-start | bytes 3145732
  100.1 14.9 %copy-start.5 = (f32[16,72,128]{2,1,0:T(8,128)S(1)}, f32[16,72,128]{2,1,0:T(8,128)}, u32[]{:S(2)}) copy-start(f32[16,72,128]{2,1,0:T(8,128)} %copy-done.4) | copy-start | bytes 1769476
  100.1 14.9 %copy-start.13 = (f32[16]{0:T(128)S(1)}, f32[16]{0:T(128)}, u32[]{:S(2)}) copy-start(f32[16]{0:T(128)} %copy-done.12) | copy-start | bytes 196
  100.1 14.8 %collective-permute-start.2 = (f32[1032,128]{1,0:T(8,128)}, f32[1032,128]{1,0:T(8,128)S(1)}, u32[]{:S(2)}, u32[]{:S(2)}) collective-permute-start(f32[1032,128]{1,0:T(8,128)} %pad_maximum_fusion.4), channel_id=1, source_target_pairs={{0,16},{1,17},{4,20},{5,21},{8,24},{9,25},{12,28},{13,29},{18,2},{... | collective-permute-start | bytes 1585160 | tf_op jit(solution)/shard_map/ppermute | solution.py:105
  109.0 7.3 %copy-start.3 = (f32[16,64,128]{2,1,0:T(8,128)S(1)}, f32[16,64,128]{2,1,0:T(8,128)}, u32[]{:S(2)}) copy-start(f32[16,64,128]{2,1,0:T(8,128)} %get-tuple-element.89) | copy-start | bytes 1572868
  109.0 7.3 %copy-start.11 = (f32[16]{0:T(128)S(1)}, f32[16]{0:T(128)}, u32[]{:S(2)}) copy-start(f32[16]{0:T(128)} %get-tuple-element.73) | copy-start | bytes 196
  118.3 18.6 %copy-start.8 = (f32[128,32]{1,0:T(8,128)S(1)}, f32[128,32]{1,0:T(8,128)}, u32[]{:S(2)}) copy-start(f32[128,32]{1,0:T(8,128)} %get-tuple-element.100) | copy-start | bytes 49156
  118.3 19.9 %copy-start.15 = (s32[16]{0:T(128)S(1)}, s32[16]{0:T(128)}, u32[]{:S(2)}) copy-start(s32[16]{0:T(128)} %param.19) | copy-start | bytes 196
  118.3 47.6 %all-to-all-start.1 = ((f32[4,16,64,128]{3,2,1,0:T(8,128)}), f32[4,16,64,128]{3,2,1,0:T(8,128)S(1)}, u32[]{:S(2)}, u32[]{:S(2)}) async-start(f32[4,16,64,128]{3,2,1,0:T(8,128)} %reverse_select_fusion.1), calls=%async_computation.1 | async-start | bytes 4194304 | tf_op jit(solution)/shard_map/all_to_all | solution.py:113
  148.2 24.1 %collective-permute-start.3 = (bf16[8,1024,128]{1,2,0:T(8,128)(2,1)}, bf16[8,1024,128]{1,2,0:T(8,128)(2,1)}, u32[]{:S(2)}, u32[]{:S(2)}) collective-permute-start(bf16[8,1024,128]{1,2,0:T(8,128)(2,1)} %all-gather.4.cloned.1.call-done), channel_id=1, source_target_pairs={{0,32},{32,0},{64,96},{96,64},{128,160},{160,128},{192,224},{224,1... | collective-permute-start | bytes 6291464 | tf_op jit(solution)/shard_map/ppermute | solution.py:127
  166.5 1.2 copy-start.7
  169.2 0.7 copy-start.10
  174.8 18.0 %collective-permute-start.4 = (bf16[128,1024]{1,0:T(8,128)(2,1)S(1)}, bf16[128,1024]{1,0:T(8,128)(2,1)S(1)}, u32[]{:S(2)}, u32[]{:S(2)}) collective-permute-start(bf16[128,1024]{1,0:T(8,128)(2,1)S(1)} %copy.106), channel_id=1, source_target_pairs={{28,32},{32,28},{60,64},{64,60},{92,96},{96,92},{124,128},{128,124... | collective-permute-start | bytes 786440 | tf_op jit(solution)/shard_map/ppermute | solution.py:226
Sparse Core Ops, SparseCore 0:
  22.9 72.7 all-gather.5
  109.1 39.0 all-gather.3
